TPU v7x, 128 devices: a whole 4x4x4 slice. The times are simulated.
128 devices in a mesh: row: 8 (over y, core), col: 16 (over z, x).
Axes of the slice: x: 4, y: 4, z: 4, core: 2. Of those that a mesh axis runs over, the one named last changes fastest.
Arguments:
- fock: bfloat16 [32768, 16, 2048], P('row', 'col'), may hold values from -6 to 6
- lmo_coef: bfloat16 [32768, 1024], P(('row', 'col')), may hold values from -0.078125 to 0.078125
- three_index: bfloat16 [32768, 512], P(('row', 'col')), may hold values from -6 to 6
- rotation: bfloat16 [16, 8, 1024, 512], P('col', 'row'), may hold values from -0.1875 to 0.1875
- lmo_ids: int32 [16, 8], replicated, may hold values from 0 to 127, as said below
- domains: int32 [128, 8], replicated, may hold values from -1 to 255, as said below
Outputs:
- proj_fock: float32 [16, 8, 512, 512], P('col', 'row')
- three_rot: bfloat16 [16, 8, 512, 512], P('col', 'row')
Inputs may be any that keep to these rules, and one draw needn't show every extreme that they name: `lmo_ids`: every LMO number appears exactly once; row o lists the 8 LMOs owned by column set o. `domains`: entry k of a list is -1 or a block of row panel k; entry 0 is never -1. The present blocks of one list lie in distinct column sets. For one owner o and one entry k, the blocks of the lists of lmo_ids[o, j] over all j lie in distinct column sets; for one j and one entry k, those of lmo_ids[o, j] over all o do too.
All inputs are finite; a program needn't handle non-finite values.
Results may differ from a plain program's by a relative error of at most 0.02.
Values may be sent and summed in bfloat16 or wider, within the bound.
No kernel may reach another device: no remote copies, remote signals or barrier semaphores. Data moves between devices by JAX's collectives and lax.ppermute only.
A program may use at most 192 MiB of HBM per device.

v0:
```python
import jax
import jax.numpy as jnp
from jax import lax
from jax.sharding import PartitionSpec as P

BLK = 128


def locate(blocks, dev_blocks, num_sets):
    present = blocks >= 0
    clipped = jnp.maximum(blocks, 0)
    flat_dev = clipped // dev_blocks
    return (present, flat_dev % num_sets, flat_dev // num_sets, clipped % dev_blocks)


def body(fock, lmo_coef, three_index, rotation, lmo_ids, domains):
    num_panels = lax.axis_size("row")
    num_sets = lax.axis_size("col")
    my_row = lax.axis_index("row")
    my_col = lax.axis_index("col")
    dev_rows = lmo_coef.shape[0]
    occ_width = lmo_coef.shape[1]
    dev_blocks = dev_rows // BLK
    dom_blocks = domains.shape[1]
    per_panel = dom_blocks // num_panels
    dev_lmos = rotation.shape[1]
    dom_width = dom_blocks * BLK
    panel_fock = fock[:, 0, :]
    gathered = lax.all_gather(lmo_coef, "row", axis=0, tiled=True)
    fock_coef = lax.psum_scatter(
        jnp.dot(panel_fock, gathered, preferred_element_type=jnp.float32).astype(jnp.bfloat16),
        "col",
        scatter_dimension=0,
        tiled=True,
    ).astype(jnp.float32)
    occ_term = jnp.einsum(
        "ri,rj->ij", lmo_coef, fock_coef.astype(jnp.bfloat16), preferred_element_type=jnp.float32
    )
    occ_fock = lax.psum(occ_term, ("row", "col"))
    correction = jnp.dot(
        lmo_coef, occ_fock.astype(jnp.bfloat16), preferred_element_type=jnp.float32
    )
    proj_rows = (fock_coef - 0.5 * correction).astype(jnp.bfloat16)
    all_rows = jnp.concatenate([lmo_coef, proj_rows, three_index], axis=1)
    row_width = all_rows.shape[1]
    row_blocks = all_rows.reshape(dev_blocks, BLK, row_width)
    fock_tiles = panel_fock.reshape(num_sets * dev_blocks, BLK, num_panels * dev_blocks, BLK)
    owner_doms = jnp.take(domains, lmo_ids, axis=0)
    present, col_set, panel_id, sub_block = locate(owner_doms, dev_blocks, num_sets)
    row_tile = col_set * dev_blocks + sub_block
    col_tile = panel_id * dev_blocks + sub_block
    holds_col = present & (col_set == my_col)
    my_col_tile = jnp.sum(jnp.where(holds_col, col_tile, 0), axis=2)
    has_col = jnp.any(holds_col, axis=2)
    sub_range = jnp.arange(dev_blocks, dtype=jnp.int32)
    set_range = jnp.arange(num_sets, dtype=jnp.int32)
    slot_start = my_row * per_panel
    mine_slot = lax.dynamic_slice_in_dim(holds_col, slot_start, per_panel, 2)
    sub_slot = lax.dynamic_slice_in_dim(sub_block, slot_start, per_panel, 2)
    row_slot = lax.dynamic_slice_in_dim(row_tile, slot_start, per_panel, 2)
    live_slot = lax.dynamic_slice_in_dim(present, slot_start, per_panel, 2) & has_col[:, :, None]
    owner_present = lax.dynamic_index_in_dim(present, my_col, 0, keepdims=False)
    owner_sets = lax.dynamic_index_in_dim(col_set, my_col, 0, keepdims=False)
    pick_rows = (mine_slot[..., None] & (sub_slot[..., None] == sub_range)).astype(jnp.bfloat16)
    rows_out = jnp.einsum(
        "ojps,sbw->opbw", pick_rows, row_blocks, preferred_element_type=jnp.float32
    ).astype(jnp.bfloat16)
    tiles_out = fock_tiles[row_slot, :, my_col_tile[:, :, None], :]
    tiles_out = jnp.where(live_slot[..., None, None], tiles_out, jnp.zeros_like(tiles_out))
    got_rows, got_tiles = (
        lax.all_to_all(rows_out, "col", split_axis=0, concat_axis=0, tiled=True),
        lax.all_to_all(tiles_out, "col", split_axis=0, concat_axis=0, tiled=True),
    )
    source = ((owner_sets[..., None] == set_range) & owner_present[..., None]).astype(jnp.bfloat16)
    source_slot = lax.dynamic_slice_in_dim(source, slot_start, per_panel, 1)
    source_slot = source_slot.reshape(num_panels, dev_lmos, per_panel, num_sets)
    strip_rows = jnp.einsum(
        "rdps,spbw->drpbw", source_slot, got_rows, preferred_element_type=jnp.float32
    ).astype(jnp.bfloat16)
    source_all = source.reshape(num_panels, dev_lmos, dom_blocks, num_sets)
    tiles_in = got_tiles.reshape(num_sets, num_panels, dev_lmos, per_panel, BLK, BLK)
    strip_fock = jnp.einsum(
        "rdks,srdpab->drpakb", source_all, tiles_in, preferred_element_type=jnp.float32
    ).astype(jnp.bfloat16)
    strip_fock = strip_fock.reshape(dev_lmos, num_panels, per_panel, BLK, dom_width)
    fin_rows, fin_fock = (
        lax.all_to_all(strip_rows, "row", split_axis=1, concat_axis=1, tiled=True),
        lax.all_to_all(strip_fock, "row", split_axis=1, concat_axis=1, tiled=True),
    )
    fin_rows = fin_rows.reshape(dev_lmos, dom_width, row_width)
    fin_fock = fin_fock.reshape(dev_lmos, dom_width, dom_width)
    slot_rot = rotation[0]
    coef_dom = fin_rows[:, :, :occ_width]
    proj_dom = fin_rows[:, :, occ_width : 2 * occ_width]
    three_dom = fin_rows[:, :, 2 * occ_width :]
    fock_half = jnp.einsum(
        "dxy,dyn->dxn", fin_fock, slot_rot, preferred_element_type=jnp.float32
    ).astype(jnp.bfloat16)
    fock_rot = jnp.einsum("dxm,dxn->dmn", slot_rot, fock_half, preferred_element_type=jnp.float32)
    coef_rot = jnp.einsum(
        "dxm,dxi->dmi", slot_rot, coef_dom, preferred_element_type=jnp.float32
    ).astype(jnp.bfloat16)
    proj_rot = jnp.einsum(
        "dxm,dxi->dmi", slot_rot, proj_dom, preferred_element_type=jnp.float32
    ).astype(jnp.bfloat16)
    proj_fock = fock_rot - jnp.einsum(
        "dmi,dni->dmn", coef_rot, proj_rot, preferred_element_type=jnp.float32
    )
    proj_fock = proj_fock - jnp.einsum(
        "dmi,dni->dmn", proj_rot, coef_rot, preferred_element_type=jnp.float32
    )
    three_rot = jnp.einsum(
        "dxm,dxu->dmu", slot_rot, three_dom, preferred_element_type=jnp.float32
    ).astype(jnp.bfloat16)
    return (proj_fock[None], three_rot[None])


def solution(mesh):
    placed = (
        P("row", "col", None),
        P(("row", "col"), None),
        P(("row", "col"), None),
        P("col", "row", None, None),
        P(),
        P(),
    )
    return jax.shard_map(
        body,
        mesh=mesh,
        in_specs=placed,
        out_specs=(P("col", "row", None, None), P("col", "row", None, None)),
        check_vma=False,
    )
```

profile of v0, /device:TPU:1, one launch (start us, length us, event | category | flops | bytes accessed | tf_op | source)
XLA Modules:
  0.0 609.3 jit_solution(9066787770218420429)
XLA Ops:
  7.2 0.7 all-gather.2.cloned.1.call-update
  8.0 37.6 %all-gather.2.cloned.1.call-done = bf16[2048,1024]{1,0:T(8,128)(2,1)} async-done(((bf16[256,1024]{1,0:T(8,128)(2,1)}), bf16[2048,1024]{1,0:T(8,128)(2,1)}) %all-gather.2.cloned.1.call-update) | async-done | bytes 4194320 | tf_op jit(solution)/shard_map/all_gather | solution.py:29
  45.5 23.4 %fusion.5 = bf16[4096,1024]{1,0:T(8,128)(2,1)} fusion(bf16[2048,1024]{1,0:T(8,128)(2,1)} %all-gather.2.cloned.1.call-done, bf16[4096,1,2048]{2,0,1:T(8,128)(2,1)} %param.6), kind=kOutput, calls=%fused_computation.8 | convolution fusion | flops 17184063488 | bytes 29360128 | tf_op jit(solution)/shard_map/dot_general | solution.py:31
  69.0 9.7 %copy.120 = bf16[512,8,16,128]{3,2,1,0:T(8,128)(2,1)S(1)} copy(bf16[512,8,16,128]{3,1,2,0:T(8,128)(2,1)} %bitcast.129) | data formatting | bytes 33554432
  78.6 8.1 %copy.94 = bf16[32,128,16,128]{3,1,2,0:T(8,128)(2,1)} copy(bf16[32,128,16,128]{3,2,1,0:T(8,128)(2,1)S(1)} %bitcast.127) | data formatting | bytes 33554432 | tf_op jit(solution)/shard_map/reshape;squeeze | solution.py:47
  88.3 9.6 %gather_fusion.1 = bf16[128,128,128]{2,1,0:T(8,128)(2,1)} fusion(bf16[32,128,16,128]{3,1,2,0:T(8,128)(2,1)} %copy.94, s32[128]{0:T(128)S(1)} %reshape.172), kind=kCustom, calls=%fused_computation.1 | custom fusion | bytes 8389632 | tf_op jit(solution)/shard_map/gather | solution.py:68
  97.8 4.6 select_bitcast_fusion
  102.4 6.9 %all-to-all-start = ((bf16[16,8,1,128,128]{4,3,1,2,0:T(8,128)(2,1)}), bf16[16,8,1,128,128]{4,3,1,2,0:T(8,128)(2,1)}, u32[]{:S(2)}, u32[]{:S(2)}) async-start(bf16[16,8,1,128,128]{4,3,1,2,0:T(8,128)(2,1)} %select_bitcast_fusion), calls=%async_computation | async-start | bytes 8388608 | tf_op jit(solution)/shard_map/all_to_all | solution.py:72
  109.3 92.5 %reduce-scatter.2.cloned.1.call-done = bf16[256,1024]{1,0:T(8,128)(2,1)} async-done(((bf16[4096,1024]{1,0:T(8,128)(2,1)}), bf16[256,1024]{1,0:T(8,128)(2,1)}) %reduce-scatter.2.cloned.1.call-update) | async-done | bytes 524304 | tf_op jit(solution)/shard_map/reduce_scatter | solution.py:30
  201.8 3.7 convolution_bitcast_fusion
  205.5 104.6 %all-reduce.1 = bf16[1024,1024]{0,1:T(8,128)(2,1)} all-reduce(f32[1024,1024]{0,1:T(8,128)} %convolution_bitcast_fusion), channel_id=1, replica_groups=mesh['row'=8,'col'=16] {'row','col'}, use_global_device_ids=true, to_apply=%region_4.5 | all-reduce | flops 1048576 | bytes 6291456 | tf_op jit(solution)/shard_map/psum | solution.py:39
  310.2 2.4 fusion.36
  312.7 5.9 convert_bitcast_fusion
  318.6 13.7 %copy.105 = bf16[16,1,128,2560]{3,2,1,0:T(8,128)(2,1)} copy(bf16[16,1,128,2560]{3,0,2,1:T(8,128)(2,1)} %convert_bitcast_fusion) | data formatting | bytes 20971520 | tf_op jit(solution)/shard_map/convert_element_type | solution.py:67
  332.3 5.2 all-to-all-start.2
  338.0 4.6 convert_bitcast_fusion.1
  342.7 2.3 reshape.152
  345.0 144.6 %all-to-all-done.2 = bf16[16,1,128,2560]{3,2,1,0:T(8,128)(2,1)} async-done(((bf16[16,1,128,2560]{3,2,1,0:T(8,128)(2,1)}), bf16[16,1,128,2560]{3,2,1,0:T(8,128)(2,1)}, u32[]{:S(2)}, u32[]{:S(2)}) %all-to-all-start.2) | async-done | bytes 10485792 | tf_op jit(solution)/shard_map/all_to_all | solution.py:71
  489.5 9.3 %all-to-all-start.1 = ((bf16[1,8,1,128,1024]{4,3,2,0,1:T(8,128)(2,1)}), bf16[1,8,1,128,1024]{4,3,2,0,1:T(8,128)(2,1)S(1)}, u32[]{:S(2)}, u32[]{:S(2)}) async-start(bf16[1,8,1,128,1024]{4,3,2,0,1:T(8,128)(2,1)} %bitcast.16), calls=%async_computation.1 | async-start | bytes 4194304 | tf_op jit(solution)/shard_map/all_to_all | solution.py:88
  498.8 10.1 %fusion.11 = bf16[1,8,1,128,2560]{4,1,3,0,2:T(8,128)(2,1)S(1)} fusion(bf16[16,1,128,2560]{3,2,1,0:T(8,128)(2,1)} %all-to-all-done.2, pred[8,8,16]{2,0,1:T(8,128)(4,1)S(1)} %get-tuple-element.20, s32[]{:T(128)S(6)} %select_n.74), kind=kOutput, calls=%fused_computation.10 | convolution fusion | flops 86507520 | bytes 15729668 | tf_op jit(solution)/shard_map/rdps,spbw->drpbw/dot_general | solution.py:77
  508.9 3.8 copy.107
  512.8 12.4 %all-to-all-done.1 = bf16[1,8,1,128,1024]{4,3,2,0,1:T(8,128)(2,1)S(1)} async-done(((bf16[1,8,1,128,1024]{4,3,2,0,1:T(8,128)(2,1)}), bf16[1,8,1,128,1024]{4,3,2,0,1:T(8,128)(2,1)S(1)}, u32[]{:S(2)}, u32[]{:S(2)}) %all-to-all-start.1) | async-done | bytes 2097184 | tf_op jit(solution)/shard_map/all_to_all | solution.py:88
  525.2 5.4 all-to-all-start.3
  530.6 2.8 convolution_bitcast_fusion.1
  533.4 57.4 %all-to-all-done.3 = bf16[1,8,1,128,2560]{4,3,0,2,1:T(8,128)(2,1)} async-done(((bf16[1,8,1,128,2560]{4,3,0,2,1:T(8,128)(2,1)}), bf16[1,8,1,128,2560]{4,3,0,2,1:T(8,128)(2,1)}, u32[]{:S(2)}, u32[]{:S(2)}) %all-to-all-start.3) | async-done | bytes 5242912 | tf_op jit(solution)/shard_map/all_to_all | solution.py:87
  590.8 2.9 fusion.23
  593.6 2.9 fusion.24
  596.5 2.0 fusion.39
  598.6 0.8 convolution_subtract_fusion.1
  599.4 0.8 fusion.34
  600.1 1.3 copy.110
  601.4 1.0 copy.111
  (44 shorter events, 2.2 us)
Async XLA Ops:
  7.2 523.5 %copy-start = (bf16[1,1,1024,512]{3,2,1,0:T(8,128)(2,1)S(1)}, bf16[1,1,1024,512]{3,2,1,0:T(8,128)(2,1)}, u32[]{:S(2)}) copy-start(bf16[1,1,1024,512]{3,2,1,0:T(8,128)(2,1)} %param.9) | copy-start | bytes 3145732
  7.2 38.3 %all-gather.2.cloned.1.call-start = ((), (), s32[]{:S(2)}) async-start(), calls=%async_computation.5 | async-start | bytes 4718592 | tf_op jit(solution)/shard_map/all_gather | solution.py:29
  7.9 193.9 %reduce-scatter.2.cloned.1.call-start = ((), (), s32[]{:S(2)}) async-start(), calls=%async_computation.6 | async-start | bytes 8912896 | tf_op jit(solution)/shard_map/reduce_scatter | solution.py:30
  78.6 8.2 %copy-start.6 = (s32[128,8]{0,1:T(8,128)S(1)}, s32[128,8]{0,1:T(8,128)}, u32[]{:S(2)}) copy-start(s32[128,8]{0,1:T(8,128)} %param.11) | copy-start | bytes 12292
  78.6 8.3 %copy-start.5 = (s32[16,8]{0,1:T(8,128)S(1)}, s32[16,8]{0,1:T(8,128)}, u32[]{:S(2)}) copy-start(s32[16,8]{0,1:T(8,128)} %param.10) | copy-start | bytes 1540
  102.4 99.4 %copy-start.1 = (bf16[256,1024]{1,0:T(8,128)(2,1)S(1)}, bf16[256,1024]{1,0:T(8,128)(2,1)}, u32[]{:S(2)}) copy-start(bf16[256,1024]{1,0:T(8,128)(2,1)} %param.7) | copy-start | bytes 1572868
  102.4 229.9 %all-to-all-start = ((bf16[16,8,1,128,128]{4,3,1,2,0:T(8,128)(2,1)}), bf16[16,8,1,128,128]{4,3,1,2,0:T(8,128)(2,1)}, u32[]{:S(2)}, u32[]{:S(2)}) async-start(bf16[16,8,1,128,128]{4,3,1,2,0:T(8,128)(2,1)} %select_bitcast_fusion), calls=%async_computation | async-start | bytes 8388608 | tf_op jit(solution)/shard_map/all_to_all | solution.py:72
  205.5 104.7 %copy-start.2 = (bf16[256,1024]{1,0:T(8,128)(2,1)S(1)}, bf16[256,1024]{1,0:T(8,128)(2,1)}, u32[]{:S(2)}) copy-start(bf16[256,1024]{1,0:T(8,128)(2,1)} %reduce-scatter.2.cloned.1.call-done) | copy-start | bytes 1572868
  310.2 2.4 copy-start.4
  332.3 157.2 %all-to-all-start.2 = ((bf16[16,1,128,2560]{3,2,1,0:T(8,128)(2,1)}), bf16[16,1,128,2560]{3,2,1,0:T(8,128)(2,1)}, u32[]{:S(2)}, u32[]{:S(2)}) async-start(bf16[16,1,128,2560]{3,2,1,0:T(8,128)(2,1)} %copy.105), calls=%async_computation.3 | async-start | bytes 20971520 | tf_op jit(solution)/shard_map/all_to_all | solution.py:71
  489.5 35.7 %all-to-all-start.1 = ((bf16[1,8,1,128,1024]{4,3,2,0,1:T(8,128)(2,1)}), bf16[1,8,1,128,1024]{4,3,2,0,1:T(8,128)(2,1)S(1)}, u32[]{:S(2)}, u32[]{:S(2)}) async-start(bf16[1,8,1,128,1024]{4,3,2,0,1:T(8,128)(2,1)} %bitcast.16), calls=%async_computation.1 | async-start | bytes 4194304 | tf_op jit(solution)/shard_map/all_to_all | solution.py:88
  525.2 65.6 %all-to-all-start.3 = ((bf16[1,8,1,128,2560]{4,3,0,2,1:T(8,128)(2,1)}), bf16[1,8,1,128,2560]{4,3,0,2,1:T(8,128)(2,1)}, u32[]{:S(2)}, u32[]{:S(2)}) async-start(bf16[1,8,1,128,2560]{4,3,0,2,1:T(8,128)(2,1)} %copy.107), calls=%async_computation.4 | async-start | bytes 10485760 | tf_op jit(solution)/shard_map/all_to_all | solution.py:87
  596.5 2.1 copy-start.3
Sparse Core Ops, SparseCore 0:
  9.7 35.7 all-gather.1
  69.1 132.6 reduce-scatter.1
where the time goes:
time: 610 us; the launch traced here: 609 us
  waiting for transfers between devices  345 us (57%)
  blocking collectives  105 us (17%)
  matrix products  62.2 us (10%)
  local copies, waits for them, and re-layouts  51.2 us (8%)
  starting transfers between devices  26.9 us (4%)
  between operations  14.3 us (2%)
    all_to_all x1, waiting for transfers between devices, body(): lax.all_to_all(rows_out, 'col', split_axis=0, concat_axis=0, tiled=True)  145 us
    psum x1, blocking collectives, body(): occ_fock = lax.psum(occ_term, ('row', 'col'))  105 us
    reduce_scatter x1, waiting for transfers between devices, body(): lax.psum_scatter(jnp.dot(panel_fock, gathered, preferred_element_type=jnp...  92.5 us
    all_to_all x1, waiting for transfers between devices, body(): lax.all_to_all(strip_rows, 'row', split_axis=1, concat_axis=1, tiled=True)  57.4 us
    all_gather x1, waiting for transfers between devices, body(): gathered = lax.all_gather(lmo_coef, 'row', axis=0, tiled=True)  37.6 us
    dot_general x1, matrix products, body(): jnp.dot(panel_fock, gathered, preferred_element_type=jnp.float32)  23.4 us
    convert_element_type x1, local copies, waits for them, and re-layouts, body(): rows_out = jnp.einsum('ojps,sbw->opbw', pick_rows, row_blocks, preferred_...  13.7 us
    all_to_all x1, waiting for transfers between devices, body(): lax.all_to_all(strip_fock, 'row', split_axis=1, concat_axis=1, tiled=True)  12.4 us
  transfers between devices with their start and end apart: 6, of which 5 were waited for; matrix products, arithmetic and copies ran while one was open for 14% of the time, Pallas kernels for 0%

commit v1 on v0

v1 whole, which is shorter than its diff:
```python
import jax
import jax.numpy as jnp
from jax import lax
from jax.sharding import PartitionSpec as P

BLK = 128
F32 = jnp.float32
BF16 = jnp.bfloat16


def pick(mask, table):
    return jnp.sum(jnp.where(mask, table, 0), axis=-1)


def body(fock, lmo_coef, three_index, rotation, lmo_ids, domains):
    num_sets = lax.axis_size("col")
    my_row = lax.axis_index("row")
    my_col = lax.axis_index("col")
    dev_rows = lmo_coef.shape[0]
    occ_width = lmo_coef.shape[1]
    dev_blocks = dev_rows // BLK
    dom_blocks = domains.shape[1]
    dom_width = dom_blocks * BLK
    panel_fock = fock[:, 0, :]
    panel_blocks = panel_fock.shape[0] // BLK
    col_blocks = panel_fock.shape[1] // BLK

    doms = jnp.take(domains, lmo_ids, axis=0)
    present = doms >= 0
    clipped = jnp.maximum(doms, 0)
    flat = clipped // dev_blocks
    cset = flat % num_sets
    sub = clipped % dev_blocks
    panel = flat // num_sets
    row_tile = cset * dev_blocks + sub
    col_tile = panel * dev_blocks + sub

    pres_k = lax.dynamic_index_in_dim(present, my_row, 2, keepdims=False)
    cset_k = lax.dynamic_index_in_dim(cset, my_row, 2, keepdims=False)
    sub_k = lax.dynamic_index_in_dim(sub, my_row, 2, keepdims=False)
    rtile_k = lax.dynamic_index_in_dim(row_tile, my_row, 2, keepdims=False)
    mine_k = pres_k & (cset_k == my_col)
    sub_range = jnp.arange(dev_blocks, dtype=jnp.int32)
    sel1 = jnp.any(mine_k[:, :, None] & (sub_k[:, :, None] == sub_range), axis=0).astype(BF16)

    mine2 = present & (cset == my_col)
    has2 = jnp.any(mine2, axis=0)
    rt = pick(mine2.transpose(1, 2, 0), jnp.broadcast_to(rtile_k.T[:, None, :], mine2.transpose(1, 2, 0).shape))
    ok1 = jnp.any(mine2.transpose(1, 2, 0) & pres_k.T[:, None, :], axis=-1)
    ct = pick(mine2.transpose(1, 2, 0), col_tile.transpose(1, 2, 0))
    fock_tiles = panel_fock.reshape(panel_blocks, BLK, col_blocks, BLK)
    send1_fock = fock_tiles[rt, :, ct, :]
    send1_fock = jnp.where((has2 & ok1)[:, :, None, None], send1_fock, jnp.zeros_like(send1_fock))

    in_rows = jnp.concatenate([lmo_coef, three_index], axis=1).reshape(dev_blocks, BLK, -1)
    send1_rows = jnp.einsum("js,sbw->jbw", sel1, in_rows, preferred_element_type=F32).astype(BF16)

    recv1_rows, recv1_fock = (
        lax.all_to_all(send1_rows, "row", 0, 0, tiled=True),
        lax.all_to_all(send1_fock, "row", 0, 0, tiled=True),
    )

    pres_j = lax.dynamic_index_in_dim(present, my_row, 1, keepdims=False)
    cset_j = lax.dynamic_index_in_dim(cset, my_row, 1, keepdims=False)
    sel2 = (pres_j & (cset_j == my_col)).astype(BF16)
    send2_rows = jnp.einsum("ok,kbw->obw", sel2, recv1_rows, preferred_element_type=F32).astype(BF16)
    send2_fock = jnp.einsum("ok,akbt->oabt", sel2, recv1_fock, preferred_element_type=F32).astype(BF16)
    recv2_rows, recv2_fock = (
        lax.all_to_all(send2_rows, "col", 0, 0, tiled=True),
        lax.all_to_all(send2_fock, "col", 0, 0, tiled=True),
    )

    pres_o = lax.dynamic_index_in_dim(pres_j, my_col, 0, keepdims=False)
    cset_o = lax.dynamic_index_in_dim(cset_j, my_col, 0, keepdims=False)
    set_range = jnp.arange(num_sets, dtype=jnp.int32)
    sel3 = (pres_o[:, None] & (cset_o[:, None] == set_range)).astype(BF16)
    rows_dom = jnp.einsum("ks,sbw->kbw", sel3, recv2_rows, preferred_element_type=F32).astype(BF16)
    rows_dom = rows_dom.reshape(dom_width, -1)
    domain_fock = jnp.einsum("ks,sabt->abkt", sel3, recv2_fock, preferred_element_type=F32).astype(BF16)
    domain_fock = domain_fock.reshape(dom_width, dom_width)

    gathered = lax.all_gather(lmo_coef, "row", axis=0, tiled=True)
    coef_b = lax.psum_scatter(
        jnp.dot(panel_fock, gathered, preferred_element_type=F32).astype(BF16),
        "col",
        scatter_dimension=0,
        tiled=True,
    )
    occ_term = jnp.einsum("ri,rj->ij", lmo_coef, coef_b, preferred_element_type=F32)
    occ_part = lax.psum_scatter(occ_term, ("row", "col"), scatter_dimension=0, tiled=True)
    occ_b = lax.all_gather(occ_part.astype(BF16), ("row", "col"), axis=0, tiled=True)

    fc_blocks = coef_b.reshape(dev_blocks, BLK, occ_width)
    fc1 = jnp.einsum("js,sbw->jbw", sel1, fc_blocks, preferred_element_type=F32).astype(BF16)
    fc1 = lax.all_to_all(fc1, "row", 0, 0, tiled=True)
    fc2 = jnp.einsum("ok,kbw->obw", sel2, fc1, preferred_element_type=F32).astype(BF16)
    fc2 = lax.all_to_all(fc2, "col", 0, 0, tiled=True)
    fc_dom = jnp.einsum("ks,sbw->kbw", sel3, fc2, preferred_element_type=F32).reshape(dom_width, occ_width)

    coef_dom = rows_dom[:, :occ_width]
    three_dom = rows_dom[:, occ_width:]
    correction = jnp.dot(coef_dom, occ_b, preferred_element_type=F32)
    proj_dom = (fc_dom - 0.5 * correction).astype(BF16)

    slot_rot = rotation[0, 0]
    fock_half = jnp.dot(domain_fock, slot_rot, preferred_element_type=F32).astype(BF16)
    fock_rot = jnp.einsum("xm,xn->mn", slot_rot, fock_half, preferred_element_type=F32)
    coef_rot = jnp.einsum("xm,xi->mi", slot_rot, coef_dom, preferred_element_type=F32).astype(BF16)
    proj_rot = jnp.einsum("xm,xi->mi", slot_rot, proj_dom, preferred_element_type=F32).astype(BF16)
    proj_fock = fock_rot - jnp.einsum("mi,ni->mn", coef_rot, proj_rot, preferred_element_type=F32)
    proj_fock = proj_fock - jnp.einsum("mi,ni->mn", proj_rot, coef_rot, preferred_element_type=F32)
    three_rot = jnp.einsum("xm,xu->mu", slot_rot, three_dom, preferred_element_type=F32).astype(BF16)
    return (proj_fock[None, None], three_rot[None, None])


def solution(mesh):
    placed = (
        P("row", "col", None),
        P(("row", "col"), None),
        P(("row", "col"), None),
        P("col", "row", None, None),
        P(),
        P(),
    )
    return jax.shard_map(
        body,
        mesh=mesh,
        in_specs=placed,
        out_specs=(P("col", "row", None, None), P("col", "row", None, None)),
        check_vma=False,
    )
```

time: 610 us -> 976 us (1.60)
  waiting for transfers between devices: 345 us -> 777 us
  blocking collectives: 105 us -> 0 us
  starting transfers between devices: 26.9 us -> 40.5 us
  local copies, waits for them, and re-layouts: 51.2 us -> 61.3 us
    reduce_scatter x1 -> x2, waiting for transfers between devices: 92.5 us -> 458 us  [the longest x1 458 us: body(): lax.psum_scatter(occ_term, ('row', 'col'), scatter_dimension=0, tiled=True)]
    psum x1 -> x0, blocking collectives: 105 us -> none  [body(): occ_fock = lax.psum(occ_term, ('row', 'col'))]
    all_gather x0 -> x1, waiting for transfers between devices: none -> 68.5 us  [body(): lax.all_gather(occ_part.astype(BF16), ('row', 'col'), axis=0, tiled=True)]
    unnamed x18 -> x22, local copies, waits for them, and re-layouts: 12.1 us -> 20.2 us
    dot_general x12 -> x17, matrix products: 62.2 us -> 67.9 us  [the longest x1 23.4 us: body(): jnp.dot(panel_fock, gathered, preferred_element_type=F32).astype(BF16)]
    all_to_all x4 -> x6, starting transfers between devices: 26.8 us -> 31.6 us  [the longest x1 6.71 us: body(): lax.all_to_all(send2_fock, 'col', 0, 0, tiled=True)]
    all_to_all x4 -> x6, waiting for transfers between devices: 214 us -> 212 us  [the longest x1 90.8 us: body(): lax.all_to_all(send2_rows, 'col', 0, 0, tiled=True)]
  transfers between devices with their start and end apart: 6 -> 10, of which waited for: 5 -> 8; matrix products, arithmetic and copies ran while one was open for 14% -> 10% of each run, Pallas kernels for 0% -> 0%
where the time goes in v1:
time: 976 us; the launch traced here: 967 us
  waiting for transfers between devices  777 us (80%)
  matrix products  67.9 us (7%)
  local copies, waits for them, and re-layouts  61.3 us (6%)
  starting transfers between devices  40.5 us (4%)
  between operations  14.3 us (1%)
    reduce_scatter x1, waiting for transfers between devices, body(): lax.psum_scatter(occ_term, ('row', 'col'), scatter_dimension=0, tiled=True)  458 us
    all_to_all x1, waiting for transfers between devices, body(): lax.all_to_all(send2_rows, 'col', 0, 0, tiled=True)  90.8 us
    all_gather x1, waiting for transfers between devices, body(): lax.all_gather(occ_part.astype(BF16), ('row', 'col'), axis=0, tiled=True)  68.5 us
    all_to_all x1, waiting for transfers between devices, body(): lax.all_to_all(send2_fock, 'col', 0, 0, tiled=True)  51 us
    all_gather x1, waiting for transfers between devices, body(): gathered = lax.all_gather(lmo_coef, 'row', axis=0, tiled=True)  37.6 us
    all_to_all x1, waiting for transfers between devices, body(): lax.all_to_all(send1_rows, 'row', 0, 0, tiled=True)  33 us
    dot_general x1, matrix products, body(): jnp.dot(panel_fock, gathered, preferred_element_type=F32).astype(BF16)  23.4 us
    all_to_all x1, waiting for transfers between devices, body(): lax.all_to_all(send1_fock, 'row', 0, 0, tiled=True)  21.1 us
  transfers between devices with their start and end apart: 10, of which 8 were waited for; matrix products, arithmetic and copies ran while one was open for 10% of the time, Pallas kernels for 0%

profile of v1, /device:TPU:1, one launch (start us, length us, event | category | flops | bytes accessed | tf_op | source)
XLA Modules:
  0.0 966.6 jit_solution(5314930313470861836)
XLA Ops:
  8.0 37.6 %all-gather.3.cloned.1.call-done = bf16[2048,1024]{1,0:T(8,128)(2,1)} async-done(((bf16[256,1024]{1,0:T(8,128)(2,1)}), bf16[2048,1024]{1,0:T(8,128)(2,1)}) %all-gather.3.cloned.1.call-update) | async-done | bytes 4194320 | tf_op jit(solution)/shard_map/all_gather | solution.py:82
  45.5 23.4 %fusion.2 = bf16[4096,1024]{1,0:T(8,128)(2,1)} fusion(bf16[2048,1024]{1,0:T(8,128)(2,1)} %all-gather.3.cloned.1.call-done, bf16[4096,1,2048]{2,0,1:T(8,128)(2,1)} %param.6), kind=kOutput, calls=%fused_computation.4 | convolution fusion | flops 17184063488 | bytes 29360128 | tf_op jit(solution)/shard_map/dot_general | solution.py:84
  69.0 9.7 copy.160
  78.6 8.1 copy.130
  88.8 7.4 gather_fusion.1
  99.0 3.9 all-to-all-start
  108.2 21.1 %all-to-all-done = bf16[8,8,128,128]{3,1,2,0:T(8,128)(2,1)S(1)} async-done(((bf16[8,8,128,128]{3,1,2,0:T(8,128)(2,1)}), bf16[8,8,128,128]{3,1,2,0:T(8,128)(2,1)S(1)}, u32[]{:S(2)}, u32[]{:S(2)}) %all-to-all-start) | async-done | bytes 2097184 | tf_op jit(solution)/shard_map/all_to_all | solution.py:60
  129.2 5.5 all-to-all-start.2
  136.4 3.1 copy.132
  139.4 33.0 %all-to-all-done.2 = bf16[8,128,1536]{2,1,0:T(8,128)(2,1)} async-done(((bf16[8,128,1536]{2,1,0:T(8,128)(2,1)}), bf16[8,128,1536]{2,1,0:T(8,128)(2,1)}, u32[]{:S(2)}, u32[]{:S(2)}) %all-to-all-start.2) | async-done | bytes 3145760 | tf_op jit(solution)/shard_map/all_to_all | solution.py:59
  172.4 6.7 all-to-all-start.1
  179.2 3.8 convolution_bitcast_fusion
  183.0 5.4 copy.155
  192.9 51.0 %all-to-all-done.1 = bf16[16,8,128,128]{3,2,1,0:T(8,128)(2,1)} async-done(((bf16[16,8,128,128]{3,2,1,0:T(8,128)(2,1)}), bf16[16,8,128,128]{3,2,1,0:T(8,128)(2,1)}, u32[]{:S(2)}, u32[]{:S(2)}) %all-to-all-start.1) | async-done | bytes 4194336 | tf_op jit(solution)/shard_map/all_to_all | solution.py:70
  243.9 5.8 all-to-all-start.4
  249.7 4.2 convolution_convert_fusion
  253.9 6.2 copy.137
  260.1 15.9 %all-to-all-done.4 = bf16[8,128,1024]{2,1,0:T(8,128)(2,1)S(1)} async-done(((bf16[8,128,1024]{2,1,0:T(8,128)(2,1)}), bf16[8,128,1024]{2,1,0:T(8,128)(2,1)S(1)}, u32[]{:S(2)}, u32[]{:S(2)}) %all-to-all-start.4) | async-done | bytes 2097184 | tf_op jit(solution)/shard_map/all_to_all | solution.py:95
  276.0 4.6 all-to-all-start.3
  282.3 4.3 copy.143
  286.6 90.8 %all-to-all-done.3 = bf16[16,128,1536]{2,1,0:T(8,128)(2,1)} async-done(((bf16[16,128,1536]{2,1,0:T(8,128)(2,1)}), bf16[16,128,1536]{2,1,0:T(8,128)(2,1)}, u32[]{:S(2)}, u32[]{:S(2)}) %all-to-all-start.3) | async-done | bytes 6291488 | tf_op jit(solution)/shard_map/all_to_all | solution.py:69
  377.5 5.0 all-to-all-start.5
  382.5 8.8 all-gather.5.cloned.1.call-start
  391.3 458.0 %reduce-scatter.7.cloned.1.call-done = f32[8,1024]{1,0:T(8,128)} async-done(((f32[1024,1024]{1,0:T(8,128)}), f32[8,1024]{1,0:T(8,128)}) %reduce-scatter.7.cloned.1.call-update) | async-done | bytes 32784 | tf_op jit(solution)/shard_map/reduce_scatter | solution.py:90
  851.0 4.6 fusion.20
  855.7 2.8 convolution_bitcast_fusion.1
  858.4 6.4 fusion.12
  869.2 2.9 fusion.26
  872.1 4.9 fusion.8
  877.0 4.4 copy.145
  881.3 68.5 %all-gather.5.cloned.1.call-done = bf16[1024,1024]{1,0:T(8,128)(2,1)} async-done(((bf16[8,1024]{1,0:T(8,128)(2,1)}), bf16[1024,1024]{1,0:T(8,128)(2,1)}) %all-gather.5.cloned.1.call-update) | async-done | bytes 2097168 | tf_op jit(solution)/shard_map/all_gather | solution.py:91
  949.8 5.8 fusion.7
  (66 shorter events, 28.9 us)
Async XLA Ops:
  7.2 848.5 %copy-start = (bf16[1,1,1024,512]{3,2,1,0:T(8,128)(2,1)S(1)}, bf16[1,1,1024,512]{3,2,1,0:T(8,128)(2,1)}, u32[]{:S(2)}) copy-start(bf16[1,1,1024,512]{3,2,1,0:T(8,128)(2,1)} %param.9) | copy-start | bytes 3145732
  7.2 38.3 %all-gather.3.cloned.1.call-start = ((), (), s32[]{:S(2)}) async-start(), calls=%async_computation.8 | async-start | bytes 4718592 | tf_op jit(solution)/shard_map/all_gather | solution.py:82
  7.9 171.3 %reduce-scatter.5.cloned.1.call-start = ((), (), s32[]{:S(2)}) async-start(), calls=%async_computation.9 | async-start | bytes 8912896 | tf_op jit(solution)/shard_map/reduce_scatter | solution.py:83
  78.6 8.2 copy-start.7
  78.6 8.3 copy-start.6
  99.0 4.1 copy-start.5
  99.0 30.3 %all-to-all-start = ((bf16[8,8,128,128]{3,1,2,0:T(8,128)(2,1)}), bf16[8,8,128,128]{3,1,2,0:T(8,128)(2,1)S(1)}, u32[]{:S(2)}, u32[]{:S(2)}) async-start(bf16[8,8,128,128]{3,1,2,0:T(8,128)(2,1)} %copy_select_fusion), calls=%async_computation | async-start | bytes 4194304 | tf_op jit(solution)/shard_map/all_to_all | solution.py:60
  129.2 43.2 %all-to-all-start.2 = ((bf16[8,128,1536]{2,1,0:T(8,128)(2,1)}), bf16[8,128,1536]{2,1,0:T(8,128)(2,1)}, u32[]{:S(2)}, u32[]{:S(2)}) async-start(bf16[8,128,1536]{2,1,0:T(8,128)(2,1)} %copy.135), calls=%async_computation.2 | async-start | bytes 6291456 | tf_op jit(solution)/shard_map/all_to_all | solution.py:59
  139.4 39.8 %copy-start.1 = (bf16[256,1024]{1,0:T(8,128)(2,1)S(1)}, bf16[256,1024]{1,0:T(8,128)(2,1)}, u32[]{:S(2)}) copy-start(bf16[256,1024]{1,0:T(8,128)(2,1)} %param.7) | copy-start | bytes 1572868
  172.4 71.5 %all-to-all-start.1 = ((bf16[16,8,128,128]{3,2,1,0:T(8,128)(2,1)}), bf16[16,8,128,128]{3,2,1,0:T(8,128)(2,1)}, u32[]{:S(2)}, u32[]{:S(2)}) async-start(bf16[16,8,128,128]{3,2,1,0:T(8,128)(2,1)} %copy.132), calls=%async_computation.1 | async-start | bytes 8388608 | tf_op jit(solution)/shard_map/all_to_all | solution.py:70
  179.1 670.1 %reduce-scatter.7.cloned.1.call-start = ((), (), s32[]{:S(2)}) async-start(), calls=%async_computation.11 | async-start | bytes 4227072 | tf_op jit(solution)/shard_map/reduce_scatter | solution.py:90
  188.3 1.0 copy-start.2
  243.9 32.1 %all-to-all-start.4 = ((bf16[8,128,1024]{2,1,0:T(8,128)(2,1)}), bf16[8,128,1024]{2,1,0:T(8,128)(2,1)S(1)}, u32[]{:S(2)}, u32[]{:S(2)}) async-start(bf16[8,128,1024]{2,1,0:T(8,128)(2,1)} %copy.141), calls=%async_computation.5 | async-start | bytes 4194304 | tf_op jit(solution)/shard_map/all_to_all | solution.py:95
  276.0 101.5 %all-to-all-start.3 = ((bf16[16,128,1536]{2,1,0:T(8,128)(2,1)}), bf16[16,128,1536]{2,1,0:T(8,128)(2,1)}, u32[]{:S(2)}, u32[]{:S(2)}) async-start(bf16[16,128,1536]{2,1,0:T(8,128)(2,1)} %copy.137), calls=%async_computation.3 | async-start | bytes 12582912 | tf_op jit(solution)/shard_map/all_to_all | solution.py:69
  377.5 494.6 %all-to-all-start.5 = ((bf16[16,128,1024]{2,1,0:T(8,128)(2,1)}), bf16[16,128,1024]{2,1,0:T(8,128)(2,1)}, u32[]{:S(2)}, u32[]{:S(2)}) async-start(bf16[16,128,1024]{2,1,0:T(8,128)(2,1)} %copy.143), calls=%async_computation.6 | async-start | bytes 8388608 | tf_op jit(solution)/shard_map/all_to_all | solution.py:97
  382.5 567.3 %all-gather.5.cloned.1.call-start = ((), (), s32[]{:S(2)}) async-start(), calls=%async_computation.10 | async-start | bytes 2113536 | tf_op jit(solution)/shard_map/all_gather | solution.py:91
  865.7 1.8 copy-start.3
  955.6 1.3 copy-start.4
Sparse Core Ops, SparseCore 0:
  9.7 35.7 all-gather.2
  69.1 83.5 reduce-scatter.4
  188.5 660.7 reduce-scatter.6
  852.5 97.2 all-gather.4

commit v2 on v1

v2 whole, which is shorter than its diff:
```python
import jax
import jax.numpy as jnp
from jax import lax
from jax.sharding import PartitionSpec as P

BLK = 128
F32 = jnp.float32
BF16 = jnp.bfloat16


def pick(mask, table):
    return jnp.sum(jnp.where(mask, table, 0), axis=-1)


def body(fock, lmo_coef, three_index, rotation, lmo_ids, domains):
    num_sets = lax.axis_size("col")
    my_row = lax.axis_index("row")
    my_col = lax.axis_index("col")
    dev_rows = lmo_coef.shape[0]
    occ_width = lmo_coef.shape[1]
    dev_blocks = dev_rows // BLK
    dom_blocks = domains.shape[1]
    dom_width = dom_blocks * BLK
    panel_fock = fock[:, 0, :]
    panel_blocks = panel_fock.shape[0] // BLK
    col_blocks = panel_fock.shape[1] // BLK

    doms = jnp.take(domains, lmo_ids, axis=0)
    present = doms >= 0
    clipped = jnp.maximum(doms, 0)
    flat = clipped // dev_blocks
    cset = flat % num_sets
    sub = clipped % dev_blocks
    panel = flat // num_sets
    row_tile = cset * dev_blocks + sub
    col_tile = panel * dev_blocks + sub
    set_range = jnp.arange(num_sets, dtype=jnp.int32)
    sub_range = jnp.arange(dev_blocks, dtype=jnp.int32)

    pres_k = lax.dynamic_index_in_dim(present, my_row, 2, keepdims=False)
    cset_k = lax.dynamic_index_in_dim(cset, my_row, 2, keepdims=False)
    sub_k = lax.dynamic_index_in_dim(sub, my_row, 2, keepdims=False)
    rtile_k = lax.dynamic_index_in_dim(row_tile, my_row, 2, keepdims=False)
    mine_k = pres_k & (cset_k == my_col)
    sel_a = jnp.any(mine_k[:, :, None] & (sub_k[:, :, None] == sub_range), axis=1).astype(BF16)
    mine2 = present & (cset == my_col)
    ct = pick(mine2, col_tile)
    ok_tile = jnp.any(mine2, axis=2) & pres_k
    fock_tiles = panel_fock.reshape(panel_blocks, BLK, col_blocks, BLK)
    tiles_a = fock_tiles[rtile_k, :, ct, :]
    tiles_a = jnp.where(ok_tile[:, :, None, None], tiles_a, jnp.zeros_like(tiles_a))
    in_rows = jnp.concatenate([lmo_coef, three_index], axis=1).reshape(dev_blocks, BLK, -1)
    rows_a = jnp.einsum("os,sbw->obw", sel_a, in_rows, preferred_element_type=F32).astype(BF16)
    tiles_a = tiles_a.transpose(0, 2, 1, 3).reshape(num_sets, BLK, -1)
    recv_a = lax.all_to_all(jnp.concatenate([rows_a, tiles_a], axis=2), "col", 0, 0, tiled=True)

    pres_o = lax.dynamic_index_in_dim(present, my_col, 0, keepdims=False)
    cset_o = lax.dynamic_index_in_dim(cset, my_col, 0, keepdims=False)
    from_set = (pres_o[:, :, None] & (cset_o[:, :, None] == set_range)).astype(BF16)
    from_k = lax.dynamic_index_in_dim(from_set, my_row, 1, keepdims=False)
    row_width = in_rows.shape[2]
    rows_b = jnp.einsum("js,sbw->jbw", from_k, recv_a[:, :, :row_width], preferred_element_type=F32).astype(BF16)
    tiles_in = recv_a[:, :, row_width:].reshape(num_sets, BLK, dom_blocks, BLK)
    tiles_b = jnp.einsum("jks,sajb->jakb", from_set, tiles_in, preferred_element_type=F32).astype(BF16)
    tiles_b = tiles_b.reshape(dom_blocks, BLK, dom_width)
    recv_b = lax.all_to_all(jnp.concatenate([rows_b, tiles_b], axis=2), "row", 0, 0, tiled=True)
    rows_dom = recv_b[:, :, :row_width].reshape(dom_width, row_width)
    domain_fock = recv_b[:, :, row_width:].reshape(dom_width, dom_width)

    gathered = lax.all_gather(lmo_coef, "row", axis=0, tiled=True)
    coef_b = lax.psum_scatter(
        jnp.dot(panel_fock, gathered, preferred_element_type=F32).astype(BF16),
        "col",
        scatter_dimension=0,
        tiled=True,
    )
    occ_term = jnp.einsum("ri,rj->ij", lmo_coef, coef_b, preferred_element_type=F32)
    occ_b = lax.psum(occ_term, ("row", "col")).astype(BF16)

    fc_blocks = coef_b.reshape(dev_blocks, BLK, occ_width)
    fc_a = jnp.einsum("os,sbw->obw", sel_a, fc_blocks, preferred_element_type=F32).astype(BF16)
    fc_a = lax.all_to_all(fc_a, "col", 0, 0, tiled=True)
    fc_b = jnp.einsum("js,sbw->jbw", from_k, fc_a, preferred_element_type=F32).astype(BF16)
    fc_dom = lax.all_to_all(fc_b, "row", 0, 0, tiled=True).reshape(dom_width, occ_width)

    coef_dom = rows_dom[:, :occ_width]
    three_dom = rows_dom[:, occ_width:]
    correction = jnp.dot(coef_dom, occ_b, preferred_element_type=F32)
    proj_dom = (fc_dom.astype(F32) - 0.5 * correction).astype(BF16)

    slot_rot = rotation[0, 0]
    fock_half = jnp.dot(domain_fock, slot_rot, preferred_element_type=F32).astype(BF16)
    fock_rot = jnp.einsum("xm,xn->mn", slot_rot, fock_half, preferred_element_type=F32)
    coef_rot = jnp.einsum("xm,xi->mi", slot_rot, coef_dom, preferred_element_type=F32).astype(BF16)
    proj_rot = jnp.einsum("xm,xi->mi", slot_rot, proj_dom, preferred_element_type=F32).astype(BF16)
    proj_fock = fock_rot - jnp.einsum("mi,ni->mn", coef_rot, proj_rot, preferred_element_type=F32)
    proj_fock = proj_fock - jnp.einsum("mi,ni->mn", proj_rot, coef_rot, preferred_element_type=F32)
    three_rot = jnp.einsum("xm,xu->mu", slot_rot, three_dom, preferred_element_type=F32).astype(BF16)
    return (proj_fock[None, None], three_rot[None, None])


def solution(mesh):
    placed = (
        P("row", "col", None),
        P(("row", "col"), None),
        P(("row", "col"), None),
        P("col", "row", None, None),
        P(),
        P(),
    )
    return jax.shard_map(
        body,
        mesh=mesh,
        in_specs=placed,
        out_specs=(P("col", "row", None, None), P("col", "row", None, None)),
        check_vma=False,
    )
```

time: 976 us -> 606 us (0.62)
  waiting for transfers between devices: 777 us -> 274 us
  blocking collectives: 0 us -> 111 us
  local copies, waits for them, and re-layouts: 61.3 us -> 94.2 us
  starting transfers between devices: 40.5 us -> 24.8 us
  other arithmetic: 5.96 us -> 16.3 us
    reduce_scatter x1 -> x0, waiting for transfers between devices: 458 us -> none  [body(): lax.psum_scatter(occ_term, ('row', 'col'), scatter_dimension=0, tiled=True)]
    psum x0 -> x1, blocking collectives: none -> 111 us  [body(): occ_b = lax.psum(occ_term, ('row', 'col')).astype(BF16)]
    all_gather x1 -> x0, waiting for transfers between devices: 68.5 us -> none  [body(): lax.all_gather(occ_part.astype(BF16), ('row', 'col'), axis=0, tiled=True)]
    all_to_all x6 -> x4, waiting for transfers between devices: 212 us -> 272 us  [the longest x1 168 us: body(): lax.all_to_all(jnp.concatenate([rows_a, tiles_a], axis=2), 'col', 0, 0, t...]
    all_gather x1, waiting for transfers between devices: 37.6 us -> 1.21 us  [body(): gathered = lax.all_gather(lmo_coef, 'row', axis=0, tiled=True)]
    concatenate x1 -> x4, local copies, waits for them, and re-layouts: 0.08 us -> 17.8 us  [the longest x1 13.7 us: body(): jnp.concatenate([rows_a, tiles_a], axis=2)]
    dot_general x9 -> x5, matrix products: 31.6 us -> 16 us  [the longest x1 4.6 us: body(): jnp.einsum('js,sbw->jbw', from_k, fc_a, preferred_element_type=F32)]
    reshape x0 -> x2, local copies, waits for them, and re-layouts: none -> 14.3 us  [the longest x1 7.43 us: body(): tiles_a = tiles_a.transpose(0, 2, 1, 3).reshape(num_sets, BLK, -1)]
  transfers between devices with their start and end apart: 10 -> 6, of which waited for: 8 -> 4; matrix products, arithmetic and copies ran while one was open for 10% -> 21% of each run, Pallas kernels for 0% -> 0%
where the time goes in v2:
time: 606 us; the launch traced here: 596 us
  waiting for transfers between devices  274 us (45%)
  blocking collectives  111 us (18%)
  local copies, waits for them, and re-layouts  94.2 us (16%)
  matrix products  60.7 us (10%)
  starting transfers between devices  24.8 us (4%)
  other arithmetic  16.3 us (3%)
  between operations  14.5 us (2%)
    all_to_all x1, waiting for transfers between devices, body(): lax.all_to_all(jnp.concatenate([rows_a, tiles_a], axis=2), 'col', 0, 0, t...  168 us
    psum x1, blocking collectives, body(): occ_b = lax.psum(occ_term, ('row', 'col')).astype(BF16)  111 us
    all_to_all x1, waiting for transfers between devices, body(): lax.all_to_all(jnp.concatenate([rows_b, tiles_b], axis=2), 'row', 0, 0, t...  53.3 us
    all_to_all x1, waiting for transfers between devices, body(): fc_a = lax.all_to_all(fc_a, 'col', 0, 0, tiled=True)  51.2 us
    dot_general x1, matrix products, body(): jnp.dot(panel_fock, gathered, preferred_element_type=F32).astype(BF16)  23.4 us
    unnamed x24, local copies, waits for them, and re-layouts  21 us
    concatenate x1, local copies, waits for them, and re-layouts, body(): jnp.concatenate([rows_a, tiles_a], axis=2)  13.7 us
  transfers between devices with their start and end apart: 6, of which 4 were waited for; matrix products, arithmetic and copies ran while one was open for 21% of the time, Pallas kernels for 0%

profile of v2, /device:TPU:1, one launch (start us, length us, event | category | flops | bytes accessed | tf_op | source)
XLA Modules:
  0.0 596.0 jit_solution(16878008167908243615)
XLA Ops:
  8.0 9.7 %copy.251 = bf16[512,8,16,128]{3,2,1,0:T(8,128)(2,1)S(1)} copy(bf16[512,8,16,128]{3,1,2,0:T(8,128)(2,1)} %bitcast.92) | data formatting | bytes 33554432
  17.7 8.1 %copy.221 = bf16[32,128,16,128]{3,1,2,0:T(8,128)(2,1)} copy(bf16[32,128,16,128]{3,2,1,0:T(8,128)(2,1)S(1)} %bitcast.90) | data formatting | bytes 33554432 | tf_op jit(solution)/shard_map/reshape;squeeze | solution.py:49
  27.3 9.1 %gather_fusion.1 = bf16[128,128,128]{2,1,0:T(8,128)(2,1)} fusion(bf16[32,128,16,128]{3,1,2,0:T(8,128)(2,1)} %copy.221, s32[128]{0:T(128)S(1)} %reshape.73), kind=kCustom, calls=%fused_computation.1 | custom fusion | bytes 8389632 | tf_op jit(solution)/shard_map/gather | solution.py:50
  36.5 7.8 %fusion.10 = bf16[16,128,8,128]{3,2,0,1:T(8,128)(2,1)} fusion(bf16[16,8,128,128]{3,2,1,0:T(8,128)(2,1)} %bitcast.91, pred[16,8]{1,0:T(8,128)(4,1)S(1)} %and.71), kind=kLoop, calls=%fused_computation.15 | loop fusion | flops 2097152 | bytes 8388736 | tf_op jit(solution)/shard_map/jit(_where)/select_n | solution.py:51
  45.5 23.4 %fusion.2 = bf16[4096,1024]{1,0:T(8,128)(2,1)} fusion(bf16[2048,1024]{1,0:T(8,128)(2,1)} %all-gather.2.cloned.1.call-done, bf16[4096,1,2048]{2,0,1:T(8,128)(2,1)} %param.6), kind=kOutput, calls=%fused_computation.5 | convolution fusion | flops 17184063488 | bytes 29360128 | tf_op jit(solution)/shard_map/dot_general | solution.py:72
  69.0 7.4 %reshape.58 = bf16[16,128,1024]{2,0,1:T(8,128)(2,1)} reshape(bf16[16,128,8,128]{3,2,0,1:T(8,128)(2,1)} %fusion.10) | data formatting | bytes 8388608 | tf_op jit(solution)/shard_map/reshape | solution.py:54
  78.9 7.7 %pad_maximum_fusion = bf16[16,128,2560]{2,0,1:T(8,128)(2,1)} fusion(bf16[16,128,1024]{2,0,1:T(8,128)(2,1)S(1)} %copy-done.1, bf16[16,128,1536]{2,0,1:T(8,128)(2,1)S(1)} %convolution_convert_fusion), kind=kLoop, calls=%fused_computation.4 | loop fusion | flops 20971520 | bytes 20971520 | tf_op jit(solution)/shard_map/concatenate | solution.py:55
  86.6 13.7 %copy.223 = bf16[16,128,2560]{2,1,0:T(8,128)(2,1)} copy(bf16[16,128,2560]{2,0,1:T(8,128)(2,1)} %pad_maximum_fusion) | data formatting | bytes 20971520 | tf_op jit(solution)/shard_map/concatenate | solution.py:55
  100.4 8.1 %all-to-all-start = ((bf16[16,128,2560]{2,1,0:T(8,128)(2,1)}), bf16[16,128,2560]{2,1,0:T(8,128)(2,1)}, u32[]{:S(2)}, u32[]{:S(2)}) async-start(bf16[16,128,2560]{2,1,0:T(8,128)(2,1)} %copy.223), calls=%async_computation | async-start | bytes 20971520 | tf_op jit(solution)/shard_map/all_to_all | solution.py:55
  108.9 167.8 %all-to-all-done = bf16[16,128,2560]{2,1,0:T(8,128)(2,1)} async-done(((bf16[16,128,2560]{2,1,0:T(8,128)(2,1)}), bf16[16,128,2560]{2,1,0:T(8,128)(2,1)}, u32[]{:S(2)}, u32[]{:S(2)}) %all-to-all-start) | async-done | bytes 10485792 | tf_op jit(solution)/shard_map/all_to_all | solution.py:55
  276.8 4.7 slice.29
  281.5 6.4 %copy.250 = bf16[16,128,1024]{1,2,0:T(8,128)(2,1)} copy(bf16[16,128,1024]{2,1,0:T(8,128)(2,1)} %slice.29) | data formatting | bytes 8388608
  288.0 6.8 %copy.226 = bf16[16,128,8,128]{3,0,1,2:T(8,128)(2,1)} copy(bf16[16,128,8,128]{1,3,2,0:T(8,128)(2,1)} %bitcast.93) | data formatting | bytes 8388608 | tf_op jit(solution)/shard_map/reshape | solution.py:63
  294.8 3.0 convert_bitcast_fusion
  297.7 2.4 copy.270
  300.2 3.4 slice.28
  303.6 3.6 fusion.11
  307.6 3.9 copy.229
  311.5 6.0 %all-to-all-start.1 = ((bf16[8,128,2560]{2,1,0:T(8,128)(2,1)}), bf16[8,128,2560]{2,1,0:T(8,128)(2,1)}, u32[]{:S(2)}, u32[]{:S(2)}) async-start(bf16[8,128,2560]{2,1,0:T(8,128)(2,1)} %copy.229), calls=%async_computation.1 | async-start | bytes 10485760 | tf_op jit(solution)/shard_map/all_to_all | solution.py:66
  319.9 4.4 copy.231
  324.2 53.3 %all-to-all-done.1 = bf16[8,128,2560]{2,1,0:T(8,128)(2,1)} async-done(((bf16[8,128,2560]{2,1,0:T(8,128)(2,1)}), bf16[8,128,2560]{2,1,0:T(8,128)(2,1)}, u32[]{:S(2)}, u32[]{:S(2)}) %all-to-all-start.1) | async-done | bytes 5242912 | tf_op jit(solution)/shard_map/all_to_all | solution.py:66
  377.5 4.6 all-to-all-start.2
  382.1 3.1 slice.30
  388.9 4.4 convolution_bitcast_fusion.1
  393.2 51.2 %all-to-all-done.2 = bf16[16,128,1024]{2,1,0:T(8,128)(2,1)} async-done(((bf16[16,128,1024]{2,1,0:T(8,128)(2,1)}), bf16[16,128,1024]{2,1,0:T(8,128)(2,1)}, u32[]{:S(2)}, u32[]{:S(2)}) %all-to-all-start.2) | async-done | bytes 4194336 | tf_op jit(solution)/shard_map/all_to_all | solution.py:82
  444.5 4.6 fusion.15
  449.1 2.5 copy.233
  451.6 6.1 %all-to-all-start.3 = ((bf16[8,128,1024]{2,1,0:T(8,128)(2,1)}), bf16[8,128,1024]{2,1,0:T(8,128)(2,1)}, u32[]{:S(2)}, u32[]{:S(2)}) async-start(bf16[8,128,1024]{2,1,0:T(8,128)(2,1)} %copy.233), calls=%async_computation.4 | async-start | bytes 4194304 | tf_op jit(solution)/shard_map/all_to_all | solution.py:84
  457.7 2.8 fusion.25
  462.5 2.7 convolution_bitcast_fusion
  465.2 111.2 %all-reduce.1 = bf16[1024,1024]{0,1:T(8,128)(2,1)} all-reduce(f32[1024,1024]{0,1:T(8,128)} %convolution_bitcast_fusion), channel_id=1, replica_groups=mesh['row'=8,'col'=16] {'row','col'}, use_global_device_ids=true, to_apply=%region_4.5 | all-reduce | flops 1048576 | bytes 6291456 | tf_op jit(solution)/shard_map/psum | solution.py:78
  576.4 6.3 %convolution_convert_fusion.2 = bf16[1024,512]{1,0:T(8,128)(2,1)S(1)} fusion(bf16[1,1,1024,512]{3,2,1,0:T(8,128)(2,1)S(1)} %copy-done, bf16[1024,1024]{1,0:T(8,128)(2,1)} %bitcast.30, bf16[1024,1024]{0,1:T(8,128)(2,1)} %all-reduce.1, bf16[1024,1536]{1,0:T(8,128)(2,1)} %bitcast.99), kind=kOutput, calls=%fused_computation.27 | convolution fusion | flops 3225944064 | bytes 8388608 | tf_op jit(solution)/shard_map/xm,xi->mi/dot_general | solution.py:95
  (58 shorter events, 21.3 us)
Async XLA Ops:
  7.2 380.1 %copy-start = (bf16[1,1,1024,512]{3,2,1,0:T(8,128)(2,1)S(1)}, bf16[1,1,1024,512]{3,2,1,0:T(8,128)(2,1)}, u32[]{:S(2)}) copy-start(bf16[1,1,1024,512]{3,2,1,0:T(8,128)(2,1)} %param.9) | copy-start | bytes 3145732
  7.2 38.3 %all-gather.2.cloned.1.call-start = ((), (), s32[]{:S(2)}) async-start(), calls=%async_computation.5 | async-start | bytes 4718592 | tf_op jit(solution)/shard_map/all_gather | solution.py:70
  7.9 309.5 %reduce-scatter.2.cloned.1.call-start = ((), (), s32[]{:S(2)}) async-start(), calls=%async_computation.6 | async-start | bytes 8912896 | tf_op jit(solution)/shard_map/reduce_scatter | solution.py:71
  17.6 8.2 %copy-start.8 = (s32[128,8]{0,1:T(8,128)S(1)}, s32[128,8]{0,1:T(8,128)}, u32[]{:S(2)}) copy-start(s32[128,8]{0,1:T(8,128)} %param.11) | copy-start | bytes 12292
  17.6 8.2 %copy-start.7 = (s32[16,8]{0,1:T(8,128)S(1)}, s32[16,8]{0,1:T(8,128)}, u32[]{:S(2)}) copy-start(s32[16,8]{0,1:T(8,128)} %param.10) | copy-start | bytes 1540
  69.0 7.5 %copy-start.2 = (bf16[256,1024]{1,0:T(8,128)(2,1)S(1)}, bf16[256,1024]{1,0:T(8,128)(2,1)}, u32[]{:S(2)}) copy-start(bf16[256,1024]{1,0:T(8,128)(2,1)} %param.7) | copy-start | bytes 1572868
  69.0 7.4 %copy-start.6 = (bf16[256,512]{1,0:T(8,128)(2,1)S(1)}, bf16[256,512]{1,0:T(8,128)(2,1)}, u32[]{:S(2)}) copy-start(bf16[256,512]{1,0:T(8,128)(2,1)} %param.8) | copy-start | bytes 786436
  76.4 2.5 copy-start.1
  100.4 176.4 %all-to-all-start = ((bf16[16,128,2560]{2,1,0:T(8,128)(2,1)}), bf16[16,128,2560]{2,1,0:T(8,128)(2,1)}, u32[]{:S(2)}, u32[]{:S(2)}) async-start(bf16[16,128,2560]{2,1,0:T(8,128)(2,1)} %copy.223), calls=%async_computation | async-start | bytes 20971520 | tf_op jit(solution)/shard_map/all_to_all | solution.py:55
  311.5 66.1 %all-to-all-start.1 = ((bf16[8,128,2560]{2,1,0:T(8,128)(2,1)}), bf16[8,128,2560]{2,1,0:T(8,128)(2,1)}, u32[]{:S(2)}, u32[]{:S(2)}) async-start(bf16[8,128,2560]{2,1,0:T(8,128)(2,1)} %copy.229), calls=%async_computation.1 | async-start | bytes 10485760 | tf_op jit(solution)/shard_map/all_to_all | solution.py:66
  377.5 67.0 %all-to-all-start.2 = ((bf16[16,128,1024]{2,1,0:T(8,128)(2,1)}), bf16[16,128,1024]{2,1,0:T(8,128)(2,1)}, u32[]{:S(2)}, u32[]{:S(2)}) async-start(bf16[16,128,1024]{2,1,0:T(8,128)(2,1)} %copy.231), calls=%async_computation.3 | async-start | bytes 8388608 | tf_op jit(solution)/shard_map/all_to_all | solution.py:82
  387.3 1.6 copy-start.5
  451.6 10.9 %copy-start.4 = (bf16[256,1024]{1,0:T(8,128)(2,1)S(1)}, bf16[256,1024]{1,0:T(8,128)(2,1)}, u32[]{:S(2)}) copy-start(bf16[256,1024]{1,0:T(8,128)(2,1)} %reduce-scatter.2.cloned.1.call-done) | copy-start | bytes 1572868
  451.6 124.8 %all-to-all-start.3 = ((bf16[8,128,1024]{2,1,0:T(8,128)(2,1)}), bf16[8,128,1024]{2,1,0:T(8,128)(2,1)}, u32[]{:S(2)}, u32[]{:S(2)}) async-start(bf16[8,128,1024]{2,1,0:T(8,128)(2,1)} %copy.233), calls=%async_computation.4 | async-start | bytes 4194304 | tf_op jit(solution)/shard_map/all_to_all | solution.py:84
  582.7 1.0 copy-start.3
Sparse Core Ops, SparseCore 0:
  9.7 35.7 all-gather.1
  69.1 228.8 reduce-scatter.1

commit v3 on v2

--- a/solution.py
+++ b/solution.py
@@ -63,11 +63,9 @@
     tiles_in = recv_a[:, :, row_width:].reshape(num_sets, BLK, dom_blocks, BLK)
     tiles_b = jnp.einsum("jks,sajb->jakb", from_set, tiles_in, preferred_element_type=F32).astype(BF16)
     tiles_b = tiles_b.reshape(dom_blocks, BLK, dom_width)
-    recv_b = lax.all_to_all(jnp.concatenate([rows_b, tiles_b], axis=2), "row", 0, 0, tiled=True)
-    rows_dom = recv_b[:, :, :row_width].reshape(dom_width, row_width)
-    domain_fock = recv_b[:, :, row_width:].reshape(dom_width, dom_width)
 
     gathered = lax.all_gather(lmo_coef, "row", axis=0, tiled=True)
+    rows_b, tiles_b, gathered = lax.optimization_barrier((rows_b, tiles_b, gathered))
     coef_b = lax.psum_scatter(
         jnp.dot(panel_fock, gathered, preferred_element_type=F32).astype(BF16),
         "col",
@@ -81,7 +79,10 @@
     fc_a = jnp.einsum("os,sbw->obw", sel_a, fc_blocks, preferred_element_type=F32).astype(BF16)
     fc_a = lax.all_to_all(fc_a, "col", 0, 0, tiled=True)
     fc_b = jnp.einsum("js,sbw->jbw", from_k, fc_a, preferred_element_type=F32).astype(BF16)
-    fc_dom = lax.all_to_all(fc_b, "row", 0, 0, tiled=True).reshape(dom_width, occ_width)
+    recv_b = lax.all_to_all(jnp.concatenate([rows_b, tiles_b, fc_b], axis=2), "row", 0, 0, tiled=True)
+    rows_dom = recv_b[:, :, :row_width].reshape(dom_width, row_width)
+    domain_fock = recv_b[:, :, row_width : row_width + dom_width].reshape(dom_width, dom_width)
+    fc_dom = recv_b[:, :, row_width + dom_width :].reshape(dom_width, occ_width)
 
     coef_dom = rows_dom[:, :occ_width]
     three_dom = rows_dom[:, occ_width:]

time: 606 us -> 679 us (1.12)
  blocking collectives: 111 us -> 227 us
  waiting for transfers between devices: 274 us -> 239 us
  starting transfers between devices: 24.8 us -> 15.9 us
    all_to_all x3 -> x1, waiting for transfers between devices: 105 us -> 0.01 us  [body(): lax.all_to_all(jnp.concatenate([rows_b, tiles_b, fc_b], axis=2), 'row', 0...]
    reduce_scatter x1, waiting for transfers between devices: 0.02 us -> 84.8 us  [body(): lax.psum_scatter(jnp.dot(panel_fock, gathered, preferred_element_type=F32...]
    psum x1, blocking collectives: 111 us -> 172 us  [body(): occ_b = lax.psum(occ_term, ('row', 'col')).astype(BF16)]
    all_to_all x0 -> x1, blocking collectives: none -> 55.1 us  [body(): fc_a = lax.all_to_all(fc_a, 'col', 0, 0, tiled=True)]
    all_to_all x1, waiting for transfers between devices: 168 us -> 153 us  [body(): lax.all_to_all(jnp.concatenate([rows_a, tiles_a], axis=2), 'col', 0, 0, t...]
    all_to_all x3 -> x1, starting transfers between devices: 16.6 us -> 7.37 us  [body(): lax.all_to_all(jnp.concatenate([rows_b, tiles_b, fc_b], axis=2), 'row', 0...]
    unnamed x24 -> x26, local copies, waits for them, and re-layouts: 21 us -> 21.2 us
  transfers between devices with their start and end apart: 6 -> 4, of which waited for: 4 -> 2; matrix products, arithmetic and copies ran while one was open for 21% -> 5% of each run, Pallas kernels for 0% -> 0%
where the time goes in v3:
time: 679 us; the launch traced here: 671 us
  waiting for transfers between devices  239 us (35%)
  blocking collectives  227 us (33%)
  local copies, waits for them, and re-layouts  97.6 us (14%)
  matrix products  59 us (9%)
  other arithmetic  17.6 us (3%)
  starting transfers between devices  15.9 us (2%)
  between operations  14.5 us (2%)
    psum x1, blocking collectives, body(): occ_b = lax.psum(occ_term, ('row', 'col')).astype(BF16)  172 us
    all_to_all x1, waiting for transfers between devices, body(): lax.all_to_all(jnp.concatenate([rows_a, tiles_a], axis=2), 'col', 0, 0, t...  153 us
    reduce_scatter x1, waiting for transfers between devices, body(): lax.psum_scatter(jnp.dot(panel_fock, gathered, preferred_element_type=F32...  84.8 us
    all_to_all x1, blocking collectives, body(): fc_a = lax.all_to_all(fc_a, 'col', 0, 0, tiled=True)  55.1 us
    dot_general x1, matrix products, body(): jnp.dot(panel_fock, gathered, preferred_element_type=F32).astype(BF16)  23.5 us
    unnamed x26, local copies, waits for them, and re-layouts  21.2 us
    concatenate x1, local copies, waits for them, and re-layouts, body(): jnp.concatenate([rows_a, tiles_a], axis=2)  13.6 us
  transfers between devices with their start and end apart: 4, of which 2 were waited for; matrix products, arithmetic and copies ran while one was open for 5% of the time, Pallas kernels for 0%

profile of v3, /device:TPU:1, one launch (start us, length us, event | category | flops | bytes accessed | tf_op | source)
XLA Modules:
  0.0 670.6 jit_solution(590415783933990857)
XLA Ops:
  8.7 9.6 %copy.246 = bf16[512,8,16,128]{3,2,1,0:T(8,128)(2,1)S(1)} copy(bf16[512,8,16,128]{3,1,2,0:T(8,128)(2,1)} %bitcast.96) | data formatting | bytes 33554432
  18.3 8.1 %copy.217 = bf16[32,128,16,128]{3,1,2,0:T(8,128)(2,1)} copy(bf16[32,128,16,128]{3,2,1,0:T(8,128)(2,1)S(1)} %bitcast.94) | data formatting | bytes 33554432 | tf_op jit(solution)/shard_map/reshape;squeeze | solution.py:49
  28.0 8.8 %gather_fusion.1 = bf16[128,128,128]{2,1,0:T(8,128)(2,1)} fusion(bf16[32,128,16,128]{3,1,2,0:T(8,128)(2,1)} %copy.217, s32[128]{0:T(128)S(1)} %reshape.73), kind=kCustom, calls=%fused_computation.1 | custom fusion | bytes 8389632 | tf_op jit(solution)/shard_map/gather | solution.py:50
  36.8 7.8 %fusion.9 = bf16[16,128,8,128]{3,2,0,1:T(8,128)(2,1)} fusion(bf16[16,8,128,128]{3,2,1,0:T(8,128)(2,1)} %bitcast.95, pred[16,8]{1,0:T(8,128)(4,1)S(1)} %and.71), kind=kLoop, calls=%fused_computation.15 | loop fusion | flops 2097152 | bytes 8388736 | tf_op jit(solution)/shard_map/jit(_where)/select_n | solution.py:51
  44.6 7.4 %reshape.58 = bf16[16,128,1024]{2,0,1:T(8,128)(2,1)} reshape(bf16[16,128,8,128]{3,2,0,1:T(8,128)(2,1)} %fusion.9) | data formatting | bytes 8388608 | tf_op jit(solution)/shard_map/reshape | solution.py:54
  52.1 2.4 convolution_convert_fusion
  54.6 7.5 %pad_maximum_fusion = bf16[16,128,2560]{2,0,1:T(8,128)(2,1)} fusion(bf16[16,128,1024]{2,0,1:T(8,128)(2,1)S(1)} %copy-done.1, bf16[16,128,1536]{2,0,1:T(8,128)(2,1)S(1)} %convolution_convert_fusion), kind=kLoop, calls=%fused_computation.4 | loop fusion | flops 20971520 | bytes 20971520 | tf_op jit(solution)/shard_map/concatenate | solution.py:55
  62.1 13.6 %copy.219 = bf16[16,128,2560]{2,1,0:T(8,128)(2,1)} copy(bf16[16,128,2560]{2,0,1:T(8,128)(2,1)} %pad_maximum_fusion) | data formatting | bytes 20971520 | tf_op jit(solution)/shard_map/concatenate | solution.py:55
  75.7 8.5 %all-to-all-start = ((bf16[16,128,2560]{2,1,0:T(8,128)(2,1)}), bf16[16,128,2560]{2,1,0:T(8,128)(2,1)}, u32[]{:S(2)}, u32[]{:S(2)}) async-start(bf16[16,128,2560]{2,1,0:T(8,128)(2,1)} %copy.219), calls=%async_computation | async-start | bytes 20971520 | tf_op jit(solution)/shard_map/all_to_all | solution.py:55
  85.5 153.3 %all-to-all-done = bf16[16,128,2560]{2,1,0:T(8,128)(2,1)} async-done(((bf16[16,128,2560]{2,1,0:T(8,128)(2,1)}), bf16[16,128,2560]{2,1,0:T(8,128)(2,1)}, u32[]{:S(2)}, u32[]{:S(2)}) %all-to-all-start) | async-done | bytes 10485792 | tf_op jit(solution)/shard_map/all_to_all | solution.py:55
  238.7 4.8 slice.33
  243.5 6.6 copy.245
  250.1 6.8 %copy.222 = bf16[16,128,8,128]{3,0,1,2:T(8,128)(2,1)} copy(bf16[16,128,8,128]{1,3,2,0:T(8,128)(2,1)} %bitcast.97) | data formatting | bytes 8388608 | tf_op jit(solution)/shard_map/reshape | solution.py:63
  256.9 2.9 convert_bitcast_fusion.1
  259.8 2.4 copy.263
  262.2 3.4 slice.32
  265.6 5.3 fusion.10
  270.9 23.5 %convert_bitcast_fusion = bf16[4096,1024]{0,1:T(8,128)(2,1)} fusion(bf16[2048,1024]{1,0:T(8,128)(2,1)} %all-gather.2.cloned.1.call-done, bf16[4096,1,2048]{2,0,1:T(8,128)(2,1)} %param.6), kind=kOutput, calls=%fused_computation.5 | convolution fusion | flops 17184063488 | bytes 29360128 | tf_op jit(solution)/shard_map/dot_general | solution.py:70
  294.5 84.8 %reduce-scatter.2.cloned.1.call-done = bf16[256,1024]{0,1:T(8,128)(2,1)} async-done(((bf16[4096,1024]{0,1:T(8,128)(2,1)}), bf16[256,1024]{0,1:T(8,128)(2,1)}) %reduce-scatter.2.cloned.1.call-update) | async-done | bytes 524304 | tf_op jit(solution)/shard_map/reduce_scatter | solution.py:69
  381.2 3.0 copy.225
  384.2 2.4 convolution_convert_fusion.1
  386.6 2.3 copy.226
  388.9 55.1 %all_to_all.15 = bf16[16,128,1024]{2,1,0:T(8,128)(2,1)S(1)} all-to-all(bf16[16,128,1024]{2,1,0:T(8,128)(2,1)S(1)} %copy.226), channel_id=1, replica_groups=mesh['row'=8,'col'=16] {'col'}, dimensions={0} | all-to-all | bytes 8388608 | tf_op jit(solution)/shard_map/all_to_all | solution.py:80
  444.0 2.4 fusion.14
  447.0 5.2 copy.228
  452.2 7.4 %all-to-all-start.2 = ((bf16[8,128,3584]{2,1,0:T(8,128)(2,1)}), bf16[8,128,3584]{2,1,0:T(8,128)(2,1)}, u32[]{:S(2)}, u32[]{:S(2)}) async-start(bf16[8,128,3584]{2,1,0:T(8,128)(2,1)} %copy.228), calls=%async_computation.3 | async-start | bytes 14680064 | tf_op jit(solution)/shard_map/all_to_all | solution.py:82
  459.5 2.7 convolution_bitcast_fusion
  462.2 172.1 %all-reduce.1 = bf16[1024,1024]{0,1:T(8,128)(2,1)} all-reduce(f32[1024,1024]{0,1:T(8,128)} %convolution_bitcast_fusion), channel_id=1, replica_groups=mesh['row'=8,'col'=16] {'row','col'}, use_global_device_ids=true, to_apply=%region_4.5 | all-reduce | flops 1048576 | bytes 6291456 | tf_op jit(solution)/shard_map/psum | solution.py:76
  634.3 2.1 slice.35
  639.6 4.9 fusion.65
  644.5 4.3 convolution_bitcast_fusion.1
  648.9 6.3 convolution_convert_fusion.2
  (58 shorter events, 18.4 us)
Async XLA Ops:
  7.2 629.3 %copy-start = (bf16[1,1,1024,512]{3,2,1,0:T(8,128)(2,1)S(1)}, bf16[1,1,1024,512]{3,2,1,0:T(8,128)(2,1)}, u32[]{:S(2)}) copy-start(bf16[1,1,1024,512]{3,2,1,0:T(8,128)(2,1)} %param.9) | copy-start | bytes 3145732
  18.3 8.1 %copy-start.9 = (s32[128,8]{0,1:T(8,128)S(1)}, s32[128,8]{0,1:T(8,128)}, u32[]{:S(2)}) copy-start(s32[128,8]{0,1:T(8,128)} %param.11) | copy-start | bytes 12292
  44.6 7.4 %copy-start.3 = (bf16[256,1024]{1,0:T(8,128)(2,1)S(1)}, bf16[256,1024]{1,0:T(8,128)(2,1)}, u32[]{:S(2)}) copy-start(bf16[256,1024]{1,0:T(8,128)(2,1)} %param.7) | copy-start | bytes 1572868
  44.6 7.4 %copy-start.8 = (bf16[256,512]{1,0:T(8,128)(2,1)S(1)}, bf16[256,512]{1,0:T(8,128)(2,1)}, u32[]{:S(2)}) copy-start(bf16[256,512]{1,0:T(8,128)(2,1)} %param.8) | copy-start | bytes 786436
  52.0 2.5 copy-start.1
  75.7 163.0 %all-to-all-start = ((bf16[16,128,2560]{2,1,0:T(8,128)(2,1)}), bf16[16,128,2560]{2,1,0:T(8,128)(2,1)}, u32[]{:S(2)}, u32[]{:S(2)}) async-start(bf16[16,128,2560]{2,1,0:T(8,128)(2,1)} %copy.219), calls=%async_computation | async-start | bytes 20971520 | tf_op jit(solution)/shard_map/all_to_all | solution.py:55
  84.2 186.8 %all-gather.2.cloned.1.call-start = ((), (), s32[]{:S(2)}) async-start(), calls=%async_computation.4 | async-start | bytes 4718592 | tf_op jit(solution)/shard_map/all_gather | solution.py:67
  84.9 294.4 %reduce-scatter.2.cloned.1.call-start = ((), (), s32[]{:S(2)}) async-start(), calls=%async_computation.5 | async-start | bytes 8912896 | tf_op jit(solution)/shard_map/reduce_scatter | solution.py:69
  444.0 2.4 copy-start.2
  452.1 7.4 %copy-start.4 = (bf16[256,1024]{1,0:T(8,128)(2,1)S(1)}, bf16[256,1024]{1,0:T(8,128)(2,1)}, u32[]{:S(2)}) copy-start(bf16[256,1024]{1,0:T(8,128)(2,1)} %param.7) | copy-start | bytes 1572868
  452.1 7.4 %copy-start.6 = (bf16[256,1024]{0,1:T(8,128)(2,1)S(1)}, bf16[256,1024]{0,1:T(8,128)(2,1)}, u32[]{:S(2)}) copy-start(bf16[256,1024]{0,1:T(8,128)(2,1)} %reduce-scatter.2.cloned.1.call-done) | copy-start | bytes 1572868
  452.2 182.2 %all-to-all-start.2 = ((bf16[8,128,3584]{2,1,0:T(8,128)(2,1)}), bf16[8,128,3584]{2,1,0:T(8,128)(2,1)}, u32[]{:S(2)}, u32[]{:S(2)}) async-start(bf16[8,128,3584]{2,1,0:T(8,128)(2,1)} %copy.228), calls=%async_computation.3 | async-start | bytes 14680064 | tf_op jit(solution)/shard_map/all_to_all | solution.py:82
  636.4 1.7 copy-start.7
  655.2 1.0 copy-start.5
Sparse Core Ops, SparseCore 0:
  86.7 34.4 all-gather.1
  294.6 84.6 reduce-scatter.1

commit v4 on v2

--- a/solution.py
+++ b/solution.py
@@ -42,7 +42,8 @@
     sub_k = lax.dynamic_index_in_dim(sub, my_row, 2, keepdims=False)
     rtile_k = lax.dynamic_index_in_dim(row_tile, my_row, 2, keepdims=False)
     mine_k = pres_k & (cset_k == my_col)
-    sel_a = jnp.any(mine_k[:, :, None] & (sub_k[:, :, None] == sub_range), axis=1).astype(BF16)
+    has_o = jnp.any(mine_k, axis=1)
+    sub_o = pick(mine_k, sub_k)
     mine2 = present & (cset == my_col)
     ct = pick(mine2, col_tile)
     ok_tile = jnp.any(mine2, axis=2) & pres_k
@@ -50,22 +51,27 @@
     tiles_a = fock_tiles[rtile_k, :, ct, :]
     tiles_a = jnp.where(ok_tile[:, :, None, None], tiles_a, jnp.zeros_like(tiles_a))
     in_rows = jnp.concatenate([lmo_coef, three_index], axis=1).reshape(dev_blocks, BLK, -1)
-    rows_a = jnp.einsum("os,sbw->obw", sel_a, in_rows, preferred_element_type=F32).astype(BF16)
-    tiles_a = tiles_a.transpose(0, 2, 1, 3).reshape(num_sets, BLK, -1)
-    recv_a = lax.all_to_all(jnp.concatenate([rows_a, tiles_a], axis=2), "col", 0, 0, tiled=True)
+    rows_a = jnp.take(in_rows, sub_o, axis=0)
+    rows_a = jnp.where(has_o[:, None, None], rows_a, jnp.zeros_like(rows_a))
+    rows_a, tiles_a = (
+        lax.all_to_all(rows_a, "col", 0, 0, tiled=True),
+        lax.all_to_all(tiles_a, "col", 0, 0, tiled=True),
+    )
 
     pres_o = lax.dynamic_index_in_dim(present, my_col, 0, keepdims=False)
     cset_o = lax.dynamic_index_in_dim(cset, my_col, 0, keepdims=False)
-    from_set = (pres_o[:, :, None] & (cset_o[:, :, None] == set_range)).astype(BF16)
-    from_k = lax.dynamic_index_in_dim(from_set, my_row, 1, keepdims=False)
-    row_width = in_rows.shape[2]
-    rows_b = jnp.einsum("js,sbw->jbw", from_k, recv_a[:, :, :row_width], preferred_element_type=F32).astype(BF16)
-    tiles_in = recv_a[:, :, row_width:].reshape(num_sets, BLK, dom_blocks, BLK)
-    tiles_b = jnp.einsum("jks,sajb->jakb", from_set, tiles_in, preferred_element_type=F32).astype(BF16)
-    tiles_b = tiles_b.reshape(dom_blocks, BLK, dom_width)
-    recv_b = lax.all_to_all(jnp.concatenate([rows_b, tiles_b], axis=2), "row", 0, 0, tiled=True)
-    rows_dom = recv_b[:, :, :row_width].reshape(dom_width, row_width)
-    domain_fock = recv_b[:, :, row_width:].reshape(dom_width, dom_width)
+    pres_jk = lax.dynamic_index_in_dim(pres_o, my_row, 1, keepdims=False)
+    cset_jk = lax.dynamic_index_in_dim(cset_o, my_row, 1, keepdims=False)
+    rows_b = jnp.take(rows_a, cset_jk, axis=0)
+    rows_b = jnp.where(pres_jk[:, None, None], rows_b, jnp.zeros_like(rows_b))
+    slot_ids = jnp.broadcast_to(jnp.arange(dom_blocks, dtype=jnp.int32)[:, None], cset_o.shape)
+    tiles_b = tiles_a[cset_o, slot_ids]
+    tiles_b = jnp.where(pres_o[:, :, None, None], tiles_b, jnp.zeros_like(tiles_b))
+    rows_dom, tiles_dom = (
+        lax.all_to_all(rows_b, "row", 0, 0, tiled=True),
+        lax.all_to_all(tiles_b, "row", 0, 0, tiled=True),
+    )
+    rows_dom = rows_dom.reshape(dom_width, -1)
 
     gathered = lax.all_gather(lmo_coef, "row", axis=0, tiled=True)
     coef_b = lax.psum_scatter(
@@ -77,10 +83,11 @@
     occ_term = jnp.einsum("ri,rj->ij", lmo_coef, coef_b, preferred_element_type=F32)
     occ_b = lax.psum(occ_term, ("row", "col")).astype(BF16)
 
-    fc_blocks = coef_b.reshape(dev_blocks, BLK, occ_width)
-    fc_a = jnp.einsum("os,sbw->obw", sel_a, fc_blocks, preferred_element_type=F32).astype(BF16)
+    fc_a = jnp.take(coef_b.reshape(dev_blocks, BLK, occ_width), sub_o, axis=0)
+    fc_a = jnp.where(has_o[:, None, None], fc_a, jnp.zeros_like(fc_a))
     fc_a = lax.all_to_all(fc_a, "col", 0, 0, tiled=True)
-    fc_b = jnp.einsum("js,sbw->jbw", from_k, fc_a, preferred_element_type=F32).astype(BF16)
+    fc_b = jnp.take(fc_a, cset_jk, axis=0)
+    fc_b = jnp.where(pres_jk[:, None, None], fc_b, jnp.zeros_like(fc_b))
     fc_dom = lax.all_to_all(fc_b, "row", 0, 0, tiled=True).reshape(dom_width, occ_width)
 
     coef_dom = rows_dom[:, :occ_width]
@@ -89,7 +96,9 @@
     proj_dom = (fc_dom.astype(F32) - 0.5 * correction).astype(BF16)
 
     slot_rot = rotation[0, 0]
-    fock_half = jnp.dot(domain_fock, slot_rot, preferred_element_type=F32).astype(BF16)
+    rot_tiles = slot_rot.reshape(dom_blocks, BLK, -1)
+    fock_half = jnp.einsum("abtu,bun->atn", tiles_dom, rot_tiles, preferred_element_type=F32)
+    fock_half = fock_half.reshape(dom_width, -1).astype(BF16)
     fock_rot = jnp.einsum("xm,xn->mn", slot_rot, fock_half, preferred_element_type=F32)
     coef_rot = jnp.einsum("xm,xi->mi", slot_rot, coef_dom, preferred_element_type=F32).astype(BF16)
     proj_rot = jnp.einsum("xm,xi->mi", slot_rot, proj_dom, preferred_element_type=F32).astype(BF16)

time: 606 us -> 578 us (0.954); the launches traced: 596 us -> 576 us
  local copies, waits for them, and re-layouts: 94.2 us -> 52 us
  waiting for transfers between devices: 274 us -> 295 us
  matrix products: 60.7 us -> 45.1 us
  other arithmetic: 16.3 us -> 24.3 us
  starting transfers between devices: 24.8 us -> 32.4 us
    all_gather x1, waiting for transfers between devices: 1.21 us -> 37.6 us  [body(): gathered = lax.all_gather(lmo_coef, 'row', axis=0, tiled=True)]
    all_to_all x2 -> x4, waiting for transfers between devices: 221 us -> 201 us  [the longest x1 94.1 us: body(): lax.all_to_all(rows_a, 'col', 0, 0, tiled=True)]
    select_n x0 -> x7, other arithmetic: none -> 19.4 us  [the longest x1 6.38 us: body(): rows_a = jnp.where(has_o[:, None, None], rows_a, jnp.zeros_like(rows_a))]
    gather x0 -> x5, local copies, waits for them, and re-layouts: none -> 19.1 us  [the longest x1 5.26 us: body(): rows_b = jnp.take(rows_a, cset_jk, axis=0)]
    concatenate x2 -> x1, local copies, waits for them, and re-layouts: 17.6 us -> 0.08 us  [body(): tiles_b = tiles_a[cset_o, slot_ids]]
    dot_general x5 -> x0, matrix products: 16 us -> none  [the longest x1 4.6 us: body(): jnp.einsum('js,sbw->jbw', from_k, fc_a, preferred_element_type=F32)]
    reshape x2 -> x0, local copies, waits for them, and re-layouts: 14.3 us -> none  [the longest x1 7.43 us: body(): tiles_a = tiles_a.transpose(0, 2, 1, 3).reshape(num_sets, BLK, -1)]
    slice x4 -> x0, local copies, waits for them, and re-layouts: 13.3 us -> none  [the longest x1 4.75 us: body(): tiles_in = recv_a[:, :, row_width:].reshape(num_sets, BLK, dom_blocks, BLK)]
  transfers between devices with their start and end apart: 6 -> 8, of which waited for: 4 -> 6; matrix products, arithmetic and copies ran while one was open for 21% -> 14% of each run, Pallas kernels for 0% -> 0%
where the time goes in v4:
time: 578 us; the launch traced here: 576 us
  waiting for transfers between devices  295 us (51%)
  blocking collectives  113 us (20%)
  local copies, waits for them, and re-layouts  52 us (9%)
  matrix products  45.1 us (8%)
  starting transfers between devices  32.4 us (6%)
  other arithmetic  24.3 us (4%)
  between operations  14.3 us (2%)
    psum x1, blocking collectives, body(): occ_b = lax.psum(occ_term, ('row', 'col')).astype(BF16)  113 us
    all_to_all x1, waiting for transfers between devices, body(): lax.all_to_all(rows_a, 'col', 0, 0, tiled=True)  94.1 us
    all_to_all x1, waiting for transfers between devices, body(): lax.all_to_all(tiles_a, 'col', 0, 0, tiled=True)  61.4 us
    all_to_all x1, waiting for transfers between devices, body(): fc_a = lax.all_to_all(fc_a, 'col', 0, 0, tiled=True)  55.8 us
    all_gather x1, waiting for transfers between devices, body(): gathered = lax.all_gather(lmo_coef, 'row', axis=0, tiled=True)  37.6 us
    all_to_all x1, waiting for transfers between devices, body(): lax.all_to_all(rows_b, 'row', 0, 0, tiled=True)  29.2 us
    dot_general x1, matrix products, body(): jnp.dot(panel_fock, gathered, preferred_element_type=F32).astype(BF16)  23.4 us
    all_to_all x1, waiting for transfers between devices, body(): lax.all_to_all(tiles_b, 'row', 0, 0, tiled=True)  16.7 us
  transfers between devices with their start and end apart: 8, of which 6 were waited for; matrix products, arithmetic and copies ran while one was open for 14% of the time, Pallas kernels for 0%

profile of v4, /device:TPU:1, one launch (start us, length us, event | category | flops | bytes accessed | tf_op | source)
XLA Modules:
  0.0 576.4 jit_solution(154423634534320083)
XLA Ops:
  8.0 37.6 %all-gather.2.cloned.1.call-done = bf16[2048,1024]{1,0:T(8,128)(2,1)} async-done(((bf16[256,1024]{1,0:T(8,128)(2,1)}), bf16[2048,1024]{1,0:T(8,128)(2,1)}) %all-gather.2.cloned.1.call-update) | async-done | bytes 4194320 | tf_op jit(solution)/shard_map/all_gather | solution.py:76
  45.5 23.4 %fusion.2 = bf16[4096,1024]{1,0:T(8,128)(2,1)} fusion(bf16[2048,1024]{1,0:T(8,128)(2,1)} %all-gather.2.cloned.1.call-done, bf16[4096,1,2048]{2,0,1:T(8,128)(2,1)} %param.6), kind=kOutput, calls=%fused_computation.9 | convolution fusion | flops 17184063488 | bytes 29360128 | tf_op jit(solution)/shard_map/dot_general | solution.py:78
  69.0 9.7 %copy.112 = bf16[512,8,16,128]{3,2,1,0:T(8,128)(2,1)S(1)} copy(bf16[512,8,16,128]{3,1,2,0:T(8,128)(2,1)} %bitcast.88) | data formatting | bytes 33554432
  78.6 8.2 %copy.98 = bf16[32,128,16,128]{3,1,2,0:T(8,128)(2,1)} copy(bf16[32,128,16,128]{3,2,1,0:T(8,128)(2,1)S(1)} %bitcast.84) | data formatting | bytes 33554432 | tf_op jit(solution)/shard_map/reshape;squeeze | solution.py:50
  88.4 9.6 %gather_fusion.1 = bf16[128,128,128]{2,1,0:T(8,128)(2,1)} fusion(bf16[32,128,16,128]{3,1,2,0:T(8,128)(2,1)} %copy.98, s32[128]{0:T(128)S(1)} %reshape.158), kind=kCustom, calls=%fused_computation.1 | custom fusion | bytes 8389632 | tf_op jit(solution)/shard_map/gather | solution.py:51
  97.9 4.6 broadcast_select_fusion
  102.5 6.8 %all-to-all-start = ((bf16[16,8,128,128]{3,2,1,0:T(8,128)(2,1)}), bf16[16,8,128,128]{3,2,1,0:T(8,128)(2,1)}, u32[]{:S(2)}, u32[]{:S(2)}) async-start(bf16[16,8,128,128]{3,2,1,0:T(8,128)(2,1)} %broadcast_select_fusion), calls=%async_computation | async-start | bytes 8388608 | tf_op jit(solution)/shard_map/all_to_all | solution.py:58
  109.5 3.6 gather_fusion.3
  113.1 6.4 %select_select_fusion = bf16[16,128,1536]{2,1,0:T(8,128)(2,1)} fusion(bf16[16,128,1536]{2,1,0:T(8,128)(2,1)} %gather_fusion.3, pred[16]{0:T(512)(128)(4,1)S(1)} %compare_and_fusion.2, pred[16]{0:T(512)(128)(4,1)S(1)} %get-tuple-element.14), kind=kLoop, calls=%fused_computation.10 | loop fusion | flops 6291456 | bytes 12582944 | tf_op jit(solution)/shard_map/jit(_where)/select_n | solution.py:55
  119.5 61.4 %all-to-all-done = bf16[16,8,128,128]{3,2,1,0:T(8,128)(2,1)} async-done(((bf16[16,8,128,128]{3,2,1,0:T(8,128)(2,1)}), bf16[16,8,128,128]{3,2,1,0:T(8,128)(2,1)}, u32[]{:S(2)}, u32[]{:S(2)}) %all-to-all-start) | async-done | bytes 4194336 | tf_op jit(solution)/shard_map/all_to_all | solution.py:58
  180.8 4.6 all-to-all-start.2
  186.0 3.5 gather_fusion.2
  189.6 2.7 copy_select_fusion
  192.2 94.1 %all-to-all-done.2 = bf16[16,128,1536]{2,1,0:T(8,128)(2,1)} async-done(((bf16[16,128,1536]{2,1,0:T(8,128)(2,1)}), bf16[16,128,1536]{2,1,0:T(8,128)(2,1)}, u32[]{:S(2)}, u32[]{:S(2)}) %all-to-all-start.2) | async-done | bytes 6291488 | tf_op jit(solution)/shard_map/all_to_all | solution.py:57
  286.3 5.1 all-to-all-start.1
  291.8 5.3 gather_fusion.4
  297.1 4.0 select_select_fusion.2
  301.1 16.7 %all-to-all-done.1 = bf16[8,8,128,128]{3,1,2,0:T(8,128)(2,1)S(1)} async-done(((bf16[8,8,128,128]{3,1,2,0:T(8,128)(2,1)}), bf16[8,8,128,128]{3,1,2,0:T(8,128)(2,1)S(1)}, u32[]{:S(2)}, u32[]{:S(2)}) %all-to-all-start.1) | async-done | bytes 2097184 | tf_op jit(solution)/shard_map/all_to_all | solution.py:72
  317.8 5.2 all-to-all-start.3
  323.0 3.8 gather_fusion.5
  326.8 4.7 select_select_fusion.1
  331.5 29.2 %all-to-all-done.3 = bf16[8,128,1536]{2,1,0:T(8,128)(2,1)} async-done(((bf16[8,128,1536]{2,1,0:T(8,128)(2,1)}), bf16[8,128,1536]{2,1,0:T(8,128)(2,1)}, u32[]{:S(2)}, u32[]{:S(2)}) %all-to-all-start.3) | async-done | bytes 3145760 | tf_op jit(solution)/shard_map/all_to_all | solution.py:71
  360.7 4.5 all-to-all-start.4
  365.3 2.8 convolution_bitcast_fusion.1
  368.0 3.9 fusion.12
  371.9 55.8 %all-to-all-done.4 = bf16[16,128,1024]{2,1,0:T(8,128)(2,1)} async-done(((bf16[16,128,1024]{2,1,0:T(8,128)(2,1)}), bf16[16,128,1024]{2,1,0:T(8,128)(2,1)}, u32[]{:S(2)}, u32[]{:S(2)}) %all-to-all-start.4) | async-done | bytes 4194336 | tf_op jit(solution)/shard_map/all_to_all | solution.py:88
  427.6 2.9 gather_fusion.6
  432.2 6.0 %all-to-all-start.5 = ((bf16[8,128,1024]{2,1,0:T(8,128)(2,1)}), bf16[8,128,1024]{2,1,0:T(8,128)(2,1)}, u32[]{:S(2)}, u32[]{:S(2)}) async-start(bf16[8,128,1024]{2,1,0:T(8,128)(2,1)} %select_select_fusion.3), calls=%async_computation.6 | async-start | bytes 4194304 | tf_op jit(solution)/shard_map/all_to_all | solution.py:91
  438.1 2.0 fusion.18
  441.2 2.7 convolution_bitcast_fusion
  443.9 113.0 %all-reduce.1 = bf16[1024,1024]{0,1:T(8,128)(2,1)} all-reduce(f32[1024,1024]{0,1:T(8,128)} %convolution_bitcast_fusion), channel_id=1, replica_groups=mesh['row'=8,'col'=16] {'row','col'}, use_global_device_ids=true, to_apply=%region_5.6 | all-reduce | flops 1048576 | bytes 6291456 | tf_op jit(solution)/shard_map/psum | solution.py:84
  556.9 6.4 %convolution_convert_fusion = bf16[1024,512]{1,0:T(8,128)(2,1)S(1)} fusion(bf16[1,1,1024,512]{3,2,1,0:T(8,128)(2,1)S(1)} %copy-done, bf16[1024,1024]{1,0:T(8,128)(2,1)} %bitcast.28, bf16[1024,1024]{0,1:T(8,128)(2,1)} %all-reduce.1, bf16[1024,1536]{1,0:T(8,128)(2,1)} %bitcast.19), kind=kOutput, calls=%fused_computation.27 | convolution fusion | flops 3225944064 | bytes 8388608 | tf_op jit(solution)/shard_map/xm,xi->mi/dot_general | solution.py:104
  (63 shorter events, 12.2 us)
Async XLA Ops:
  7.2 358.1 %copy-start = (bf16[1,1,1024,512]{3,2,1,0:T(8,128)(2,1)S(1)}, bf16[1,1,1024,512]{3,2,1,0:T(8,128)(2,1)}, u32[]{:S(2)}) copy-start(bf16[1,1,1024,512]{3,2,1,0:T(8,128)(2,1)} %param.9) | copy-start | bytes 3145732
  7.2 38.3 %all-gather.2.cloned.1.call-start = ((), (), s32[]{:S(2)}) async-start(), calls=%async_computation.7 | async-start | bytes 4718592 | tf_op jit(solution)/shard_map/all_gather | solution.py:76
  7.9 315.1 %reduce-scatter.2.cloned.1.call-start = ((), (), s32[]{:S(2)}) async-start(), calls=%async_computation.8 | async-start | bytes 8912896 | tf_op jit(solution)/shard_map/reduce_scatter | solution.py:77
  78.6 8.2 %copy-start.8 = (s32[128,8]{0,1:T(8,128)S(1)}, s32[128,8]{0,1:T(8,128)}, u32[]{:S(2)}) copy-start(s32[128,8]{0,1:T(8,128)} %param.11) | copy-start | bytes 12292
  78.6 8.3 %copy-start.7 = (s32[16,8]{0,1:T(8,128)S(1)}, s32[16,8]{0,1:T(8,128)}, u32[]{:S(2)}) copy-start(s32[16,8]{0,1:T(8,128)} %param.10) | copy-start | bytes 1540
  102.5 6.9 %copy-start.2 = (bf16[256,1024]{1,0:T(8,128)(2,1)S(1)}, bf16[256,1024]{1,0:T(8,128)(2,1)}, u32[]{:S(2)}) copy-start(bf16[256,1024]{1,0:T(8,128)(2,1)} %param.7) | copy-start | bytes 1572868
  102.5 6.9 %copy-start.6 = (bf16[256,512]{1,0:T(8,128)(2,1)S(1)}, bf16[256,512]{1,0:T(8,128)(2,1)}, u32[]{:S(2)}) copy-start(bf16[256,512]{1,0:T(8,128)(2,1)} %param.8) | copy-start | bytes 786436
  102.5 78.3 %all-to-all-start = ((bf16[16,8,128,128]{3,2,1,0:T(8,128)(2,1)}), bf16[16,8,128,128]{3,2,1,0:T(8,128)(2,1)}, u32[]{:S(2)}, u32[]{:S(2)}) async-start(bf16[16,8,128,128]{3,2,1,0:T(8,128)(2,1)} %broadcast_select_fusion), calls=%async_computation | async-start | bytes 8388608 | tf_op jit(solution)/shard_map/all_to_all | solution.py:58
  180.8 105.5 %all-to-all-start.2 = ((bf16[16,128,1536]{2,1,0:T(8,128)(2,1)}), bf16[16,128,1536]{2,1,0:T(8,128)(2,1)}, u32[]{:S(2)}, u32[]{:S(2)}) async-start(bf16[16,128,1536]{2,1,0:T(8,128)(2,1)} %select_select_fusion), calls=%async_computation.2 | async-start | bytes 12582912 | tf_op jit(solution)/shard_map/all_to_all | solution.py:57
  286.3 31.5 %all-to-all-start.1 = ((bf16[8,8,128,128]{3,1,2,0:T(8,128)(2,1)}), bf16[8,8,128,128]{3,1,2,0:T(8,128)(2,1)S(1)}, u32[]{:S(2)}, u32[]{:S(2)}) async-start(bf16[8,8,128,128]{3,1,2,0:T(8,128)(2,1)} %copy_select_fusion), calls=%async_computation.1 | async-start | bytes 4194304 | tf_op jit(solution)/shard_map/all_to_all | solution.py:72
  317.8 42.9 %all-to-all-start.3 = ((bf16[8,128,1536]{2,1,0:T(8,128)(2,1)}), bf16[8,128,1536]{2,1,0:T(8,128)(2,1)}, u32[]{:S(2)}, u32[]{:S(2)}) async-start(bf16[8,128,1536]{2,1,0:T(8,128)(2,1)} %select_select_fusion.2), calls=%async_computation.3 | async-start | bytes 6291456 | tf_op jit(solution)/shard_map/all_to_all | solution.py:71
  360.7 66.9 %all-to-all-start.4 = ((bf16[16,128,1024]{2,1,0:T(8,128)(2,1)}), bf16[16,128,1024]{2,1,0:T(8,128)(2,1)}, u32[]{:S(2)}, u32[]{:S(2)}) async-start(bf16[16,128,1024]{2,1,0:T(8,128)(2,1)} %select_select_fusion.1), calls=%async_computation.5 | async-start | bytes 8388608 | tf_op jit(solution)/shard_map/all_to_all | solution.py:88
  432.2 124.7 %all-to-all-start.5 = ((bf16[8,128,1024]{2,1,0:T(8,128)(2,1)}), bf16[8,128,1024]{2,1,0:T(8,128)(2,1)}, u32[]{:S(2)}, u32[]{:S(2)}) async-start(bf16[8,128,1024]{2,1,0:T(8,128)(2,1)} %select_select_fusion.3), calls=%async_computation.6 | async-start | bytes 4194304 | tf_op jit(solution)/shard_map/all_to_all | solution.py:91
  438.1 3.1 copy-start.1
  438.1 3.1 copy-start.3
  556.9 7.4 %copy-start.4 = (bf16[1024,512]{1,0:T(8,128)(2,1)S(1)}, bf16[1024,512]{1,0:T(8,128)(2,1)}, u32[]{:S(2)}) copy-start(bf16[1024,512]{1,0:T(8,128)(2,1)} %fusion.12) | copy-start | bytes 3145732
  563.3 1.0 copy-start.5
Sparse Core Ops, SparseCore 0:
  9.7 35.7 all-gather.1
  69.1 199.0 reduce-scatter.1

commit v5 on v4

--- a/solution.py
+++ b/solution.py
@@ -34,8 +34,6 @@
     panel = flat // num_sets
     row_tile = cset * dev_blocks + sub
     col_tile = panel * dev_blocks + sub
-    set_range = jnp.arange(num_sets, dtype=jnp.int32)
-    sub_range = jnp.arange(dev_blocks, dtype=jnp.int32)
 
     pres_k = lax.dynamic_index_in_dim(present, my_row, 2, keepdims=False)
     cset_k = lax.dynamic_index_in_dim(cset, my_row, 2, keepdims=False)
@@ -58,21 +56,6 @@
         lax.all_to_all(tiles_a, "col", 0, 0, tiled=True),
     )
 
-    pres_o = lax.dynamic_index_in_dim(present, my_col, 0, keepdims=False)
-    cset_o = lax.dynamic_index_in_dim(cset, my_col, 0, keepdims=False)
-    pres_jk = lax.dynamic_index_in_dim(pres_o, my_row, 1, keepdims=False)
-    cset_jk = lax.dynamic_index_in_dim(cset_o, my_row, 1, keepdims=False)
-    rows_b = jnp.take(rows_a, cset_jk, axis=0)
-    rows_b = jnp.where(pres_jk[:, None, None], rows_b, jnp.zeros_like(rows_b))
-    slot_ids = jnp.broadcast_to(jnp.arange(dom_blocks, dtype=jnp.int32)[:, None], cset_o.shape)
-    tiles_b = tiles_a[cset_o, slot_ids]
-    tiles_b = jnp.where(pres_o[:, :, None, None], tiles_b, jnp.zeros_like(tiles_b))
-    rows_dom, tiles_dom = (
-        lax.all_to_all(rows_b, "row", 0, 0, tiled=True),
-        lax.all_to_all(tiles_b, "row", 0, 0, tiled=True),
-    )
-    rows_dom = rows_dom.reshape(dom_width, -1)
-
     gathered = lax.all_gather(lmo_coef, "row", axis=0, tiled=True)
     coef_b = lax.psum_scatter(
         jnp.dot(panel_fock, gathered, preferred_element_type=F32).astype(BF16),
@@ -86,6 +69,23 @@
     fc_a = jnp.take(coef_b.reshape(dev_blocks, BLK, occ_width), sub_o, axis=0)
     fc_a = jnp.where(has_o[:, None, None], fc_a, jnp.zeros_like(fc_a))
     fc_a = lax.all_to_all(fc_a, "col", 0, 0, tiled=True)
+
+    pres_o = lax.dynamic_index_in_dim(present, my_col, 0, keepdims=False)
+    cset_o = lax.dynamic_index_in_dim(cset, my_col, 0, keepdims=False)
+    pres_jk = lax.dynamic_index_in_dim(pres_o, my_row, 1, keepdims=False)
+    cset_jk = lax.dynamic_index_in_dim(cset_o, my_row, 1, keepdims=False)
+    rows_a, tiles_a, fc_a, occ_b = lax.optimization_barrier((rows_a, tiles_a, fc_a, occ_b))
+    rows_b = jnp.take(rows_a, cset_jk, axis=0)
+    rows_b = jnp.where(pres_jk[:, None, None], rows_b, jnp.zeros_like(rows_b))
+    slot_ids = jnp.broadcast_to(jnp.arange(dom_blocks, dtype=jnp.int32)[:, None], cset_o.shape)
+    tiles_b = tiles_a[cset_o, slot_ids]
+    tiles_b = jnp.where(pres_o[:, :, None, None], tiles_b, jnp.zeros_like(tiles_b))
+    rows_dom, tiles_dom = (
+        lax.all_to_all(rows_b, "row", 0, 0, tiled=True),
+        lax.all_to_all(tiles_b, "row", 0, 0, tiled=True),
+    )
+    rows_dom = rows_dom.reshape(dom_width, -1)
+
     fc_b = jnp.take(fc_a, cset_jk, axis=0)
     fc_b = jnp.where(pres_jk[:, None, None], fc_b, jnp.zeros_like(fc_b))
     fc_dom = lax.all_to_all(fc_b, "row", 0, 0, tiled=True).reshape(dom_width, occ_width)

time: 578 us -> 582 us (level)
  blocking collectives: 113 us -> 150 us
  waiting for transfers between devices: 295 us -> 261 us
    all_to_all x1, waiting for transfers between devices: 94.1 us -> 9.85 us  [body(): lax.all_to_all(rows_a, 'col', 0, 0, tiled=True)]
    reduce_scatter x1, waiting for transfers between devices: 0.01 us -> 83.8 us  [body(): lax.psum_scatter(jnp.dot(panel_fock, gathered, preferred_element_type=F32...]
    all_to_all x1, waiting for transfers between devices: 55.8 us -> 0.01 us  [body(): fc_a = lax.all_to_all(fc_a, 'col', 0, 0, tiled=True)]
    psum x1, blocking collectives: 113 us -> 150 us  [body(): occ_b = lax.psum(occ_term, ('row', 'col')).astype(BF16)]
    all_to_all x1, waiting for transfers between devices: 0.01 us -> 18.1 us  [body(): lax.all_to_all(fc_b, 'row', 0, 0, tiled=True).reshape(dom_width, occ_width)]
  transfers between devices with their start and end apart: 8 -> 8, of which waited for: 6 -> 7; matrix products, arithmetic and copies ran while one was open for 14% -> 13% of each run, Pallas kernels for 0% -> 0%
where the time goes in v5:
time: 582 us; the launch traced here: 580 us
  waiting for transfers between devices  261 us (45%)
  blocking collectives  150 us (26%)
  local copies, waits for them, and re-layouts  54.8 us (9%)
  matrix products  44.7 us (8%)
  starting transfers between devices  31 us (5%)
  other arithmetic  24.4 us (4%)
  between operations  14.3 us (2%)
    psum x1, blocking collectives, body(): occ_b = lax.psum(occ_term, ('row', 'col')).astype(BF16)  150 us
    reduce_scatter x1, waiting for transfers between devices, body(): lax.psum_scatter(jnp.dot(panel_fock, gathered, preferred_element_type=F32...  83.8 us
    all_to_all x1, waiting for transfers between devices, body(): lax.all_to_all(tiles_a, 'col', 0, 0, tiled=True)  61.2 us
    all_gather x1, waiting for transfers between devices, body(): gathered = lax.all_gather(lmo_coef, 'row', axis=0, tiled=True)  37.6 us
    all_to_all x1, waiting for transfers between devices, body(): lax.all_to_all(rows_b, 'row', 0, 0, tiled=True)  33.2 us
    dot_general x1, matrix products, body(): jnp.dot(panel_fock, gathered, preferred_element_type=F32).astype(BF16)  23.4 us
    all_to_all x1, waiting for transfers between devices, body(): lax.all_to_all(fc_b, 'row', 0, 0, tiled=True).reshape(dom_width, occ_width)  18.1 us
    all_to_all x1, waiting for transfers between devices, body(): lax.all_to_all(tiles_b, 'row', 0, 0, tiled=True)  16.6 us
  transfers between devices with their start and end apart: 8, of which 7 were waited for; matrix products, arithmetic and copies ran while one was open for 13% of the time, Pallas kernels for 0%

profile of v5, /device:TPU:1, one launch (start us, length us, event | category | flops | bytes accessed | tf_op | source)
XLA Modules:
  0.0 580.4 jit_solution(3458699840535303516)
XLA Ops:
  8.0 37.6 %all-gather.2.cloned.1.call-done = bf16[2048,1024]{1,0:T(8,128)(2,1)} async-done(((bf16[256,1024]{1,0:T(8,128)(2,1)}), bf16[2048,1024]{1,0:T(8,128)(2,1)}) %all-gather.2.cloned.1.call-update) | async-done | bytes 4194320 | tf_op jit(solution)/shard_map/all_gather | solution.py:59
  45.5 23.4 %fusion.2 = bf16[4096,1024]{1,0:T(8,128)(2,1)} fusion(bf16[2048,1024]{1,0:T(8,128)(2,1)} %all-gather.2.cloned.1.call-done, bf16[4096,1,2048]{2,0,1:T(8,128)(2,1)} %param.6), kind=kOutput, calls=%fused_computation.9 | convolution fusion | flops 17184063488 | bytes 29360128 | tf_op jit(solution)/shard_map/dot_general | solution.py:61
  70.6 9.8 %copy.112 = bf16[512,8,16,128]{3,2,1,0:T(8,128)(2,1)S(1)} copy(bf16[512,8,16,128]{3,1,2,0:T(8,128)(2,1)} %bitcast.88) | data formatting | bytes 33554432
  80.4 8.2 %copy.98 = bf16[32,128,16,128]{3,1,2,0:T(8,128)(2,1)} copy(bf16[32,128,16,128]{3,2,1,0:T(8,128)(2,1)S(1)} %bitcast.84) | data formatting | bytes 33554432 | tf_op jit(solution)/shard_map/reshape;squeeze | solution.py:48
  89.1 9.6 %gather_fusion.2 = bf16[128,128,128]{2,1,0:T(8,128)(2,1)} fusion(bf16[32,128,16,128]{3,1,2,0:T(8,128)(2,1)} %copy.98, s32[128]{0:T(128)S(1)} %reshape.166), kind=kCustom, calls=%fused_computation.2 | custom fusion | bytes 8389632 | tf_op jit(solution)/shard_map/gather | solution.py:49
  98.7 4.7 broadcast_select_fusion
  103.3 6.7 %all-to-all-start.1 = ((bf16[16,8,128,128]{3,2,1,0:T(8,128)(2,1)}), bf16[16,8,128,128]{3,2,1,0:T(8,128)(2,1)}, u32[]{:S(2)}, u32[]{:S(2)}) async-start(bf16[16,8,128,128]{3,2,1,0:T(8,128)(2,1)} %broadcast_select_fusion), calls=%async_computation.1 | async-start | bytes 8388608 | tf_op jit(solution)/shard_map/all_to_all | solution.py:56
  110.2 3.6 gather_fusion.1
  113.8 6.4 %select_select_fusion = bf16[16,128,1536]{2,1,0:T(8,128)(2,1)} fusion(bf16[16,128,1536]{2,1,0:T(8,128)(2,1)} %gather_fusion.1, pred[16]{0:T(512)(128)(4,1)S(1)} %compare_and_fusion.3, pred[16]{0:T(512)(128)(4,1)S(1)} %get-tuple-element.26), kind=kLoop, calls=%fused_computation.10 | loop fusion | flops 6291456 | bytes 12582944 | tf_op jit(solution)/shard_map/jit(_where)/select_n | solution.py:53
  120.1 61.2 %all-to-all-done.1 = bf16[16,8,128,128]{3,2,1,0:T(8,128)(2,1)} async-done(((bf16[16,8,128,128]{3,2,1,0:T(8,128)(2,1)}), bf16[16,8,128,128]{3,2,1,0:T(8,128)(2,1)}, u32[]{:S(2)}, u32[]{:S(2)}) %all-to-all-start.1) | async-done | bytes 4194336 | tf_op jit(solution)/shard_map/all_to_all | solution.py:56
  181.3 4.6 all-to-all-start
  186.0 83.8 %reduce-scatter.2.cloned.1.call-done = bf16[256,1024]{1,0:T(8,128)(2,1)} async-done(((bf16[4096,1024]{1,0:T(8,128)(2,1)}), bf16[256,1024]{1,0:T(8,128)(2,1)}) %reduce-scatter.2.cloned.1.call-update) | async-done | bytes 524304 | tf_op jit(solution)/shard_map/reduce_scatter | solution.py:60
  269.7 3.8 gather_fusion.3
  273.6 4.7 select_select_fusion.1
  278.3 9.8 %all-to-all-done = bf16[16,128,1536]{2,1,0:T(8,128)(2,1)} async-done(((bf16[16,128,1536]{2,1,0:T(8,128)(2,1)}), bf16[16,128,1536]{2,1,0:T(8,128)(2,1)}, u32[]{:S(2)}, u32[]{:S(2)}) %all-to-all-start) | async-done | bytes 6291488 | tf_op jit(solution)/shard_map/all_to_all | solution.py:55
  288.1 4.5 all-to-all-start.2
  293.2 2.7 convolution_bitcast_fusion
  295.9 150.4 %all-reduce.1 = bf16[1024,1024]{0,1:T(8,128)(2,1)} all-reduce(f32[1024,1024]{0,1:T(8,128)} %convolution_bitcast_fusion), channel_id=1, replica_groups=mesh['row'=8,'col'=16] {'row','col'}, use_global_device_ids=true, to_apply=%region_5.6 | all-reduce | flops 1048576 | bytes 6291456 | tf_op jit(solution)/shard_map/psum | solution.py:67
  446.3 3.1 gather_fusion.4
  452.1 4.7 all-to-all-start.3
  457.2 5.3 gather_fusion.5
  462.5 4.0 select_select_fusion.2
  466.5 16.6 %all-to-all-done.3 = bf16[8,8,128,128]{3,1,2,0:T(8,128)(2,1)S(1)} async-done(((bf16[8,8,128,128]{3,1,2,0:T(8,128)(2,1)}), bf16[8,8,128,128]{3,1,2,0:T(8,128)(2,1)S(1)}, u32[]{:S(2)}, u32[]{:S(2)}) %all-to-all-start.3) | async-done | bytes 2097184 | tf_op jit(solution)/shard_map/all_to_all | solution.py:85
  484.5 5.2 all-to-all-start.4
  489.7 2.9 gather_fusion.6
  494.2 33.2 %all-to-all-done.4 = bf16[8,128,1536]{2,1,0:T(8,128)(2,1)} async-done(((bf16[8,128,1536]{2,1,0:T(8,128)(2,1)}), bf16[8,128,1536]{2,1,0:T(8,128)(2,1)}, u32[]{:S(2)}, u32[]{:S(2)}) %all-to-all-start.4) | async-done | bytes 3145760 | tf_op jit(solution)/shard_map/all_to_all | solution.py:84
  527.4 5.1 all-to-all-start.5
  532.5 2.8 convolution_bitcast_fusion.1
  535.3 2.7 fusion.17
  538.0 2.9 fusion.11
  540.9 18.1 %all-to-all-done.5 = bf16[8,128,1024]{2,1,0:T(8,128)(2,1)} async-done(((bf16[8,128,1024]{2,1,0:T(8,128)(2,1)}), bf16[8,128,1024]{2,1,0:T(8,128)(2,1)}, u32[]{:S(2)}, u32[]{:S(2)}) %all-to-all-start.5) | async-done | bytes 2097184 | tf_op jit(solution)/shard_map/all_to_all | solution.py:91
  558.9 6.3 %convolution_convert_fusion = bf16[1024,512]{1,0:T(8,128)(2,1)S(1)} fusion(bf16[1,1,1024,512]{3,2,1,0:T(8,128)(2,1)S(1)} %copy-done, bf16[1024,1024]{1,0:T(8,128)(2,1)} %bitcast.28, bf16[1024,1024]{0,1:T(8,128)(2,1)} %all-reduce.1, bf16[1024,1536]{1,0:T(8,128)(2,1)} %bitcast.22), kind=kOutput, calls=%fused_computation.26 | convolution fusion | flops 3225944064 | bytes 8388608 | tf_op jit(solution)/shard_map/xm,xi->mi/dot_general | solution.py:104
  (63 shorter events, 17.9 us)
Async XLA Ops:
  7.2 525.3 %copy-start = (bf16[1,1,1024,512]{3,2,1,0:T(8,128)(2,1)S(1)}, bf16[1,1,1024,512]{3,2,1,0:T(8,128)(2,1)}, u32[]{:S(2)}) copy-start(bf16[1,1,1024,512]{3,2,1,0:T(8,128)(2,1)} %param.9) | copy-start | bytes 3145732
  7.2 38.3 %all-gather.2.cloned.1.call-start = ((), (), s32[]{:S(2)}) async-start(), calls=%async_computation.7 | async-start | bytes 4718592 | tf_op jit(solution)/shard_map/all_gather | solution.py:59
  7.9 261.8 %reduce-scatter.2.cloned.1.call-start = ((), (), s32[]{:S(2)}) async-start(), calls=%async_computation.8 | async-start | bytes 8912896 | tf_op jit(solution)/shard_map/reduce_scatter | solution.py:60
  68.9 0.7 copy-start.8
  68.9 0.8 copy-start.7
  103.3 6.8 %copy-start.2 = (bf16[256,1024]{1,0:T(8,128)(2,1)S(1)}, bf16[256,1024]{1,0:T(8,128)(2,1)}, u32[]{:S(2)}) copy-start(bf16[256,1024]{1,0:T(8,128)(2,1)} %param.7) | copy-start | bytes 1572868
  103.3 6.8 %copy-start.6 = (bf16[256,512]{1,0:T(8,128)(2,1)S(1)}, bf16[256,512]{1,0:T(8,128)(2,1)}, u32[]{:S(2)}) copy-start(bf16[256,512]{1,0:T(8,128)(2,1)} %param.8) | copy-start | bytes 786436
  103.3 78.0 %all-to-all-start.1 = ((bf16[16,8,128,128]{3,2,1,0:T(8,128)(2,1)}), bf16[16,8,128,128]{3,2,1,0:T(8,128)(2,1)}, u32[]{:S(2)}, u32[]{:S(2)}) async-start(bf16[16,8,128,128]{3,2,1,0:T(8,128)(2,1)} %broadcast_select_fusion), calls=%async_computation.1 | async-start | bytes 8388608 | tf_op jit(solution)/shard_map/all_to_all | solution.py:56
  181.3 106.8 %all-to-all-start = ((bf16[16,128,1536]{2,1,0:T(8,128)(2,1)}), bf16[16,128,1536]{2,1,0:T(8,128)(2,1)}, u32[]{:S(2)}, u32[]{:S(2)}) async-start(bf16[16,128,1536]{2,1,0:T(8,128)(2,1)} %select_select_fusion), calls=%async_computation | async-start | bytes 12582912 | tf_op jit(solution)/shard_map/all_to_all | solution.py:55
  278.3 14.9 %copy-start.1 = (bf16[256,1024]{1,0:T(8,128)(2,1)S(1)}, bf16[256,1024]{1,0:T(8,128)(2,1)}, u32[]{:S(2)}) copy-start(bf16[256,1024]{1,0:T(8,128)(2,1)} %reduce-scatter.2.cloned.1.call-done) | copy-start | bytes 1572868
  288.1 158.2 %all-to-all-start.2 = ((bf16[16,128,1024]{2,1,0:T(8,128)(2,1)}), bf16[16,128,1024]{2,1,0:T(8,128)(2,1)}, u32[]{:S(2)}, u32[]{:S(2)}) async-start(bf16[16,128,1024]{2,1,0:T(8,128)(2,1)} %select_select_fusion.1), calls=%async_computation.3 | async-start | bytes 8388608 | tf_op jit(solution)/shard_map/all_to_all | solution.py:71
  452.1 31.1 %all-to-all-start.3 = ((bf16[8,8,128,128]{3,1,2,0:T(8,128)(2,1)}), bf16[8,8,128,128]{3,1,2,0:T(8,128)(2,1)S(1)}, u32[]{:S(2)}, u32[]{:S(2)}) async-start(bf16[8,8,128,128]{3,1,2,0:T(8,128)(2,1)} %copy_select_fusion), calls=%async_computation.4 | async-start | bytes 4194304 | tf_op jit(solution)/shard_map/all_to_all | solution.py:85
  483.2 1.3 copy-start.4
  484.5 42.9 %all-to-all-start.4 = ((bf16[8,128,1536]{2,1,0:T(8,128)(2,1)}), bf16[8,128,1536]{2,1,0:T(8,128)(2,1)}, u32[]{:S(2)}, u32[]{:S(2)}) async-start(bf16[8,128,1536]{2,1,0:T(8,128)(2,1)} %select_select_fusion.2), calls=%async_computation.5 | async-start | bytes 6291456 | tf_op jit(solution)/shard_map/all_to_all | solution.py:84
  494.2 38.3 %copy-start.5 = (bf16[8,8,128,128]{3,1,2,0:T(8,128)(2,1)S(1)}, bf16[8,8,128,128]{3,1,2,0:T(8,128)(2,1)}, u32[]{:S(2)}) copy-start(bf16[8,8,128,128]{3,1,2,0:T(8,128)(2,1)} %copy-done.4) | copy-start | bytes 6291460
  527.4 31.6 %all-to-all-start.5 = ((bf16[8,128,1024]{2,1,0:T(8,128)(2,1)}), bf16[8,128,1024]{2,1,0:T(8,128)(2,1)}, u32[]{:S(2)}, u32[]{:S(2)}) async-start(bf16[8,128,1024]{2,1,0:T(8,128)(2,1)} %select_select_fusion.3), calls=%async_computation.6 | async-start | bytes 4194304 | tf_op jit(solution)/shard_map/all_to_all | solution.py:91
  565.3 1.0 copy-start.3
Sparse Core Ops, SparseCore 0:
  9.7 35.7 all-gather.1
  69.1 200.6 reduce-scatter.1

commit v6 on v5

--- a/solution.py
+++ b/solution.py
@@ -51,14 +51,14 @@
     in_rows = jnp.concatenate([lmo_coef, three_index], axis=1).reshape(dev_blocks, BLK, -1)
     rows_a = jnp.take(in_rows, sub_o, axis=0)
     rows_a = jnp.where(has_o[:, None, None], rows_a, jnp.zeros_like(rows_a))
-    rows_a, tiles_a = (
-        lax.all_to_all(rows_a, "col", 0, 0, tiled=True),
-        lax.all_to_all(tiles_a, "col", 0, 0, tiled=True),
-    )
+    rows_a = lax.all_to_all(rows_a, "col", 0, 0, tiled=True)
+    tiles_a = lax.all_to_all(tiles_a, "col", 0, 0, tiled=True)
 
     gathered = lax.all_gather(lmo_coef, "row", axis=0, tiled=True)
+    fock_lmo = jnp.dot(panel_fock, gathered, preferred_element_type=F32).astype(BF16)
+    rows_a, fock_lmo = lax.optimization_barrier((rows_a, fock_lmo))
     coef_b = lax.psum_scatter(
-        jnp.dot(panel_fock, gathered, preferred_element_type=F32).astype(BF16),
+        fock_lmo,
         "col",
         scatter_dimension=0,
         tiled=True,
@@ -66,15 +66,10 @@
     occ_term = jnp.einsum("ri,rj->ij", lmo_coef, coef_b, preferred_element_type=F32)
     occ_b = lax.psum(occ_term, ("row", "col")).astype(BF16)
 
-    fc_a = jnp.take(coef_b.reshape(dev_blocks, BLK, occ_width), sub_o, axis=0)
-    fc_a = jnp.where(has_o[:, None, None], fc_a, jnp.zeros_like(fc_a))
-    fc_a = lax.all_to_all(fc_a, "col", 0, 0, tiled=True)
-
     pres_o = lax.dynamic_index_in_dim(present, my_col, 0, keepdims=False)
     cset_o = lax.dynamic_index_in_dim(cset, my_col, 0, keepdims=False)
     pres_jk = lax.dynamic_index_in_dim(pres_o, my_row, 1, keepdims=False)
     cset_jk = lax.dynamic_index_in_dim(cset_o, my_row, 1, keepdims=False)
-    rows_a, tiles_a, fc_a, occ_b = lax.optimization_barrier((rows_a, tiles_a, fc_a, occ_b))
     rows_b = jnp.take(rows_a, cset_jk, axis=0)
     rows_b = jnp.where(pres_jk[:, None, None], rows_b, jnp.zeros_like(rows_b))
     slot_ids = jnp.broadcast_to(jnp.arange(dom_blocks, dtype=jnp.int32)[:, None], cset_o.shape)
@@ -86,6 +81,9 @@
     )
     rows_dom = rows_dom.reshape(dom_width, -1)
 
+    fc_a = jnp.take(coef_b.reshape(dev_blocks, BLK, occ_width), sub_o, axis=0)
+    fc_a = jnp.where(has_o[:, None, None], fc_a, jnp.zeros_like(fc_a))
+    fc_a = lax.all_to_all(fc_a, "col", 0, 0, tiled=True)
     fc_b = jnp.take(fc_a, cset_jk, axis=0)
     fc_b = jnp.where(pres_jk[:, None, None], fc_b, jnp.zeros_like(fc_b))
     fc_dom = lax.all_to_all(fc_b, "row", 0, 0, tiled=True).reshape(dom_width, occ_width)

time: 582 us -> 530 us (0.911)
  blocking collectives: 150 us -> 113 us
  waiting for transfers between devices: 261 us -> 242 us
    reduce_scatter x1, waiting for transfers between devices: 83.8 us -> 0.01 us  [body(): coef_b = lax.psum_scatter(fock_lmo, 'col', scatter_dimension=0, tiled=True)]
    all_to_all x1, waiting for transfers between devices: 0.01 us -> 55.6 us  [body(): fc_a = lax.all_to_all(fc_a, 'col', 0, 0, tiled=True)]
    all_to_all x2, waiting for transfers between devices: 71 us -> 125 us  [the longest x1 70.9 us: body(): tiles_a = lax.all_to_all(tiles_a, 'col', 0, 0, tiled=True)]
    psum x1, blocking collectives: 150 us -> 113 us  [body(): occ_b = lax.psum(occ_term, ('row', 'col')).astype(BF16)]
    all_gather x1, waiting for transfers between devices: 37.6 us -> 14.7 us  [body(): gathered = lax.all_gather(lmo_coef, 'row', axis=0, tiled=True)]
    all_to_all x1, waiting for transfers between devices: 18.1 us -> 0.01 us  [body(): lax.all_to_all(fc_b, 'row', 0, 0, tiled=True).reshape(dom_width, occ_width)]
    unnamed x23 -> x15, local copies, waits for them, and re-layouts: 16.3 us -> 13.8 us
  transfers between devices with their start and end apart: 8 -> 8, of which waited for: 7 -> 6; matrix products, arithmetic and copies ran while one was open for 13% -> 20% of each run, Pallas kernels for 0% -> 0%
where the time goes in v6:
time: 530 us; the launch traced here: 528 us
  waiting for transfers between devices  242 us (46%)
  blocking collectives  113 us (21%)
  local copies, waits for them, and re-layouts  51.9 us (10%)
  matrix products  45.1 us (9%)
  starting transfers between devices  35.7 us (7%)
  other arithmetic  26.5 us (5%)
  between operations  14.2 us (3%)
    psum x1, blocking collectives, body(): occ_b = lax.psum(occ_term, ('row', 'col')).astype(BF16)  113 us
    all_to_all x1, waiting for transfers between devices, body(): tiles_a = lax.all_to_all(tiles_a, 'col', 0, 0, tiled=True)  70.9 us
    all_to_all x1, waiting for transfers between devices, body(): fc_a = lax.all_to_all(fc_a, 'col', 0, 0, tiled=True)  55.6 us
    all_to_all x1, waiting for transfers between devices, body(): rows_a = lax.all_to_all(rows_a, 'col', 0, 0, tiled=True)  54.3 us
    all_to_all x1, waiting for transfers between devices, body(): lax.all_to_all(rows_b, 'row', 0, 0, tiled=True)  29.2 us
    dot_general x1, matrix products, body(): jnp.dot(panel_fock, gathered, preferred_element_type=F32).astype(BF16)  23.4 us
    all_to_all x1, waiting for transfers between devices, body(): lax.all_to_all(tiles_b, 'row', 0, 0, tiled=True)  16.8 us
    all_gather x1, waiting for transfers between devices, body(): gathered = lax.all_gather(lmo_coef, 'row', axis=0, tiled=True)  14.7 us
  transfers between devices with their start and end apart: 8, of which 6 were waited for; matrix products, arithmetic and copies ran while one was open for 20% of the time, Pallas kernels for 0%

profile of v6, /device:TPU:1, one launch (start us, length us, event | category | flops | bytes accessed | tf_op | source)
XLA Modules:
  0.0 528.2 jit_solution(3955710803716426408)
XLA Ops:
  12.4 3.6 gather_fusion.3
  16.0 6.2 %select_select_fusion = bf16[16,128,1536]{2,1,0:T(8,128)(2,1)} fusion(bf16[16,128,1536]{2,1,0:T(8,128)(2,1)} %gather_fusion.3, pred[16]{0:T(512)(128)(4,1)S(1)} %compare_and_fusion.2, pred[16]{0:T(512)(128)(4,1)S(1)} %get-tuple-element.18), kind=kLoop, calls=%fused_computation.10 | loop fusion | flops 6291456 | bytes 12582944 | tf_op jit(solution)/shard_map/jit(_where)/select_n | solution.py:53
  22.2 8.5 %all-to-all-start.2 = ((bf16[16,128,1536]{2,1,0:T(8,128)(2,1)}), bf16[16,128,1536]{2,1,0:T(8,128)(2,1)}, u32[]{:S(2)}, u32[]{:S(2)}) async-start(bf16[16,128,1536]{2,1,0:T(8,128)(2,1)} %select_select_fusion), calls=%async_computation.2 | async-start | bytes 12582912 | tf_op jit(solution)/shard_map/all_to_all | solution.py:54
  30.8 14.7 %all-gather.2.cloned.1.call-done = bf16[2048,1024]{1,0:T(8,128)(2,1)} async-done(((bf16[256,1024]{1,0:T(8,128)(2,1)}), bf16[2048,1024]{1,0:T(8,128)(2,1)}) %all-gather.2.cloned.1.call-update) | async-done | bytes 4194320 | tf_op jit(solution)/shard_map/all_gather | solution.py:57
  45.5 23.4 %fusion.2 = bf16[4096,1024]{1,0:T(8,128)(2,1)} fusion(bf16[2048,1024]{1,0:T(8,128)(2,1)} %all-gather.2.cloned.1.call-done, bf16[4096,1,2048]{2,0,1:T(8,128)(2,1)} %param.6), kind=kOutput, calls=%fused_computation.9 | convolution fusion | flops 17184063488 | bytes 29360128 | tf_op jit(solution)/shard_map/dot_general | solution.py:58
  68.9 54.3 %all-to-all-done.2 = bf16[16,128,1536]{2,1,0:T(8,128)(2,1)} async-done(((bf16[16,128,1536]{2,1,0:T(8,128)(2,1)}), bf16[16,128,1536]{2,1,0:T(8,128)(2,1)}, u32[]{:S(2)}, u32[]{:S(2)}) %all-to-all-start.2) | async-done | bytes 6291488 | tf_op jit(solution)/shard_map/all_to_all | solution.py:54
  123.2 9.7 %copy.112 = bf16[512,8,16,128]{3,2,1,0:T(8,128)(2,1)S(1)} copy(bf16[512,8,16,128]{3,1,2,0:T(8,128)(2,1)} %bitcast.88) | data formatting | bytes 33554432
  132.9 8.2 %copy.98 = bf16[32,128,16,128]{3,1,2,0:T(8,128)(2,1)} copy(bf16[32,128,16,128]{3,2,1,0:T(8,128)(2,1)S(1)} %bitcast.84) | data formatting | bytes 33554432 | tf_op jit(solution)/shard_map/reshape;squeeze | solution.py:48
  141.4 9.3 %gather_fusion.1 = bf16[128,128,128]{2,1,0:T(8,128)(2,1)} fusion(bf16[32,128,16,128]{3,1,2,0:T(8,128)(2,1)} %copy.98, s32[128]{0:T(128)S(1)} %reshape.158), kind=kCustom, calls=%fused_computation.1 | custom fusion | bytes 8389632 | tf_op jit(solution)/shard_map/gather | solution.py:49
  150.7 4.5 broadcast_select_fusion
  155.2 5.5 %all-to-all-start = ((bf16[16,8,128,128]{3,2,1,0:T(8,128)(2,1)}), bf16[16,8,128,128]{3,2,1,0:T(8,128)(2,1)}, u32[]{:S(2)}, u32[]{:S(2)}) async-start(bf16[16,8,128,128]{3,2,1,0:T(8,128)(2,1)} %broadcast_select_fusion), calls=%async_computation | async-start | bytes 8388608 | tf_op jit(solution)/shard_map/all_to_all | solution.py:55
  161.3 70.9 %all-to-all-done = bf16[16,8,128,128]{3,2,1,0:T(8,128)(2,1)} async-done(((bf16[16,8,128,128]{3,2,1,0:T(8,128)(2,1)}), bf16[16,8,128,128]{3,2,1,0:T(8,128)(2,1)}, u32[]{:S(2)}, u32[]{:S(2)}) %all-to-all-start) | async-done | bytes 4194336 | tf_op jit(solution)/shard_map/all_to_all | solution.py:55
  232.1 3.1 gather_fusion.2
  235.3 2.7 copy_select_fusion
  238.0 5.8 %all-to-all-start.1 = ((bf16[8,8,128,128]{3,1,2,0:T(8,128)(2,1)}), bf16[8,8,128,128]{3,1,2,0:T(8,128)(2,1)S(1)}, u32[]{:S(2)}, u32[]{:S(2)}) async-start(bf16[8,8,128,128]{3,1,2,0:T(8,128)(2,1)} %copy_select_fusion), calls=%async_computation.1 | async-start | bytes 4194304 | tf_op jit(solution)/shard_map/all_to_all | solution.py:80
  244.2 5.2 gather_fusion.4
  249.4 4.0 select_select_fusion.2
  253.3 16.8 %all-to-all-done.1 = bf16[8,8,128,128]{3,1,2,0:T(8,128)(2,1)S(1)} async-done(((bf16[8,8,128,128]{3,1,2,0:T(8,128)(2,1)}), bf16[8,8,128,128]{3,1,2,0:T(8,128)(2,1)S(1)}, u32[]{:S(2)}, u32[]{:S(2)}) %all-to-all-start.1) | async-done | bytes 2097184 | tf_op jit(solution)/shard_map/all_to_all | solution.py:80
  270.1 5.3 all-to-all-start.3
  275.4 3.8 gather_fusion.5
  279.2 4.7 select_select_fusion.1
  283.9 29.2 %all-to-all-done.3 = bf16[8,128,1536]{2,1,0:T(8,128)(2,1)} async-done(((bf16[8,128,1536]{2,1,0:T(8,128)(2,1)}), bf16[8,128,1536]{2,1,0:T(8,128)(2,1)}, u32[]{:S(2)}, u32[]{:S(2)}) %all-to-all-start.3) | async-done | bytes 3145760 | tf_op jit(solution)/shard_map/all_to_all | solution.py:79
  313.1 4.5 all-to-all-start.4
  317.6 2.8 convolution_bitcast_fusion.1
  320.4 3.9 fusion.12
  324.2 55.6 %all-to-all-done.4 = bf16[16,128,1024]{2,1,0:T(8,128)(2,1)} async-done(((bf16[16,128,1024]{2,1,0:T(8,128)(2,1)}), bf16[16,128,1024]{2,1,0:T(8,128)(2,1)}, u32[]{:S(2)}, u32[]{:S(2)}) %all-to-all-start.4) | async-done | bytes 4194336 | tf_op jit(solution)/shard_map/all_to_all | solution.py:86
  379.8 2.9 gather_fusion.6
  384.3 6.1 %all-to-all-start.5 = ((bf16[8,128,1024]{2,1,0:T(8,128)(2,1)}), bf16[8,128,1024]{2,1,0:T(8,128)(2,1)}, u32[]{:S(2)}, u32[]{:S(2)}) async-start(bf16[8,128,1024]{2,1,0:T(8,128)(2,1)} %select_select_fusion.3), calls=%async_computation.6 | async-start | bytes 4194304 | tf_op jit(solution)/shard_map/all_to_all | solution.py:89
  390.4 2.0 fusion.18
  393.4 2.7 convolution_bitcast_fusion
  396.1 112.6 %all-reduce.1 = bf16[1024,1024]{0,1:T(8,128)(2,1)} all-reduce(f32[1024,1024]{0,1:T(8,128)} %convolution_bitcast_fusion), channel_id=1, replica_groups=mesh['row'=8,'col'=16] {'row','col'}, use_global_device_ids=true, to_apply=%region_5.6 | all-reduce | flops 1048576 | bytes 6291456 | tf_op jit(solution)/shard_map/psum | solution.py:67
  508.7 6.4 %convolution_convert_fusion = bf16[1024,512]{1,0:T(8,128)(2,1)S(1)} fusion(bf16[1,1,1024,512]{3,2,1,0:T(8,128)(2,1)S(1)} %copy-done, bf16[1024,1024]{1,0:T(8,128)(2,1)} %bitcast.28, bf16[1024,1024]{0,1:T(8,128)(2,1)} %all-reduce.1, bf16[1024,1536]{1,0:T(8,128)(2,1)} %bitcast.20), kind=kOutput, calls=%fused_computation.27 | convolution fusion | flops 3225944064 | bytes 8388608 | tf_op jit(solution)/shard_map/xm,xi->mi/dot_general | solution.py:102
  (55 shorter events, 15.4 us)
Async XLA Ops:
  7.2 310.4 %copy-start = (bf16[1,1,1024,512]{3,2,1,0:T(8,128)(2,1)S(1)}, bf16[1,1,1024,512]{3,2,1,0:T(8,128)(2,1)}, u32[]{:S(2)}) copy-start(bf16[1,1,1024,512]{3,2,1,0:T(8,128)(2,1)} %param.9) | copy-start | bytes 3145732
  7.2 38.3 %all-gather.2.cloned.1.call-start = ((), (), s32[]{:S(2)}) async-start(), calls=%async_computation.7 | async-start | bytes 4718592 | tf_op jit(solution)/shard_map/all_gather | solution.py:57
  22.2 101.0 %all-to-all-start.2 = ((bf16[16,128,1536]{2,1,0:T(8,128)(2,1)}), bf16[16,128,1536]{2,1,0:T(8,128)(2,1)}, u32[]{:S(2)}, u32[]{:S(2)}) async-start(bf16[16,128,1536]{2,1,0:T(8,128)(2,1)} %select_select_fusion), calls=%async_computation.2 | async-start | bytes 12582912 | tf_op jit(solution)/shard_map/all_to_all | solution.py:54
  30.7 244.6 %reduce-scatter.2.cloned.1.call-start = ((), (), s32[]{:S(2)}) async-start(), calls=%async_computation.8 | async-start | bytes 8912896 | tf_op jit(solution)/shard_map/reduce_scatter | solution.py:60
  155.2 76.9 %all-to-all-start = ((bf16[16,8,128,128]{3,2,1,0:T(8,128)(2,1)}), bf16[16,8,128,128]{3,2,1,0:T(8,128)(2,1)}, u32[]{:S(2)}, u32[]{:S(2)}) async-start(bf16[16,8,128,128]{3,2,1,0:T(8,128)(2,1)} %broadcast_select_fusion), calls=%async_computation | async-start | bytes 8388608 | tf_op jit(solution)/shard_map/all_to_all | solution.py:55
  238.0 32.1 %all-to-all-start.1 = ((bf16[8,8,128,128]{3,1,2,0:T(8,128)(2,1)}), bf16[8,8,128,128]{3,1,2,0:T(8,128)(2,1)S(1)}, u32[]{:S(2)}, u32[]{:S(2)}) async-start(bf16[8,8,128,128]{3,1,2,0:T(8,128)(2,1)} %copy_select_fusion), calls=%async_computation.1 | async-start | bytes 4194304 | tf_op jit(solution)/shard_map/all_to_all | solution.py:80
  270.1 43.0 %all-to-all-start.3 = ((bf16[8,128,1536]{2,1,0:T(8,128)(2,1)}), bf16[8,128,1536]{2,1,0:T(8,128)(2,1)}, u32[]{:S(2)}, u32[]{:S(2)}) async-start(bf16[8,128,1536]{2,1,0:T(8,128)(2,1)} %select_select_fusion.2), calls=%async_computation.3 | async-start | bytes 6291456 | tf_op jit(solution)/shard_map/all_to_all | solution.py:79
  313.1 66.7 %all-to-all-start.4 = ((bf16[16,128,1024]{2,1,0:T(8,128)(2,1)}), bf16[16,128,1024]{2,1,0:T(8,128)(2,1)}, u32[]{:S(2)}, u32[]{:S(2)}) async-start(bf16[16,128,1024]{2,1,0:T(8,128)(2,1)} %select_select_fusion.1), calls=%async_computation.5 | async-start | bytes 8388608 | tf_op jit(solution)/shard_map/all_to_all | solution.py:86
  384.3 124.4 %all-to-all-start.5 = ((bf16[8,128,1024]{2,1,0:T(8,128)(2,1)}), bf16[8,128,1024]{2,1,0:T(8,128)(2,1)}, u32[]{:S(2)}, u32[]{:S(2)}) async-start(bf16[8,128,1024]{2,1,0:T(8,128)(2,1)} %select_select_fusion.3), calls=%async_computation.6 | async-start | bytes 4194304 | tf_op jit(solution)/shard_map/all_to_all | solution.py:89
  390.4 3.1 copy-start.1
  390.4 3.1 copy-start.2
  508.7 7.4 %copy-start.3 = (bf16[1024,512]{1,0:T(8,128)(2,1)S(1)}, bf16[1024,512]{1,0:T(8,128)(2,1)}, u32[]{:S(2)}) copy-start(bf16[1024,512]{1,0:T(8,128)(2,1)} %fusion.12) | copy-start | bytes 3145732
  515.1 1.0 copy-start.4
Sparse Core Ops, SparseCore 0:
  9.7 35.7 all-gather.1
  123.4 132.6 reduce-scatter.1

commit v7 on v6

--- a/solution.py
+++ b/solution.py
@@ -56,7 +56,7 @@
 
     gathered = lax.all_gather(lmo_coef, "row", axis=0, tiled=True)
     fock_lmo = jnp.dot(panel_fock, gathered, preferred_element_type=F32).astype(BF16)
-    rows_a, fock_lmo = lax.optimization_barrier((rows_a, fock_lmo))
+    rows_a, tiles_a, fock_lmo = lax.optimization_barrier((rows_a, tiles_a, fock_lmo))
     coef_b = lax.psum_scatter(
         fock_lmo,
         "col",

time: 530 us -> 520 us (0.981)
  waiting for transfers between devices: 242 us -> 230 us
    reduce_scatter x1, waiting for transfers between devices: 0.01 us -> 40.5 us  [body(): coef_b = lax.psum_scatter(fock_lmo, 'col', scatter_dimension=0, tiled=True)]
    all_to_all x1, waiting for transfers between devices: 29.2 us -> 0.01 us  [body(): lax.all_to_all(rows_b, 'row', 0, 0, tiled=True)]
    all_to_all x1, waiting for transfers between devices: 70.9 us -> 52.3 us  [body(): tiles_a = lax.all_to_all(tiles_a, 'col', 0, 0, tiled=True)]
    all_gather x1, waiting for transfers between devices: 14.7 us -> 0.02 us  [body(): gathered = lax.all_gather(lmo_coef, 'row', axis=0, tiled=True)]
    all_to_all x1, waiting for transfers between devices: 54.3 us -> 67.2 us  [body(): rows_a = lax.all_to_all(rows_a, 'col', 0, 0, tiled=True)]
    unnamed x15 -> x19, local copies, waits for them, and re-layouts: 13.8 us -> 13.8 us
  transfers between devices with their start and end apart: 8 -> 8, of which waited for: 6 -> 5; matrix products, arithmetic and copies ran while one was open for 20% -> 20% of each run, Pallas kernels for 0% -> 0%
where the time goes in v7:
time: 520 us; the launch traced here: 518 us
  waiting for transfers between devices  230 us (44%)
  blocking collectives  113 us (22%)
  local copies, waits for them, and re-layouts  51.7 us (10%)
  matrix products  45.1 us (9%)
  starting transfers between devices  38 us (7%)
  other arithmetic  25.3 us (5%)
  between operations  14.2 us (3%)
    psum x1, blocking collectives, body(): occ_b = lax.psum(occ_term, ('row', 'col')).astype(BF16)  113 us
    all_to_all x1, waiting for transfers between devices, body(): rows_a = lax.all_to_all(rows_a, 'col', 0, 0, tiled=True)  67.2 us
    all_to_all x1, waiting for transfers between devices, body(): fc_a = lax.all_to_all(fc_a, 'col', 0, 0, tiled=True)  52.7 us
    all_to_all x1, waiting for transfers between devices, body(): tiles_a = lax.all_to_all(tiles_a, 'col', 0, 0, tiled=True)  52.3 us
    reduce_scatter x1, waiting for transfers between devices, body(): coef_b = lax.psum_scatter(fock_lmo, 'col', scatter_dimension=0, tiled=True)  40.5 us
    dot_general x1, matrix products, body(): jnp.dot(panel_fock, gathered, preferred_element_type=F32).astype(BF16)  23.4 us
    all_to_all x1, waiting for transfers between devices, body(): lax.all_to_all(tiles_b, 'row', 0, 0, tiled=True)  16.8 us
    unnamed x19, local copies, waits for them, and re-layouts  13.8 us
  transfers between devices with their start and end apart: 8, of which 5 were waited for; matrix products, arithmetic and copies ran while one was open for 20% of the time, Pallas kernels for 0%

profile of v7, /device:TPU:1, one launch (start us, length us, event | category | flops | bytes accessed | tf_op | source)
XLA Modules:
  0.0 518.0 jit_solution(3878181022950921929)
XLA Ops:
  11.3 9.7 %copy.112 = bf16[512,8,16,128]{3,2,1,0:T(8,128)(2,1)S(1)} copy(bf16[512,8,16,128]{3,1,2,0:T(8,128)(2,1)} %bitcast.88) | data formatting | bytes 33554432
  21.0 8.1 %copy.98 = bf16[32,128,16,128]{3,1,2,0:T(8,128)(2,1)} copy(bf16[32,128,16,128]{3,2,1,0:T(8,128)(2,1)S(1)} %bitcast.84) | data formatting | bytes 33554432 | tf_op jit(solution)/shard_map/reshape;squeeze | solution.py:48
  29.3 9.2 %gather_fusion.2 = bf16[128,128,128]{2,1,0:T(8,128)(2,1)} fusion(bf16[32,128,16,128]{3,1,2,0:T(8,128)(2,1)} %copy.98, s32[128]{0:T(128)S(1)} %reshape.166), kind=kCustom, calls=%fused_computation.2 | custom fusion | bytes 8389632 | tf_op jit(solution)/shard_map/gather | solution.py:49
  38.5 4.6 broadcast_select_fusion
  43.0 8.6 %all-to-all-start.1 = ((bf16[16,8,128,128]{3,2,1,0:T(8,128)(2,1)}), bf16[16,8,128,128]{3,2,1,0:T(8,128)(2,1)}, u32[]{:S(2)}, u32[]{:S(2)}) async-start(bf16[16,8,128,128]{3,2,1,0:T(8,128)(2,1)} %broadcast_select_fusion), calls=%async_computation.1 | async-start | bytes 8388608 | tf_op jit(solution)/shard_map/all_to_all | solution.py:55
  51.8 3.5 gather_fusion.1
  55.3 6.1 %select_select_fusion = bf16[16,128,1536]{2,1,0:T(8,128)(2,1)} fusion(bf16[16,128,1536]{2,1,0:T(8,128)(2,1)} %gather_fusion.1, pred[16]{0:T(512)(128)(4,1)S(1)} %compare_and_fusion.3, pred[16]{0:T(512)(128)(4,1)S(1)} %get-tuple-element.24), kind=kLoop, calls=%fused_computation.10 | loop fusion | flops 6291456 | bytes 12582944 | tf_op jit(solution)/shard_map/jit(_where)/select_n | solution.py:53
  61.4 52.3 %all-to-all-done.1 = bf16[16,8,128,128]{3,2,1,0:T(8,128)(2,1)} async-done(((bf16[16,8,128,128]{3,2,1,0:T(8,128)(2,1)}), bf16[16,8,128,128]{3,2,1,0:T(8,128)(2,1)}, u32[]{:S(2)}, u32[]{:S(2)}) %all-to-all-start.1) | async-done | bytes 4194336 | tf_op jit(solution)/shard_map/all_to_all | solution.py:55
  113.7 4.7 all-to-all-start
  118.5 23.4 %fusion.2 = bf16[4096,1024]{1,0:T(8,128)(2,1)} fusion(bf16[2048,1024]{1,0:T(8,128)(2,1)} %all-gather.2.cloned.1.call-done, bf16[4096,1,2048]{2,0,1:T(8,128)(2,1)} %param.6), kind=kOutput, calls=%fused_computation.9 | convolution fusion | flops 17184063488 | bytes 29360128 | tf_op jit(solution)/shard_map/dot_general | solution.py:58
  141.9 67.2 %all-to-all-done = bf16[16,128,1536]{2,1,0:T(8,128)(2,1)} async-done(((bf16[16,128,1536]{2,1,0:T(8,128)(2,1)}), bf16[16,128,1536]{2,1,0:T(8,128)(2,1)}, u32[]{:S(2)}, u32[]{:S(2)}) %all-to-all-start) | async-done | bytes 6291488 | tf_op jit(solution)/shard_map/all_to_all | solution.py:54
  209.7 3.2 gather_fusion.3
  212.9 2.7 copy_select_fusion
  215.6 7.4 %all-to-all-start.2 = ((bf16[8,8,128,128]{3,1,2,0:T(8,128)(2,1)}), bf16[8,8,128,128]{3,1,2,0:T(8,128)(2,1)S(1)}, u32[]{:S(2)}, u32[]{:S(2)}) async-start(bf16[8,8,128,128]{3,1,2,0:T(8,128)(2,1)} %copy_select_fusion), calls=%async_computation.2 | async-start | bytes 4194304 | tf_op jit(solution)/shard_map/all_to_all | solution.py:80
  223.4 5.2 %gather_fusion.4 = bf16[8,128,1536]{2,1,0:T(8,128)(2,1)} fusion(bf16[16,128,1536]{2,1,0:T(8,128)(2,1)} %all-to-all-done, s32[1024]{0:T(1024)S(1)} %pad_clamp_fusion), kind=kCustom, calls=%fused_computation.4 | custom fusion | bytes 6291488 | tf_op jit(solution)/shard_map/jit(_take)/gather | solution.py:73
  228.6 4.0 select_select_fusion.2
  232.6 16.8 %all-to-all-done.2 = bf16[8,8,128,128]{3,1,2,0:T(8,128)(2,1)S(1)} async-done(((bf16[8,8,128,128]{3,1,2,0:T(8,128)(2,1)}), bf16[8,8,128,128]{3,1,2,0:T(8,128)(2,1)S(1)}, u32[]{:S(2)}, u32[]{:S(2)}) %all-to-all-start.2) | async-done | bytes 2097184 | tf_op jit(solution)/shard_map/all_to_all | solution.py:80
  249.3 5.3 %all-to-all-start.3 = ((bf16[8,128,1536]{2,1,0:T(8,128)(2,1)}), bf16[8,128,1536]{2,1,0:T(8,128)(2,1)}, u32[]{:S(2)}, u32[]{:S(2)}) async-start(bf16[8,128,1536]{2,1,0:T(8,128)(2,1)} %select_select_fusion.2), calls=%async_computation.3 | async-start | bytes 6291456 | tf_op jit(solution)/shard_map/all_to_all | solution.py:79
  254.6 40.5 %reduce-scatter.2.cloned.1.call-done = bf16[256,1024]{1,0:T(8,128)(2,1)} async-done(((bf16[4096,1024]{1,0:T(8,128)(2,1)}), bf16[256,1024]{1,0:T(8,128)(2,1)}) %reduce-scatter.2.cloned.1.call-update) | async-done | bytes 524304 | tf_op jit(solution)/shard_map/reduce_scatter | solution.py:60
  295.1 3.8 gather_fusion.5
  298.9 4.7 select_select_fusion.1
  303.6 4.8 all-to-all-start.4
  308.4 2.8 convolution_bitcast_fusion.1
  311.1 3.8 fusion.12
  315.0 52.7 %all-to-all-done.4 = bf16[16,128,1024]{2,1,0:T(8,128)(2,1)} async-done(((bf16[16,128,1024]{2,1,0:T(8,128)(2,1)}), bf16[16,128,1024]{2,1,0:T(8,128)(2,1)}, u32[]{:S(2)}, u32[]{:S(2)}) %all-to-all-start.4) | async-done | bytes 4194336 | tf_op jit(solution)/shard_map/all_to_all | solution.py:86
  367.7 2.9 gather_fusion.6
  372.2 7.2 %all-to-all-start.5 = ((bf16[8,128,1024]{2,1,0:T(8,128)(2,1)}), bf16[8,128,1024]{2,1,0:T(8,128)(2,1)}, u32[]{:S(2)}, u32[]{:S(2)}) async-start(bf16[8,128,1024]{2,1,0:T(8,128)(2,1)} %select_select_fusion.3), calls=%async_computation.6 | async-start | bytes 4194304 | tf_op jit(solution)/shard_map/all_to_all | solution.py:89
  379.4 2.0 fusion.18
  382.4 2.7 convolution_bitcast_fusion
  385.1 113.4 %all-reduce.1 = bf16[1024,1024]{0,1:T(8,128)(2,1)} all-reduce(f32[1024,1024]{0,1:T(8,128)} %convolution_bitcast_fusion), channel_id=1, replica_groups=mesh['row'=8,'col'=16] {'row','col'}, use_global_device_ids=true, to_apply=%region_5.6 | all-reduce | flops 1048576 | bytes 6291456 | tf_op jit(solution)/shard_map/psum | solution.py:67
  498.5 6.4 %convolution_convert_fusion = bf16[1024,512]{1,0:T(8,128)(2,1)S(1)} fusion(bf16[1,1,1024,512]{3,2,1,0:T(8,128)(2,1)S(1)} %copy-done, bf16[1024,1024]{1,0:T(8,128)(2,1)} %bitcast.28, bf16[1024,1024]{0,1:T(8,128)(2,1)} %all-reduce.1, bf16[1024,1536]{1,0:T(8,128)(2,1)} %bitcast.20), kind=kOutput, calls=%fused_computation.27 | convolution fusion | flops 3225944064 | bytes 8388608 | tf_op jit(solution)/shard_map/xm,xi->mi/dot_general | solution.py:102
  507.9 2.0 fusion.17
  (59 shorter events, 12.3 us)
Async XLA Ops:
  7.2 301.2 %copy-start = (bf16[1,1,1024,512]{3,2,1,0:T(8,128)(2,1)S(1)}, bf16[1,1,1024,512]{3,2,1,0:T(8,128)(2,1)}, u32[]{:S(2)}) copy-start(bf16[1,1,1024,512]{3,2,1,0:T(8,128)(2,1)} %param.9) | copy-start | bytes 3145732
  7.2 111.3 %all-gather.2.cloned.1.call-start = ((), (), s32[]{:S(2)}) async-start(), calls=%async_computation.7 | async-start | bytes 4718592 | tf_op jit(solution)/shard_map/all_gather | solution.py:57
  43.0 8.7 %copy-start.2 = (bf16[256,1024]{1,0:T(8,128)(2,1)S(1)}, bf16[256,1024]{1,0:T(8,128)(2,1)}, u32[]{:S(2)}) copy-start(bf16[256,1024]{1,0:T(8,128)(2,1)} %param.7) | copy-start | bytes 1572868
  43.0 8.7 %copy-start.6 = (bf16[256,512]{1,0:T(8,128)(2,1)S(1)}, bf16[256,512]{1,0:T(8,128)(2,1)}, u32[]{:S(2)}) copy-start(bf16[256,512]{1,0:T(8,128)(2,1)} %param.8) | copy-start | bytes 786436
  43.0 70.7 %all-to-all-start.1 = ((bf16[16,8,128,128]{3,2,1,0:T(8,128)(2,1)}), bf16[16,8,128,128]{3,2,1,0:T(8,128)(2,1)}, u32[]{:S(2)}, u32[]{:S(2)}) async-start(bf16[16,8,128,128]{3,2,1,0:T(8,128)(2,1)} %broadcast_select_fusion), calls=%async_computation.1 | async-start | bytes 8388608 | tf_op jit(solution)/shard_map/all_to_all | solution.py:55
  113.7 95.4 %all-to-all-start = ((bf16[16,128,1536]{2,1,0:T(8,128)(2,1)}), bf16[16,128,1536]{2,1,0:T(8,128)(2,1)}, u32[]{:S(2)}, u32[]{:S(2)}) async-start(bf16[16,128,1536]{2,1,0:T(8,128)(2,1)} %select_select_fusion), calls=%async_computation | async-start | bytes 12582912 | tf_op jit(solution)/shard_map/all_to_all | solution.py:54
  118.4 176.7 %reduce-scatter.2.cloned.1.call-start = ((), (), s32[]{:S(2)}) async-start(), calls=%async_computation.8 | async-start | bytes 8912896 | tf_op jit(solution)/shard_map/reduce_scatter | solution.py:60
  215.6 33.8 %all-to-all-start.2 = ((bf16[8,8,128,128]{3,1,2,0:T(8,128)(2,1)}), bf16[8,8,128,128]{3,1,2,0:T(8,128)(2,1)S(1)}, u32[]{:S(2)}, u32[]{:S(2)}) async-start(bf16[8,8,128,128]{3,1,2,0:T(8,128)(2,1)} %copy_select_fusion), calls=%async_computation.2 | async-start | bytes 4194304 | tf_op jit(solution)/shard_map/all_to_all | solution.py:80
  249.3 54.3 %all-to-all-start.3 = ((bf16[8,128,1536]{2,1,0:T(8,128)(2,1)}), bf16[8,128,1536]{2,1,0:T(8,128)(2,1)}, u32[]{:S(2)}, u32[]{:S(2)}) async-start(bf16[8,128,1536]{2,1,0:T(8,128)(2,1)} %select_select_fusion.2), calls=%async_computation.3 | async-start | bytes 6291456 | tf_op jit(solution)/shard_map/all_to_all | solution.py:79
  303.6 64.1 %all-to-all-start.4 = ((bf16[16,128,1024]{2,1,0:T(8,128)(2,1)}), bf16[16,128,1024]{2,1,0:T(8,128)(2,1)}, u32[]{:S(2)}, u32[]{:S(2)}) async-start(bf16[16,128,1024]{2,1,0:T(8,128)(2,1)} %select_select_fusion.1), calls=%async_computation.5 | async-start | bytes 8388608 | tf_op jit(solution)/shard_map/all_to_all | solution.py:86
  372.2 126.3 %all-to-all-start.5 = ((bf16[8,128,1024]{2,1,0:T(8,128)(2,1)}), bf16[8,128,1024]{2,1,0:T(8,128)(2,1)}, u32[]{:S(2)}, u32[]{:S(2)}) async-start(bf16[8,128,1024]{2,1,0:T(8,128)(2,1)} %select_select_fusion.3), calls=%async_computation.6 | async-start | bytes 4194304 | tf_op jit(solution)/shard_map/all_to_all | solution.py:89
  379.4 3.1 copy-start.1
  379.4 3.1 copy-start.3
  498.5 7.4 %copy-start.4 = (bf16[1024,512]{1,0:T(8,128)(2,1)S(1)}, bf16[1024,512]{1,0:T(8,128)(2,1)}, u32[]{:S(2)}) copy-start(bf16[1024,512]{1,0:T(8,128)(2,1)} %fusion.12) | copy-start | bytes 3145732
  504.9 1.0 copy-start.5
Sparse Core Ops, SparseCore 0:
  9.7 35.7 all-gather.1
  209.3 85.7 reduce-scatter.1

commit v8 on v7

--- a/solution.py
+++ b/solution.py
@@ -52,6 +52,7 @@
     rows_a = jnp.take(in_rows, sub_o, axis=0)
     rows_a = jnp.where(has_o[:, None, None], rows_a, jnp.zeros_like(rows_a))
     rows_a = lax.all_to_all(rows_a, "col", 0, 0, tiled=True)
+    tiles_a, rows_a = lax.optimization_barrier((tiles_a, rows_a))
     tiles_a = lax.all_to_all(tiles_a, "col", 0, 0, tiled=True)
 
     gathered = lax.all_gather(lmo_coef, "row", axis=0, tiled=True)

time: 520 us -> 497 us (0.956)
  waiting for transfers between devices: 230 us -> 206 us
    all_to_all x1, waiting for transfers between devices: 52.3 us -> 35.9 us  [body(): tiles_a = lax.all_to_all(tiles_a, 'col', 0, 0, tiled=True)]
    all_to_all x1, waiting for transfers between devices: 67.2 us -> 60.6 us  [body(): rows_a = lax.all_to_all(rows_a, 'col', 0, 0, tiled=True)]
    unnamed x19 -> x15, local copies, waits for them, and re-layouts: 13.8 us -> 14.1 us
  transfers between devices with their start and end apart: 8 -> 8, of which waited for: 5 -> 5; matrix products, arithmetic and copies ran while one was open for 20% -> 22% of each run, Pallas kernels for 0% -> 0%
where the time goes in v8:
time: 497 us; the launch traced here: 495 us
  waiting for transfers between devices  206 us (41%)
  blocking collectives  113 us (23%)
  local copies, waits for them, and re-layouts  52 us (10%)
  matrix products  45.1 us (9%)
  starting transfers between devices  38.5 us (8%)
  other arithmetic  26.6 us (5%)
  between operations  14.2 us (3%)
    psum x1, blocking collectives, body(): occ_b = lax.psum(occ_term, ('row', 'col')).astype(BF16)  113 us
    all_to_all x1, waiting for transfers between devices, body(): rows_a = lax.all_to_all(rows_a, 'col', 0, 0, tiled=True)  60.6 us
    all_to_all x1, waiting for transfers between devices, body(): fc_a = lax.all_to_all(fc_a, 'col', 0, 0, tiled=True)  52.7 us
    reduce_scatter x1, waiting for transfers between devices, body(): coef_b = lax.psum_scatter(fock_lmo, 'col', scatter_dimension=0, tiled=True)  39.1 us
    all_to_all x1, waiting for transfers between devices, body(): tiles_a = lax.all_to_all(tiles_a, 'col', 0, 0, tiled=True)  35.9 us
    dot_general x1, matrix products, body(): jnp.dot(panel_fock, gathered, preferred_element_type=F32).astype(BF16)  23.4 us
    all_to_all x1, waiting for transfers between devices, body(): lax.all_to_all(tiles_b, 'row', 0, 0, tiled=True)  16.5 us
    unnamed x15, local copies, waits for them, and re-layouts  14.1 us
  transfers between devices with their start and end apart: 8, of which 5 were waited for; matrix products, arithmetic and copies ran while one was open for 22% of the time, Pallas kernels for 0%

profile of v8, /device:TPU:1, one launch (start us, length us, event | category | flops | bytes accessed | tf_op | source)
XLA Modules:
  0.0 495.4 jit_solution(15191098055456916409)
XLA Ops:
  12.4 3.6 gather_fusion.2
  16.0 6.2 %select_select_fusion = bf16[16,128,1536]{2,1,0:T(8,128)(2,1)} fusion(bf16[16,128,1536]{2,1,0:T(8,128)(2,1)} %gather_fusion.2, pred[16]{0:T(512)(128)(4,1)S(1)} %compare_and_fusion.3, pred[16]{0:T(512)(128)(4,1)S(1)} %get-tuple-element.24), kind=kLoop, calls=%fused_computation.10 | loop fusion | flops 6291456 | bytes 12582944 | tf_op jit(solution)/shard_map/jit(_where)/select_n | solution.py:53
  22.2 8.5 %all-to-all-start = ((bf16[16,128,1536]{2,1,0:T(8,128)(2,1)}), bf16[16,128,1536]{2,1,0:T(8,128)(2,1)}, u32[]{:S(2)}, u32[]{:S(2)}) async-start(bf16[16,128,1536]{2,1,0:T(8,128)(2,1)} %select_select_fusion), calls=%async_computation | async-start | bytes 12582912 | tf_op jit(solution)/shard_map/all_to_all | solution.py:54
  30.7 9.9 %copy.112 = bf16[512,8,16,128]{3,2,1,0:T(8,128)(2,1)S(1)} copy(bf16[512,8,16,128]{3,1,2,0:T(8,128)(2,1)} %bitcast.88) | data formatting | bytes 33554432
  40.7 8.1 %copy.98 = bf16[32,128,16,128]{3,1,2,0:T(8,128)(2,1)} copy(bf16[32,128,16,128]{3,2,1,0:T(8,128)(2,1)S(1)} %bitcast.84) | data formatting | bytes 33554432 | tf_op jit(solution)/shard_map/reshape;squeeze | solution.py:48
  49.2 8.9 %gather_fusion.1 = bf16[128,128,128]{2,1,0:T(8,128)(2,1)} fusion(bf16[32,128,16,128]{3,1,2,0:T(8,128)(2,1)} %copy.98, s32[128]{0:T(128)S(1)} %reshape.158), kind=kCustom, calls=%fused_computation.1 | custom fusion | bytes 8389632 | tf_op jit(solution)/shard_map/gather | solution.py:49
  58.1 4.5 broadcast_select_fusion
  62.6 60.6 %all-to-all-done = bf16[16,128,1536]{2,1,0:T(8,128)(2,1)} async-done(((bf16[16,128,1536]{2,1,0:T(8,128)(2,1)}), bf16[16,128,1536]{2,1,0:T(8,128)(2,1)}, u32[]{:S(2)}, u32[]{:S(2)}) %all-to-all-start) | async-done | bytes 6291488 | tf_op jit(solution)/shard_map/all_to_all | solution.py:54
  123.2 5.3 %all-to-all-start.1 = ((bf16[16,8,128,128]{3,2,1,0:T(8,128)(2,1)}), bf16[16,8,128,128]{3,2,1,0:T(8,128)(2,1)}, u32[]{:S(2)}, u32[]{:S(2)}) async-start(bf16[16,8,128,128]{3,2,1,0:T(8,128)(2,1)} %broadcast_select_fusion), calls=%async_computation.1 | async-start | bytes 8388608 | tf_op jit(solution)/shard_map/all_to_all | solution.py:56
  128.6 23.4 %fusion.2 = bf16[4096,1024]{1,0:T(8,128)(2,1)} fusion(bf16[2048,1024]{1,0:T(8,128)(2,1)} %all-gather.2.cloned.1.call-done, bf16[4096,1,2048]{2,0,1:T(8,128)(2,1)} %param.6), kind=kOutput, calls=%fused_computation.9 | convolution fusion | flops 17184063488 | bytes 29360128 | tf_op jit(solution)/shard_map/dot_general | solution.py:59
  152.1 35.9 %all-to-all-done.1 = bf16[16,8,128,128]{3,2,1,0:T(8,128)(2,1)} async-done(((bf16[16,8,128,128]{3,2,1,0:T(8,128)(2,1)}), bf16[16,8,128,128]{3,2,1,0:T(8,128)(2,1)}, u32[]{:S(2)}, u32[]{:S(2)}) %all-to-all-start.1) | async-done | bytes 4194336 | tf_op jit(solution)/shard_map/all_to_all | solution.py:56
  188.5 3.2 gather_fusion.3
  191.7 2.7 copy_select_fusion
  194.3 7.3 %all-to-all-start.2 = ((bf16[8,8,128,128]{3,1,2,0:T(8,128)(2,1)}), bf16[8,8,128,128]{3,1,2,0:T(8,128)(2,1)S(1)}, u32[]{:S(2)}, u32[]{:S(2)}) async-start(bf16[8,8,128,128]{3,1,2,0:T(8,128)(2,1)} %copy_select_fusion), calls=%async_computation.2 | async-start | bytes 4194304 | tf_op jit(solution)/shard_map/all_to_all | solution.py:81
  202.1 5.4 %gather_fusion.4 = bf16[8,128,1536]{2,1,0:T(8,128)(2,1)} fusion(bf16[16,128,1536]{2,1,0:T(8,128)(2,1)} %all-to-all-done, s32[1024]{0:T(1024)S(1)} %pad_clamp_fusion), kind=kCustom, calls=%fused_computation.4 | custom fusion | bytes 6291488 | tf_op jit(solution)/shard_map/jit(_take)/gather | solution.py:74
  207.4 4.1 select_select_fusion.2
  211.5 16.5 %all-to-all-done.2 = bf16[8,8,128,128]{3,1,2,0:T(8,128)(2,1)S(1)} async-done(((bf16[8,8,128,128]{3,1,2,0:T(8,128)(2,1)}), bf16[8,8,128,128]{3,1,2,0:T(8,128)(2,1)S(1)}, u32[]{:S(2)}, u32[]{:S(2)}) %all-to-all-start.2) | async-done | bytes 2097184 | tf_op jit(solution)/shard_map/all_to_all | solution.py:81
  228.0 5.3 %all-to-all-start.3 = ((bf16[8,128,1536]{2,1,0:T(8,128)(2,1)}), bf16[8,128,1536]{2,1,0:T(8,128)(2,1)}, u32[]{:S(2)}, u32[]{:S(2)}) async-start(bf16[8,128,1536]{2,1,0:T(8,128)(2,1)} %select_select_fusion.2), calls=%async_computation.3 | async-start | bytes 6291456 | tf_op jit(solution)/shard_map/all_to_all | solution.py:80
  233.3 39.1 %reduce-scatter.2.cloned.1.call-done = bf16[256,1024]{1,0:T(8,128)(2,1)} async-done(((bf16[4096,1024]{1,0:T(8,128)(2,1)}), bf16[256,1024]{1,0:T(8,128)(2,1)}) %reduce-scatter.2.cloned.1.call-update) | async-done | bytes 524304 | tf_op jit(solution)/shard_map/reduce_scatter | solution.py:61
  272.3 3.8 gather_fusion.5
  276.2 4.7 select_select_fusion.1
  280.9 4.9 all-to-all-start.4
  285.8 2.8 convolution_bitcast_fusion.1
  288.5 3.9 fusion.12
  292.4 52.7 %all-to-all-done.4 = bf16[16,128,1024]{2,1,0:T(8,128)(2,1)} async-done(((bf16[16,128,1024]{2,1,0:T(8,128)(2,1)}), bf16[16,128,1024]{2,1,0:T(8,128)(2,1)}, u32[]{:S(2)}, u32[]{:S(2)}) %all-to-all-start.4) | async-done | bytes 4194336 | tf_op jit(solution)/shard_map/all_to_all | solution.py:87
  345.1 2.9 gather_fusion.6
  349.6 7.1 %all-to-all-start.5 = ((bf16[8,128,1024]{2,1,0:T(8,128)(2,1)}), bf16[8,128,1024]{2,1,0:T(8,128)(2,1)}, u32[]{:S(2)}, u32[]{:S(2)}) async-start(bf16[8,128,1024]{2,1,0:T(8,128)(2,1)} %select_select_fusion.3), calls=%async_computation.6 | async-start | bytes 4194304 | tf_op jit(solution)/shard_map/all_to_all | solution.py:90
  356.8 2.0 fusion.18
  359.8 2.7 convolution_bitcast_fusion
  362.5 113.3 %all-reduce.1 = bf16[1024,1024]{0,1:T(8,128)(2,1)} all-reduce(f32[1024,1024]{0,1:T(8,128)} %convolution_bitcast_fusion), channel_id=1, replica_groups=mesh['row'=8,'col'=16] {'row','col'}, use_global_device_ids=true, to_apply=%region_5.6 | all-reduce | flops 1048576 | bytes 6291456 | tf_op jit(solution)/shard_map/psum | solution.py:68
  475.9 6.4 %convolution_convert_fusion = bf16[1024,512]{1,0:T(8,128)(2,1)S(1)} fusion(bf16[1,1,1024,512]{3,2,1,0:T(8,128)(2,1)S(1)} %copy-done, bf16[1024,1024]{1,0:T(8,128)(2,1)} %bitcast.28, bf16[1024,1024]{0,1:T(8,128)(2,1)} %all-reduce.1, bf16[1024,1536]{1,0:T(8,128)(2,1)} %bitcast.20), kind=kOutput, calls=%fused_computation.27 | convolution fusion | flops 3225944064 | bytes 8388608 | tf_op jit(solution)/shard_map/xm,xi->mi/dot_general | solution.py:103
  485.2 2.0 fusion.17
  (55 shorter events, 13.4 us)
Async XLA Ops:
  7.2 278.6 %copy-start = (bf16[1,1,1024,512]{3,2,1,0:T(8,128)(2,1)S(1)}, bf16[1,1,1024,512]{3,2,1,0:T(8,128)(2,1)}, u32[]{:S(2)}) copy-start(bf16[1,1,1024,512]{3,2,1,0:T(8,128)(2,1)} %param.9) | copy-start | bytes 3145732
  7.2 121.5 %all-gather.2.cloned.1.call-start = ((), (), s32[]{:S(2)}) async-start(), calls=%async_computation.7 | async-start | bytes 4718592 | tf_op jit(solution)/shard_map/all_gather | solution.py:58
  22.2 101.0 %all-to-all-start = ((bf16[16,128,1536]{2,1,0:T(8,128)(2,1)}), bf16[16,128,1536]{2,1,0:T(8,128)(2,1)}, u32[]{:S(2)}, u32[]{:S(2)}) async-start(bf16[16,128,1536]{2,1,0:T(8,128)(2,1)} %select_select_fusion), calls=%async_computation | async-start | bytes 12582912 | tf_op jit(solution)/shard_map/all_to_all | solution.py:54
  123.2 64.7 %all-to-all-start.1 = ((bf16[16,8,128,128]{3,2,1,0:T(8,128)(2,1)}), bf16[16,8,128,128]{3,2,1,0:T(8,128)(2,1)}, u32[]{:S(2)}, u32[]{:S(2)}) async-start(bf16[16,8,128,128]{3,2,1,0:T(8,128)(2,1)} %broadcast_select_fusion), calls=%async_computation.1 | async-start | bytes 8388608 | tf_op jit(solution)/shard_map/all_to_all | solution.py:56
  128.6 143.8 %reduce-scatter.2.cloned.1.call-start = ((), (), s32[]{:S(2)}) async-start(), calls=%async_computation.8 | async-start | bytes 8912896 | tf_op jit(solution)/shard_map/reduce_scatter | solution.py:61
  194.3 33.7 %all-to-all-start.2 = ((bf16[8,8,128,128]{3,1,2,0:T(8,128)(2,1)}), bf16[8,8,128,128]{3,1,2,0:T(8,128)(2,1)S(1)}, u32[]{:S(2)}, u32[]{:S(2)}) async-start(bf16[8,8,128,128]{3,1,2,0:T(8,128)(2,1)} %copy_select_fusion), calls=%async_computation.2 | async-start | bytes 4194304 | tf_op jit(solution)/shard_map/all_to_all | solution.py:81
  228.0 52.9 %all-to-all-start.3 = ((bf16[8,128,1536]{2,1,0:T(8,128)(2,1)}), bf16[8,128,1536]{2,1,0:T(8,128)(2,1)}, u32[]{:S(2)}, u32[]{:S(2)}) async-start(bf16[8,128,1536]{2,1,0:T(8,128)(2,1)} %select_select_fusion.2), calls=%async_computation.3 | async-start | bytes 6291456 | tf_op jit(solution)/shard_map/all_to_all | solution.py:80
  280.9 64.3 %all-to-all-start.4 = ((bf16[16,128,1024]{2,1,0:T(8,128)(2,1)}), bf16[16,128,1024]{2,1,0:T(8,128)(2,1)}, u32[]{:S(2)}, u32[]{:S(2)}) async-start(bf16[16,128,1024]{2,1,0:T(8,128)(2,1)} %select_select_fusion.1), calls=%async_computation.5 | async-start | bytes 8388608 | tf_op jit(solution)/shard_map/all_to_all | solution.py:87
  349.6 126.2 %all-to-all-start.5 = ((bf16[8,128,1024]{2,1,0:T(8,128)(2,1)}), bf16[8,128,1024]{2,1,0:T(8,128)(2,1)}, u32[]{:S(2)}, u32[]{:S(2)}) async-start(bf16[8,128,1024]{2,1,0:T(8,128)(2,1)} %select_select_fusion.3), calls=%async_computation.6 | async-start | bytes 4194304 | tf_op jit(solution)/shard_map/all_to_all | solution.py:90
  356.8 3.1 copy-start.1
  356.8 3.1 copy-start.2
  475.9 7.4 %copy-start.3 = (bf16[1024,512]{1,0:T(8,128)(2,1)S(1)}, bf16[1024,512]{1,0:T(8,128)(2,1)}, u32[]{:S(2)}) copy-start(bf16[1024,512]{1,0:T(8,128)(2,1)} %fusion.12) | copy-start | bytes 3145732
  482.3 1.0 copy-start.4
Sparse Core Ops, SparseCore 0:
  9.7 35.7 all-gather.1
  188.1 84.1 reduce-scatter.1

commit v9 on v8

--- a/solution.py
+++ b/solution.py
@@ -85,6 +85,7 @@
     fc_a = jnp.take(coef_b.reshape(dev_blocks, BLK, occ_width), sub_o, axis=0)
     fc_a = jnp.where(has_o[:, None, None], fc_a, jnp.zeros_like(fc_a))
     fc_a = lax.all_to_all(fc_a, "col", 0, 0, tiled=True)
+    fc_a, occ_b, rows_dom, tiles_dom = lax.optimization_barrier((fc_a, occ_b, rows_dom, tiles_dom))
     fc_b = jnp.take(fc_a, cset_jk, axis=0)
     fc_b = jnp.where(pres_jk[:, None, None], fc_b, jnp.zeros_like(fc_b))
     fc_dom = lax.all_to_all(fc_b, "row", 0, 0, tiled=True).reshape(dom_width, occ_width)

time: 497 us -> 495 us (level)
  waiting for transfers between devices: 206 us -> 168 us
  blocking collectives: 113 us -> 149 us
    all_to_all x1, waiting for transfers between devices: 52.7 us -> 0.01 us  [body(): fc_a = lax.all_to_all(fc_a, 'col', 0, 0, tiled=True)]
    psum x1, blocking collectives: 113 us -> 149 us  [body(): occ_b = lax.psum(occ_term, ('row', 'col')).astype(BF16)]
    all_to_all x1, waiting for transfers between devices: 0.01 us -> 16.3 us  [body(): lax.all_to_all(fc_b, 'row', 0, 0, tiled=True).reshape(dom_width, occ_width)]
    unnamed x15 -> x14, local copies, waits for them, and re-layouts: 14.1 us -> 15.3 us
where the time goes in v9:
time: 495 us; the launch traced here: 494 us
  waiting for transfers between devices  168 us (34%)
  blocking collectives  149 us (30%)
  local copies, waits for them, and re-layouts  53.2 us (11%)
  matrix products  45.6 us (9%)
  starting transfers between devices  37.4 us (8%)
  other arithmetic  26.5 us (5%)
  between operations  14.2 us (3%)
    psum x1, blocking collectives, body(): occ_b = lax.psum(occ_term, ('row', 'col')).astype(BF16)  149 us
    all_to_all x1, waiting for transfers between devices, body(): rows_a = lax.all_to_all(rows_a, 'col', 0, 0, tiled=True)  60.7 us
    reduce_scatter x1, waiting for transfers between devices, body(): coef_b = lax.psum_scatter(fock_lmo, 'col', scatter_dimension=0, tiled=True)  38 us
    all_to_all x1, waiting for transfers between devices, body(): tiles_a = lax.all_to_all(tiles_a, 'col', 0, 0, tiled=True)  35.9 us
    dot_general x1, matrix products, body(): jnp.dot(panel_fock, gathered, preferred_element_type=F32).astype(BF16)  23.4 us
    all_to_all x1, waiting for transfers between devices, body(): lax.all_to_all(tiles_b, 'row', 0, 0, tiled=True)  16.5 us
    all_to_all x1, waiting for transfers between devices, body(): lax.all_to_all(fc_b, 'row', 0, 0, tiled=True).reshape(dom_width, occ_width)  16.3 us
    unnamed x14, local copies, waits for them, and re-layouts  15.3 us
  transfers between devices with their start and end apart: 8, of which 5 were waited for; matrix products, arithmetic and copies ran while one was open for 22% of the time, Pallas kernels for 0%

profile of v9, /device:TPU:1, one launch (start us, length us, event | category | flops | bytes accessed | tf_op | source)
XLA Modules:
  0.0 494.1 jit_solution(17728688736289639713)
XLA Ops:
  12.4 3.6 gather_fusion.2
  16.0 6.2 %select_select_fusion = bf16[16,128,1536]{2,1,0:T(8,128)(2,1)} fusion(bf16[16,128,1536]{2,1,0:T(8,128)(2,1)} %gather_fusion.2, pred[16]{0:T(512)(128)(4,1)S(1)} %compare_and_fusion.3, pred[16]{0:T(512)(128)(4,1)S(1)} %get-tuple-element.26), kind=kLoop, calls=%fused_computation.10 | loop fusion | flops 6291456 | bytes 12582944 | tf_op jit(solution)/shard_map/jit(_where)/select_n | solution.py:53
  22.2 8.5 %all-to-all-start = ((bf16[16,128,1536]{2,1,0:T(8,128)(2,1)}), bf16[16,128,1536]{2,1,0:T(8,128)(2,1)}, u32[]{:S(2)}, u32[]{:S(2)}) async-start(bf16[16,128,1536]{2,1,0:T(8,128)(2,1)} %select_select_fusion), calls=%async_computation | async-start | bytes 12582912 | tf_op jit(solution)/shard_map/all_to_all | solution.py:54
  30.7 9.9 %copy.47 = bf16[512,8,16,128]{3,2,1,0:T(8,128)(2,1)S(1)} copy(bf16[512,8,16,128]{3,1,2,0:T(8,128)(2,1)} %bitcast.87) | data formatting | bytes 33554432
  40.7 8.1 %copy.36 = bf16[32,128,16,128]{3,1,2,0:T(8,128)(2,1)} copy(bf16[32,128,16,128]{3,2,1,0:T(8,128)(2,1)S(1)} %bitcast.83) | data formatting | bytes 33554432 | tf_op jit(solution)/shard_map/reshape;squeeze | solution.py:48
  49.1 8.9 %gather_fusion.1 = bf16[128,128,128]{2,1,0:T(8,128)(2,1)} fusion(bf16[32,128,16,128]{3,1,2,0:T(8,128)(2,1)} %copy.36, s32[128]{0:T(128)S(1)} %reshape.158), kind=kCustom, calls=%fused_computation.1 | custom fusion | bytes 8389632 | tf_op jit(solution)/shard_map/gather | solution.py:49
  58.0 4.5 broadcast_select_fusion
  62.5 60.7 %all-to-all-done = bf16[16,128,1536]{2,1,0:T(8,128)(2,1)} async-done(((bf16[16,128,1536]{2,1,0:T(8,128)(2,1)}), bf16[16,128,1536]{2,1,0:T(8,128)(2,1)}, u32[]{:S(2)}, u32[]{:S(2)}) %all-to-all-start) | async-done | bytes 6291488 | tf_op jit(solution)/shard_map/all_to_all | solution.py:54
  123.2 5.3 %all-to-all-start.1 = ((bf16[16,8,128,128]{3,2,1,0:T(8,128)(2,1)}), bf16[16,8,128,128]{3,2,1,0:T(8,128)(2,1)}, u32[]{:S(2)}, u32[]{:S(2)}) async-start(bf16[16,8,128,128]{3,2,1,0:T(8,128)(2,1)} %broadcast_select_fusion), calls=%async_computation.1 | async-start | bytes 8388608 | tf_op jit(solution)/shard_map/all_to_all | solution.py:56
  128.6 23.4 %fusion.2 = bf16[4096,1024]{1,0:T(8,128)(2,1)} fusion(bf16[2048,1024]{1,0:T(8,128)(2,1)} %all-gather.2.cloned.1.call-done, bf16[4096,1,2048]{2,0,1:T(8,128)(2,1)} %param.6), kind=kOutput, calls=%fused_computation.9 | convolution fusion | flops 17184063488 | bytes 29360128 | tf_op jit(solution)/shard_map/dot_general | solution.py:59
  152.1 35.9 %all-to-all-done.1 = bf16[16,8,128,128]{3,2,1,0:T(8,128)(2,1)} async-done(((bf16[16,8,128,128]{3,2,1,0:T(8,128)(2,1)}), bf16[16,8,128,128]{3,2,1,0:T(8,128)(2,1)}, u32[]{:S(2)}, u32[]{:S(2)}) %all-to-all-start.1) | async-done | bytes 4194336 | tf_op jit(solution)/shard_map/all_to_all | solution.py:56
  188.5 3.2 gather_fusion.5
  191.7 2.7 copy_select_fusion
  194.4 7.3 %all-to-all-start.4 = ((bf16[8,8,128,128]{3,1,2,0:T(8,128)(2,1)}), bf16[8,8,128,128]{3,1,2,0:T(8,128)(2,1)S(1)}, u32[]{:S(2)}, u32[]{:S(2)}) async-start(bf16[8,8,128,128]{3,1,2,0:T(8,128)(2,1)} %copy_select_fusion), calls=%async_computation.5 | async-start | bytes 4194304 | tf_op jit(solution)/shard_map/all_to_all | solution.py:81
  202.1 5.4 %gather_fusion.4 = bf16[8,128,1536]{2,1,0:T(8,128)(2,1)} fusion(bf16[16,128,1536]{2,1,0:T(8,128)(2,1)} %all-to-all-done, s32[1024]{0:T(1024)S(1)} %pad_clamp_fusion), kind=kCustom, calls=%fused_computation.4 | custom fusion | bytes 6291488 | tf_op jit(solution)/shard_map/jit(_take)/gather | solution.py:74
  207.5 4.1 select_select_fusion.2
  211.5 16.5 %all-to-all-done.4 = bf16[8,8,128,128]{3,1,2,0:T(8,128)(2,1)S(1)} async-done(((bf16[8,8,128,128]{3,1,2,0:T(8,128)(2,1)}), bf16[8,8,128,128]{3,1,2,0:T(8,128)(2,1)S(1)}, u32[]{:S(2)}, u32[]{:S(2)}) %all-to-all-start.4) | async-done | bytes 2097184 | tf_op jit(solution)/shard_map/all_to_all | solution.py:81
  229.3 5.2 %all-to-all-start.3 = ((bf16[8,128,1536]{2,1,0:T(8,128)(2,1)}), bf16[8,128,1536]{2,1,0:T(8,128)(2,1)}, u32[]{:S(2)}, u32[]{:S(2)}) async-start(bf16[8,128,1536]{2,1,0:T(8,128)(2,1)} %select_select_fusion.2), calls=%async_computation.4 | async-start | bytes 6291456 | tf_op jit(solution)/shard_map/all_to_all | solution.py:80
  234.5 38.0 %reduce-scatter.2.cloned.1.call-done = bf16[256,1024]{1,0:T(8,128)(2,1)} async-done(((bf16[4096,1024]{1,0:T(8,128)(2,1)}), bf16[256,1024]{1,0:T(8,128)(2,1)}) %reduce-scatter.2.cloned.1.call-update) | async-done | bytes 524304 | tf_op jit(solution)/shard_map/reduce_scatter | solution.py:61
  272.5 3.8 gather_fusion.3
  276.4 4.7 select_select_fusion.1
  281.0 5.0 %all-to-all-start.2 = ((bf16[16,128,1024]{2,1,0:T(8,128)(2,1)}), bf16[16,128,1024]{2,1,0:T(8,128)(2,1)}, u32[]{:S(2)}, u32[]{:S(2)}) async-start(bf16[16,128,1024]{2,1,0:T(8,128)(2,1)} %select_select_fusion.1), calls=%async_computation.3 | async-start | bytes 8388608 | tf_op jit(solution)/shard_map/all_to_all | solution.py:87
  286.1 2.7 convolution_bitcast_fusion
  288.8 149.1 %all-reduce.1 = bf16[1024,1024]{0,1:T(8,128)(2,1)} all-reduce(f32[1024,1024]{0,1:T(8,128)} %convolution_bitcast_fusion), channel_id=1, replica_groups=mesh['row'=8,'col'=16] {'row','col'}, use_global_device_ids=true, to_apply=%region_5.6 | all-reduce | flops 1048576 | bytes 6291456 | tf_op jit(solution)/shard_map/psum | solution.py:68
  437.9 2.9 gather_fusion.6
  442.4 5.9 %all-to-all-start.5 = ((bf16[8,128,1024]{2,1,0:T(8,128)(2,1)}), bf16[8,128,1024]{2,1,0:T(8,128)(2,1)}, u32[]{:S(2)}, u32[]{:S(2)}) async-start(bf16[8,128,1024]{2,1,0:T(8,128)(2,1)} %select_select_fusion.3), calls=%async_computation.6 | async-start | bytes 4194304 | tf_op jit(solution)/shard_map/all_to_all | solution.py:91
  451.2 2.9 fusion.11
  454.1 4.3 convolution_bitcast_fusion.1
  458.4 16.3 %all-to-all-done.5 = bf16[8,128,1024]{2,1,0:T(8,128)(2,1)} async-done(((bf16[8,128,1024]{2,1,0:T(8,128)(2,1)}), bf16[8,128,1024]{2,1,0:T(8,128)(2,1)}, u32[]{:S(2)}, u32[]{:S(2)}) %all-to-all-start.5) | async-done | bytes 2097184 | tf_op jit(solution)/shard_map/all_to_all | solution.py:91
  474.7 6.3 %convolution_convert_fusion = bf16[1024,512]{1,0:T(8,128)(2,1)S(1)} fusion(bf16[1,1,1024,512]{3,2,1,0:T(8,128)(2,1)S(1)} %copy-done, bf16[1024,1024]{1,0:T(8,128)(2,1)} %bitcast.28, bf16[1024,1024]{0,1:T(8,128)(2,1)} %all-reduce.1, bf16[1024,1536]{1,0:T(8,128)(2,1)} %bitcast.13), kind=kOutput, calls=%fused_computation.26 | convolution fusion | flops 3225944064 | bytes 8388608 | tf_op jit(solution)/shard_map/xm,xi->mi/dot_general | solution.py:104
  482.0 2.0 convolution_subtract_fusion.1
  484.0 2.0 fusion.16
  (52 shorter events, 14.6 us)
Async XLA Ops:
  7.2 441.1 %copy-start = (bf16[1,1,1024,512]{3,2,1,0:T(8,128)(2,1)S(1)}, bf16[1,1,1024,512]{3,2,1,0:T(8,128)(2,1)}, u32[]{:S(2)}) copy-start(bf16[1,1,1024,512]{3,2,1,0:T(8,128)(2,1)} %param.9) | copy-start | bytes 3145732
  7.2 121.5 %all-gather.2.cloned.1.call-start = ((), (), s32[]{:S(2)}) async-start(), calls=%async_computation.7 | async-start | bytes 4718592 | tf_op jit(solution)/shard_map/all_gather | solution.py:58
  22.2 101.0 %all-to-all-start = ((bf16[16,128,1536]{2,1,0:T(8,128)(2,1)}), bf16[16,128,1536]{2,1,0:T(8,128)(2,1)}, u32[]{:S(2)}, u32[]{:S(2)}) async-start(bf16[16,128,1536]{2,1,0:T(8,128)(2,1)} %select_select_fusion), calls=%async_computation | async-start | bytes 12582912 | tf_op jit(solution)/shard_map/all_to_all | solution.py:54
  123.2 64.7 %all-to-all-start.1 = ((bf16[16,8,128,128]{3,2,1,0:T(8,128)(2,1)}), bf16[16,8,128,128]{3,2,1,0:T(8,128)(2,1)}, u32[]{:S(2)}, u32[]{:S(2)}) async-start(bf16[16,8,128,128]{3,2,1,0:T(8,128)(2,1)} %broadcast_select_fusion), calls=%async_computation.1 | async-start | bytes 8388608 | tf_op jit(solution)/shard_map/all_to_all | solution.py:56
  128.6 144.0 %reduce-scatter.2.cloned.1.call-start = ((), (), s32[]{:S(2)}) async-start(), calls=%async_computation.8 | async-start | bytes 8912896 | tf_op jit(solution)/shard_map/reduce_scatter | solution.py:61
  194.4 33.7 %all-to-all-start.4 = ((bf16[8,8,128,128]{3,1,2,0:T(8,128)(2,1)}), bf16[8,8,128,128]{3,1,2,0:T(8,128)(2,1)S(1)}, u32[]{:S(2)}, u32[]{:S(2)}) async-start(bf16[8,8,128,128]{3,1,2,0:T(8,128)(2,1)} %copy_select_fusion), calls=%async_computation.5 | async-start | bytes 4194304 | tf_op jit(solution)/shard_map/all_to_all | solution.py:81
  228.0 1.3 copy-start.4
  229.3 51.7 %all-to-all-start.3 = ((bf16[8,128,1536]{2,1,0:T(8,128)(2,1)}), bf16[8,128,1536]{2,1,0:T(8,128)(2,1)}, u32[]{:S(2)}, u32[]{:S(2)}) async-start(bf16[8,128,1536]{2,1,0:T(8,128)(2,1)} %select_select_fusion.2), calls=%async_computation.4 | async-start | bytes 6291456 | tf_op jit(solution)/shard_map/all_to_all | solution.py:80
  281.0 5.0 %copy-start.1 = (bf16[256,1024]{1,0:T(8,128)(2,1)S(1)}, bf16[256,1024]{1,0:T(8,128)(2,1)}, u32[]{:S(2)}) copy-start(bf16[256,1024]{1,0:T(8,128)(2,1)} %reduce-scatter.2.cloned.1.call-done) | copy-start | bytes 1572868
  281.0 5.0 %copy-start.2 = (bf16[256,1024]{1,0:T(8,128)(2,1)S(1)}, bf16[256,1024]{1,0:T(8,128)(2,1)}, u32[]{:S(2)}) copy-start(bf16[256,1024]{1,0:T(8,128)(2,1)} %param.7) | copy-start | bytes 1572868
  281.0 156.9 %all-to-all-start.2 = ((bf16[16,128,1024]{2,1,0:T(8,128)(2,1)}), bf16[16,128,1024]{2,1,0:T(8,128)(2,1)}, u32[]{:S(2)}, u32[]{:S(2)}) async-start(bf16[16,128,1024]{2,1,0:T(8,128)(2,1)} %select_select_fusion.1), calls=%async_computation.3 | async-start | bytes 8388608 | tf_op jit(solution)/shard_map/all_to_all | solution.py:87
  442.4 32.3 %all-to-all-start.5 = ((bf16[8,128,1024]{2,1,0:T(8,128)(2,1)}), bf16[8,128,1024]{2,1,0:T(8,128)(2,1)}, u32[]{:S(2)}, u32[]{:S(2)}) async-start(bf16[8,128,1024]{2,1,0:T(8,128)(2,1)} %select_select_fusion.3), calls=%async_computation.6 | async-start | bytes 4194304 | tf_op jit(solution)/shard_map/all_to_all | solution.py:91
  481.0 1.0 copy-start.3
Sparse Core Ops, SparseCore 0:
  9.7 35.7 all-gather.1
  188.1 84.3 reduce-scatter.1

commit v10 on v8

--- a/solution.py
+++ b/solution.py
@@ -82,12 +82,25 @@
     )
     rows_dom = rows_dom.reshape(dom_width, -1)
 
-    fc_a = jnp.take(coef_b.reshape(dev_blocks, BLK, occ_width), sub_o, axis=0)
-    fc_a = jnp.where(has_o[:, None, None], fc_a, jnp.zeros_like(fc_a))
-    fc_a = lax.all_to_all(fc_a, "col", 0, 0, tiled=True)
-    fc_b = jnp.take(fc_a, cset_jk, axis=0)
-    fc_b = jnp.where(pres_jk[:, None, None], fc_b, jnp.zeros_like(fc_b))
-    fc_dom = lax.all_to_all(fc_b, "row", 0, 0, tiled=True).reshape(dom_width, occ_width)
+    mine_j = mine_k.T
+    has_j = jnp.any(mine_j, axis=1)
+    sub_j = pick(mine_j, sub_k.T)
+    fc_1 = jnp.take(coef_b.reshape(dev_blocks, BLK, occ_width), sub_j, axis=0)
+    fc_1 = jnp.where(has_j[:, None, None], fc_1, jnp.zeros_like(fc_1))
+    fc_1 = lax.all_to_all(fc_1, "row", 0, 0, tiled=True)
+    pres_j = lax.dynamic_index_in_dim(present, my_row, 1, keepdims=False)
+    cset_j = lax.dynamic_index_in_dim(cset, my_row, 1, keepdims=False)
+    mine_o = pres_j & (cset_j == my_col)
+    has_ok = jnp.any(mine_o, axis=1)
+    k_of_o = pick(mine_o, jnp.broadcast_to(jnp.arange(dom_blocks, dtype=jnp.int32), mine_o.shape))
+    fc_2 = jnp.take(fc_1, k_of_o, axis=0)
+    fc_2 = jnp.where(has_ok[:, None, None], fc_2, jnp.zeros_like(fc_2))
+    fc_2 = lax.all_to_all(fc_2, "col", 0, 0, tiled=True)
+    fc_2, occ_b, rows_dom, tiles_dom = lax.optimization_barrier((fc_2, occ_b, rows_dom, tiles_dom))
+    pres_me = lax.dynamic_index_in_dim(pres_o, my_row, 0, keepdims=False)
+    cset_me = lax.dynamic_index_in_dim(cset_o, my_row, 0, keepdims=False)
+    fc_dom = jnp.take(fc_2, cset_me, axis=0)
+    fc_dom = jnp.where(pres_me[:, None, None], fc_dom, jnp.zeros_like(fc_dom)).reshape(dom_width, occ_width)
 
     coef_dom = rows_dom[:, :occ_width]
     three_dom = rows_dom[:, occ_width:]

time: 497 us -> 549 us (1.10)
  blocking collectives: 113 us -> 151 us
  waiting for transfers between devices: 206 us -> 215 us
    psum x1, blocking collectives: 113 us -> 151 us  [body(): occ_b = lax.psum(occ_term, ('row', 'col')).astype(BF16)]
    all_to_all x2, waiting for transfers between devices: 52.7 us -> 16.5 us  [the longest x1 16.5 us: body(): fc_1 = lax.all_to_all(fc_1, 'row', 0, 0, tiled=True)]
    reduce_scatter x1, waiting for transfers between devices: 39.1 us -> 70.8 us  [body(): coef_b = lax.psum_scatter(fock_lmo, 'col', scatter_dimension=0, tiled=True)]
    all_to_all x1, waiting for transfers between devices: 0.01 us -> 30.1 us  [body(): lax.all_to_all(rows_b, 'row', 0, 0, tiled=True)]
    all_to_all x1, waiting for transfers between devices: 16.5 us -> 0.01 us  [body(): lax.all_to_all(tiles_b, 'row', 0, 0, tiled=True)]
    unnamed x15 -> x14, local copies, waits for them, and re-layouts: 14.1 us -> 15 us
  transfers between devices with their start and end apart: 8 -> 8, of which waited for: 5 -> 5; matrix products, arithmetic and copies ran while one was open for 22% -> 18% of each run, Pallas kernels for 0% -> 0%
where the time goes in v10:
time: 549 us; the launch traced here: 548 us
  waiting for transfers between devices  215 us (39%)
  blocking collectives  151 us (28%)
  local copies, waits for them, and re-layouts  54.4 us (10%)
  matrix products  47.5 us (9%)
  starting transfers between devices  37.5 us (7%)
  other arithmetic  28.9 us (5%)
  between operations  14.3 us (3%)
    psum x1, blocking collectives, body(): occ_b = lax.psum(occ_term, ('row', 'col')).astype(BF16)  151 us
    reduce_scatter x1, waiting for transfers between devices, body(): coef_b = lax.psum_scatter(fock_lmo, 'col', scatter_dimension=0, tiled=True)  70.8 us
    all_to_all x1, waiting for transfers between devices, body(): rows_a = lax.all_to_all(rows_a, 'col', 0, 0, tiled=True)  60.6 us
    all_to_all x1, waiting for transfers between devices, body(): tiles_a = lax.all_to_all(tiles_a, 'col', 0, 0, tiled=True)  35.8 us
    all_to_all x1, waiting for transfers between devices, body(): lax.all_to_all(rows_b, 'row', 0, 0, tiled=True)  30.1 us
    dot_general x1, matrix products, body(): jnp.dot(panel_fock, gathered, preferred_element_type=F32).astype(BF16)  23.4 us
    all_to_all x1, waiting for transfers between devices, body(): fc_1 = lax.all_to_all(fc_1, 'row', 0, 0, tiled=True)  16.5 us
    unnamed x14, local copies, waits for them, and re-layouts  15 us
  transfers between devices with their start and end apart: 8, of which 5 were waited for; matrix products, arithmetic and copies ran while one was open for 18% of the time, Pallas kernels for 0%

profile of v10, /device:TPU:1, one launch (start us, length us, event | category | flops | bytes accessed | tf_op | source)
XLA Modules:
  0.0 547.9 jit_solution(2671595339909369215)
XLA Ops:
  12.6 3.6 gather_fusion.2
  16.3 6.2 %select_select_fusion = bf16[16,128,1536]{2,1,0:T(8,128)(2,1)} fusion(bf16[16,128,1536]{2,1,0:T(8,128)(2,1)} %gather_fusion.2, pred[16]{0:T(512)(128)(4,1)S(1)} %compare_and_fusion.4, pred[16]{0:T(512)(128)(4,1)S(1)} %get-tuple-element.29), kind=kLoop, calls=%fused_computation.11 | loop fusion | flops 6291456 | bytes 12582944 | tf_op jit(solution)/shard_map/jit(_where)/select_n | solution.py:53
  22.5 8.5 %all-to-all-start = ((bf16[16,128,1536]{2,1,0:T(8,128)(2,1)}), bf16[16,128,1536]{2,1,0:T(8,128)(2,1)}, u32[]{:S(2)}, u32[]{:S(2)}) async-start(bf16[16,128,1536]{2,1,0:T(8,128)(2,1)} %select_select_fusion), calls=%async_computation | async-start | bytes 12582912 | tf_op jit(solution)/shard_map/all_to_all | solution.py:54
  31.0 9.8 %copy.52 = bf16[512,8,16,128]{3,2,1,0:T(8,128)(2,1)S(1)} copy(bf16[512,8,16,128]{3,1,2,0:T(8,128)(2,1)} %bitcast.106) | data formatting | bytes 33554432
  40.8 8.2 %copy.41 = bf16[32,128,16,128]{3,1,2,0:T(8,128)(2,1)} copy(bf16[32,128,16,128]{3,2,1,0:T(8,128)(2,1)S(1)} %bitcast.102) | data formatting | bytes 33554432 | tf_op jit(solution)/shard_map/reshape;squeeze | solution.py:48
  49.3 8.9 %gather_fusion.1 = bf16[128,128,128]{2,1,0:T(8,128)(2,1)} fusion(bf16[32,128,16,128]{3,1,2,0:T(8,128)(2,1)} %copy.41, s32[128]{0:T(128)S(1)} %reshape.239), kind=kCustom, calls=%fused_computation.1 | custom fusion | bytes 8389632 | tf_op jit(solution)/shard_map/gather | solution.py:49
  58.2 4.5 broadcast_select_fusion
  62.7 60.6 %all-to-all-done = bf16[16,128,1536]{2,1,0:T(8,128)(2,1)} async-done(((bf16[16,128,1536]{2,1,0:T(8,128)(2,1)}), bf16[16,128,1536]{2,1,0:T(8,128)(2,1)}, u32[]{:S(2)}, u32[]{:S(2)}) %all-to-all-start) | async-done | bytes 6291488 | tf_op jit(solution)/shard_map/all_to_all | solution.py:54
  123.3 5.4 all-to-all-start.1
  128.8 23.4 %fusion.2 = bf16[4096,1024]{1,0:T(8,128)(2,1)} fusion(bf16[2048,1024]{1,0:T(8,128)(2,1)} %all-gather.2.cloned.1.call-done, bf16[4096,1,2048]{2,0,1:T(8,128)(2,1)} %param.6), kind=kOutput, calls=%fused_computation.10 | convolution fusion | flops 17184063488 | bytes 29360128 | tf_op jit(solution)/shard_map/dot_general | solution.py:59
  152.2 35.8 %all-to-all-done.1 = bf16[16,8,128,128]{3,2,1,0:T(8,128)(2,1)} async-done(((bf16[16,8,128,128]{3,2,1,0:T(8,128)(2,1)}), bf16[16,8,128,128]{3,2,1,0:T(8,128)(2,1)}, u32[]{:S(2)}, u32[]{:S(2)}) %all-to-all-start.1) | async-done | bytes 4194336 | tf_op jit(solution)/shard_map/all_to_all | solution.py:56
  188.8 3.2 gather_fusion.6
  191.9 2.7 copy_select_fusion
  194.7 7.3 %all-to-all-start.5 = ((bf16[8,8,128,128]{3,1,2,0:T(8,128)(2,1)}), bf16[8,8,128,128]{3,1,2,0:T(8,128)(2,1)}, u32[]{:S(2)}, u32[]{:S(2)}) async-start(bf16[8,8,128,128]{3,1,2,0:T(8,128)(2,1)} %copy_select_fusion), calls=%async_computation.6 | async-start | bytes 4194304 | tf_op jit(solution)/shard_map/all_to_all | solution.py:81
  202.0 70.8 %reduce-scatter.2.cloned.1.call-done = bf16[256,1024]{1,0:T(8,128)(2,1)} async-done(((bf16[4096,1024]{1,0:T(8,128)(2,1)}), bf16[256,1024]{1,0:T(8,128)(2,1)}) %reduce-scatter.2.cloned.1.call-update) | async-done | bytes 524304 | tf_op jit(solution)/shard_map/reduce_scatter | solution.py:61
  276.2 6.2 %all-to-all-start.2 = ((bf16[8,128,1024]{2,1,0:T(8,128)(2,1)}), bf16[8,128,1024]{2,1,0:T(8,128)(2,1)S(1)}, u32[]{:S(2)}, u32[]{:S(2)}) async-start(bf16[8,128,1024]{2,1,0:T(8,128)(2,1)} %select_select_fusion.3), calls=%async_computation.3 | async-start | bytes 4194304 | tf_op jit(solution)/shard_map/all_to_all | solution.py:90
  283.1 5.2 gather_fusion.5
  288.3 4.0 select_select_fusion.2
  292.2 16.5 %all-to-all-done.2 = bf16[8,128,1024]{2,1,0:T(8,128)(2,1)S(1)} async-done(((bf16[8,128,1024]{2,1,0:T(8,128)(2,1)}), bf16[8,128,1024]{2,1,0:T(8,128)(2,1)S(1)}, u32[]{:S(2)}, u32[]{:S(2)}) %all-to-all-start.2) | async-done | bytes 2097184 | tf_op jit(solution)/shard_map/all_to_all | solution.py:90
  308.8 5.2 all-to-all-start.4
  314.1 2.8 gather_fusion.4
  316.8 4.7 select_select_fusion.1
  321.5 30.1 %all-to-all-done.4 = bf16[8,128,1536]{2,1,0:T(8,128)(2,1)} async-done(((bf16[8,128,1536]{2,1,0:T(8,128)(2,1)}), bf16[8,128,1536]{2,1,0:T(8,128)(2,1)}, u32[]{:S(2)}, u32[]{:S(2)}) %all-to-all-start.4) | async-done | bytes 3145760 | tf_op jit(solution)/shard_map/all_to_all | solution.py:80
  351.7 4.7 all-to-all-start.3
  357.0 2.7 convolution_bitcast_fusion
  359.7 150.8 %all-reduce.1 = bf16[1024,1024]{0,1:T(8,128)(2,1)} all-reduce(f32[1024,1024]{0,1:T(8,128)} %convolution_bitcast_fusion), channel_id=1, replica_groups=mesh['row'=8,'col'=16] {'row','col'}, use_global_device_ids=true, to_apply=%region_9.10 | all-reduce | flops 1048576 | bytes 6291456 | tf_op jit(solution)/shard_map/psum | solution.py:68
  510.5 3.9 fusion.11
  514.4 2.7 fusion.17
  517.2 4.3 convolution_bitcast_fusion.1
  521.5 2.9 gather_fusion.7
  526.4 6.4 %convolution_convert_fusion = bf16[1024,512]{1,0:T(8,128)(2,1)S(1)} fusion(bf16[1,1,1024,512]{3,2,1,0:T(8,128)(2,1)S(1)} %copy-done, bf16[1024,1024]{1,0:T(8,128)(2,1)} %fusion.5, bf16[1024,1024]{0,1:T(8,128)(2,1)} %all-reduce.1, bf16[1024,1536]{1,0:T(8,128)(2,1)} %bitcast.19), kind=kOutput, calls=%fused_computation.28 | convolution fusion | flops 3225944064 | bytes 8388608 | tf_op jit(solution)/shard_map/xm,xi->mi/dot_general | solution.py:116
  539.0 2.0 copy.47
  (69 shorter events, 19.3 us)
Async XLA Ops:
  7.2 503.3 %copy-start = (bf16[1,1,1024,512]{3,2,1,0:T(8,128)(2,1)S(1)}, bf16[1,1,1024,512]{3,2,1,0:T(8,128)(2,1)}, u32[]{:S(2)}) copy-start(bf16[1,1,1024,512]{3,2,1,0:T(8,128)(2,1)} %param.9) | copy-start | bytes 3145732
  7.2 121.6 %all-gather.2.cloned.1.call-start = ((), (), s32[]{:S(2)}) async-start(), calls=%async_computation.7 | async-start | bytes 4718592 | tf_op jit(solution)/shard_map/all_gather | solution.py:58
  22.5 100.9 %all-to-all-start = ((bf16[16,128,1536]{2,1,0:T(8,128)(2,1)}), bf16[16,128,1536]{2,1,0:T(8,128)(2,1)}, u32[]{:S(2)}, u32[]{:S(2)}) async-start(bf16[16,128,1536]{2,1,0:T(8,128)(2,1)} %select_select_fusion), calls=%async_computation | async-start | bytes 12582912 | tf_op jit(solution)/shard_map/all_to_all | solution.py:54
  123.3 64.7 %all-to-all-start.1 = ((bf16[16,8,128,128]{3,2,1,0:T(8,128)(2,1)}), bf16[16,8,128,128]{3,2,1,0:T(8,128)(2,1)}, u32[]{:S(2)}, u32[]{:S(2)}) async-start(bf16[16,8,128,128]{3,2,1,0:T(8,128)(2,1)} %broadcast_select_fusion), calls=%async_computation.1 | async-start | bytes 8388608 | tf_op jit(solution)/shard_map/all_to_all | solution.py:56
  128.7 144.0 %reduce-scatter.2.cloned.1.call-start = ((), (), s32[]{:S(2)}) async-start(), calls=%async_computation.8 | async-start | bytes 8912896 | tf_op jit(solution)/shard_map/reduce_scatter | solution.py:61
  194.7 81.5 %all-to-all-start.5 = ((bf16[8,8,128,128]{3,1,2,0:T(8,128)(2,1)}), bf16[8,8,128,128]{3,1,2,0:T(8,128)(2,1)}, u32[]{:S(2)}, u32[]{:S(2)}) async-start(bf16[8,8,128,128]{3,1,2,0:T(8,128)(2,1)} %copy_select_fusion), calls=%async_computation.6 | async-start | bytes 4194304 | tf_op jit(solution)/shard_map/all_to_all | solution.py:81
  276.2 32.6 %all-to-all-start.2 = ((bf16[8,128,1024]{2,1,0:T(8,128)(2,1)}), bf16[8,128,1024]{2,1,0:T(8,128)(2,1)S(1)}, u32[]{:S(2)}, u32[]{:S(2)}) async-start(bf16[8,128,1024]{2,1,0:T(8,128)(2,1)} %select_select_fusion.3), calls=%async_computation.3 | async-start | bytes 4194304 | tf_op jit(solution)/shard_map/all_to_all | solution.py:90
  308.8 42.9 %all-to-all-start.4 = ((bf16[8,128,1536]{2,1,0:T(8,128)(2,1)}), bf16[8,128,1536]{2,1,0:T(8,128)(2,1)}, u32[]{:S(2)}, u32[]{:S(2)}) async-start(bf16[8,128,1536]{2,1,0:T(8,128)(2,1)} %select_select_fusion.2), calls=%async_computation.5 | async-start | bytes 6291456 | tf_op jit(solution)/shard_map/all_to_all | solution.py:80
  321.5 35.4 %copy-start.1 = (bf16[256,1024]{1,0:T(8,128)(2,1)S(1)}, bf16[256,1024]{1,0:T(8,128)(2,1)}, u32[]{:S(2)}) copy-start(bf16[256,1024]{1,0:T(8,128)(2,1)} %reduce-scatter.2.cloned.1.call-done) | copy-start | bytes 1572868
  321.5 35.4 %copy-start.2 = (bf16[256,1024]{1,0:T(8,128)(2,1)S(1)}, bf16[256,1024]{1,0:T(8,128)(2,1)}, u32[]{:S(2)}) copy-start(bf16[256,1024]{1,0:T(8,128)(2,1)} %param.7) | copy-start | bytes 1572868
  351.7 158.8 %all-to-all-start.3 = ((bf16[16,128,1024]{2,1,0:T(8,128)(2,1)}), bf16[16,128,1024]{2,1,0:T(8,128)(2,1)}, u32[]{:S(2)}, u32[]{:S(2)}) async-start(bf16[16,128,1024]{2,1,0:T(8,128)(2,1)} %select_select_fusion.1), calls=%async_computation.4 | async-start | bytes 8388608 | tf_op jit(solution)/shard_map/all_to_all | solution.py:98
  526.4 7.4 %copy-start.3 = (bf16[1024,512]{1,0:T(8,128)(2,1)S(1)}, bf16[1024,512]{1,0:T(8,128)(2,1)}, u32[]{:S(2)}) copy-start(bf16[1024,512]{1,0:T(8,128)(2,1)} %fusion.11) | copy-start | bytes 3145732
  532.8 1.0 copy-start.4
Sparse Core Ops, SparseCore 0:
  9.7 35.7 all-gather.1
  188.2 84.5 reduce-scatter.1

commit v11 on v9

--- a/solution.py
+++ b/solution.py
@@ -40,17 +40,13 @@
     sub_k = lax.dynamic_index_in_dim(sub, my_row, 2, keepdims=False)
     rtile_k = lax.dynamic_index_in_dim(row_tile, my_row, 2, keepdims=False)
     mine_k = pres_k & (cset_k == my_col)
-    has_o = jnp.any(mine_k, axis=1)
     sub_o = pick(mine_k, sub_k)
     mine2 = present & (cset == my_col)
     ct = pick(mine2, col_tile)
-    ok_tile = jnp.any(mine2, axis=2) & pres_k
     fock_tiles = panel_fock.reshape(panel_blocks, BLK, col_blocks, BLK)
     tiles_a = fock_tiles[rtile_k, :, ct, :]
-    tiles_a = jnp.where(ok_tile[:, :, None, None], tiles_a, jnp.zeros_like(tiles_a))
     in_rows = jnp.concatenate([lmo_coef, three_index], axis=1).reshape(dev_blocks, BLK, -1)
     rows_a = jnp.take(in_rows, sub_o, axis=0)
-    rows_a = jnp.where(has_o[:, None, None], rows_a, jnp.zeros_like(rows_a))
     rows_a = lax.all_to_all(rows_a, "col", 0, 0, tiled=True)
     tiles_a, rows_a = lax.optimization_barrier((tiles_a, rows_a))
     tiles_a = lax.all_to_all(tiles_a, "col", 0, 0, tiled=True)
@@ -75,7 +71,8 @@
     rows_b = jnp.where(pres_jk[:, None, None], rows_b, jnp.zeros_like(rows_b))
     slot_ids = jnp.broadcast_to(jnp.arange(dom_blocks, dtype=jnp.int32)[:, None], cset_o.shape)
     tiles_b = tiles_a[cset_o, slot_ids]
-    tiles_b = jnp.where(pres_o[:, :, None, None], tiles_b, jnp.zeros_like(tiles_b))
+    live_b = pres_o & pres_jk[:, None]
+    tiles_b = jnp.where(live_b[:, :, None, None], tiles_b, jnp.zeros_like(tiles_b))
     rows_dom, tiles_dom = (
         lax.all_to_all(rows_b, "row", 0, 0, tiled=True),
         lax.all_to_all(tiles_b, "row", 0, 0, tiled=True),
@@ -83,7 +80,6 @@
     rows_dom = rows_dom.reshape(dom_width, -1)
 
     fc_a = jnp.take(coef_b.reshape(dev_blocks, BLK, occ_width), sub_o, axis=0)
-    fc_a = jnp.where(has_o[:, None, None], fc_a, jnp.zeros_like(fc_a))
     fc_a = lax.all_to_all(fc_a, "col", 0, 0, tiled=True)
     fc_a, occ_b, rows_dom, tiles_dom = lax.optimization_barrier((fc_a, occ_b, rows_dom, tiles_dom))
     fc_b = jnp.take(fc_a, cset_jk, axis=0)

time: 495 us -> 495 us (level)
    select_n x5 -> x3, other arithmetic: 18.1 us -> 8.86 us  [the longest x1 6.08 us: body(): rows_a = jnp.take(in_rows, sub_o, axis=0)]
  transfers between devices with their start and end apart: 8 -> 8, of which waited for: 5 -> 5; matrix products, arithmetic and copies ran while one was open for 22% -> 21% of each run, Pallas kernels for 0% -> 0%
where the time goes in v11:
time: 495 us; the launch traced here: 494 us
  waiting for transfers between devices  172 us (35%)
  blocking collectives  148 us (30%)
  local copies, waits for them, and re-layouts  53.1 us (11%)
  matrix products  45.6 us (9%)
  starting transfers between devices  38.7 us (8%)
  other arithmetic  21.9 us (4%)
  between operations  14.2 us (3%)
    psum x1, blocking collectives, body(): occ_b = lax.psum(occ_term, ('row', 'col')).astype(BF16)  148 us
    all_to_all x1, waiting for transfers between devices, body(): rows_a = lax.all_to_all(rows_a, 'col', 0, 0, tiled=True)  65.2 us
    reduce_scatter x1, waiting for transfers between devices, body(): coef_b = lax.psum_scatter(fock_lmo, 'col', scatter_dimension=0, tiled=True)  37.6 us
    all_to_all x1, waiting for transfers between devices, body(): tiles_a = lax.all_to_all(tiles_a, 'col', 0, 0, tiled=True)  35.8 us
    dot_general x1, matrix products, body(): jnp.dot(panel_fock, gathered, preferred_element_type=F32).astype(BF16)  23.4 us
    all_to_all x1, waiting for transfers between devices, body(): lax.all_to_all(tiles_b, 'row', 0, 0, tiled=True)  16.7 us
    all_to_all x1, waiting for transfers between devices, body(): lax.all_to_all(fc_b, 'row', 0, 0, tiled=True).reshape(dom_width, occ_width)  16.3 us
    unnamed x14, local copies, waits for them, and re-layouts  15.3 us
  transfers between devices with their start and end apart: 8, of which 5 were waited for; matrix products, arithmetic and copies ran while one was open for 21% of the time, Pallas kernels for 0%

profile of v11, /device:TPU:1, one launch (start us, length us, event | category | flops | bytes accessed | tf_op | source)
XLA Modules:
  0.0 494.1 jit_solution(17007065397134510473)
XLA Ops:
  12.3 3.6 gather_fusion.2
  15.9 6.1 %broadcast_select_fusion = bf16[16,128,1536]{2,1,0:T(8,128)(2,1)} fusion(bf16[16,128,1536]{2,1,0:T(8,128)(2,1)} %gather_fusion.2, pred[16]{0:T(512)(128)(4,1)S(1)} %compare_and_fusion.2), kind=kLoop, calls=%fused_computation.10 | loop fusion | flops 3145728 | bytes 12582928 | tf_op jit(solution)/shard_map/jit(_take)/select_n | solution.py:49
  22.0 8.5 %all-to-all-start = ((bf16[16,128,1536]{2,1,0:T(8,128)(2,1)}), bf16[16,128,1536]{2,1,0:T(8,128)(2,1)}, u32[]{:S(2)}, u32[]{:S(2)}) async-start(bf16[16,128,1536]{2,1,0:T(8,128)(2,1)} %broadcast_select_fusion), calls=%async_computation | async-start | bytes 12582912 | tf_op jit(solution)/shard_map/all_to_all | solution.py:50
  30.6 9.9 %copy.44 = bf16[512,8,16,128]{3,2,1,0:T(8,128)(2,1)S(1)} copy(bf16[512,8,16,128]{3,1,2,0:T(8,128)(2,1)} %bitcast.76) | data formatting | bytes 33554432
  40.5 8.2 %copy.33 = bf16[32,128,16,128]{3,1,2,0:T(8,128)(2,1)} copy(bf16[32,128,16,128]{3,2,1,0:T(8,128)(2,1)S(1)} %bitcast.73) | data formatting | bytes 33554432 | tf_op jit(solution)/shard_map/reshape;squeeze | solution.py:46
  48.8 9.0 %gather_fusion.1 = bf16[128,128,128]{2,1,0:T(8,128)(2,1)} fusion(bf16[32,128,16,128]{3,1,2,0:T(8,128)(2,1)} %copy.33, s32[128]{0:T(128)S(1)} %reshape.174), kind=kCustom, calls=%fused_computation.1 | custom fusion | bytes 8389632 | tf_op jit(solution)/shard_map/gather | solution.py:47
  57.7 65.2 %all-to-all-done = bf16[16,128,1536]{2,1,0:T(8,128)(2,1)} async-done(((bf16[16,128,1536]{2,1,0:T(8,128)(2,1)}), bf16[16,128,1536]{2,1,0:T(8,128)(2,1)}, u32[]{:S(2)}, u32[]{:S(2)}) %all-to-all-start) | async-done | bytes 6291488 | tf_op jit(solution)/shard_map/all_to_all | solution.py:50
  122.9 5.4 %all-to-all-start.1 = ((bf16[16,8,128,128]{3,2,1,0:T(8,128)(2,1)}), bf16[16,8,128,128]{3,2,1,0:T(8,128)(2,1)}, u32[]{:S(2)}, u32[]{:S(2)}) async-start(bf16[16,8,128,128]{3,2,1,0:T(8,128)(2,1)} %bitcast.77), calls=%async_computation.1 | async-start | bytes 8388608 | tf_op jit(solution)/shard_map/all_to_all | solution.py:52
  128.4 23.4 %fusion.2 = bf16[4096,1024]{1,0:T(8,128)(2,1)} fusion(bf16[2048,1024]{1,0:T(8,128)(2,1)} %all-gather.2.cloned.1.call-done, bf16[4096,1,2048]{2,0,1:T(8,128)(2,1)} %param.6), kind=kOutput, calls=%fused_computation.9 | convolution fusion | flops 17184063488 | bytes 29360128 | tf_op jit(solution)/shard_map/dot_general | solution.py:55
  151.9 35.8 %all-to-all-done.1 = bf16[16,8,128,128]{3,2,1,0:T(8,128)(2,1)} async-done(((bf16[16,8,128,128]{3,2,1,0:T(8,128)(2,1)}), bf16[16,8,128,128]{3,2,1,0:T(8,128)(2,1)}, u32[]{:S(2)}, u32[]{:S(2)}) %all-to-all-start.1) | async-done | bytes 4194336 | tf_op jit(solution)/shard_map/all_to_all | solution.py:52
  188.5 3.2 gather_fusion.5
  191.6 2.7 copy_select_fusion
  194.3 7.5 %all-to-all-start.4 = ((bf16[8,8,128,128]{3,1,2,0:T(8,128)(2,1)}), bf16[8,8,128,128]{3,1,2,0:T(8,128)(2,1)S(1)}, u32[]{:S(2)}, u32[]{:S(2)}) async-start(bf16[8,8,128,128]{3,1,2,0:T(8,128)(2,1)} %copy_select_fusion), calls=%async_computation.5 | async-start | bytes 4194304 | tf_op jit(solution)/shard_map/all_to_all | solution.py:78
  202.1 5.3 %gather_fusion.4 = bf16[8,128,1536]{2,1,0:T(8,128)(2,1)} fusion(bf16[16,128,1536]{2,1,0:T(8,128)(2,1)} %all-to-all-done, s32[1024]{0:T(1024)S(1)} %pad_clamp_fusion), kind=kCustom, calls=%fused_computation.4 | custom fusion | bytes 6291488 | tf_op jit(solution)/shard_map/jit(_take)/gather | solution.py:70
  207.4 4.0 select_select_fusion
  211.5 16.7 %all-to-all-done.4 = bf16[8,8,128,128]{3,1,2,0:T(8,128)(2,1)S(1)} async-done(((bf16[8,8,128,128]{3,1,2,0:T(8,128)(2,1)}), bf16[8,8,128,128]{3,1,2,0:T(8,128)(2,1)S(1)}, u32[]{:S(2)}, u32[]{:S(2)}) %all-to-all-start.4) | async-done | bytes 2097184 | tf_op jit(solution)/shard_map/all_to_all | solution.py:78
  229.5 5.2 %all-to-all-start.3 = ((bf16[8,128,1536]{2,1,0:T(8,128)(2,1)}), bf16[8,128,1536]{2,1,0:T(8,128)(2,1)}, u32[]{:S(2)}, u32[]{:S(2)}) async-start(bf16[8,128,1536]{2,1,0:T(8,128)(2,1)} %select_select_fusion), calls=%async_computation.4 | async-start | bytes 6291456 | tf_op jit(solution)/shard_map/all_to_all | solution.py:77
  234.7 37.6 %reduce-scatter.2.cloned.1.call-done = bf16[256,1024]{1,0:T(8,128)(2,1)} async-done(((bf16[4096,1024]{1,0:T(8,128)(2,1)}), bf16[256,1024]{1,0:T(8,128)(2,1)}) %reduce-scatter.2.cloned.1.call-update) | async-done | bytes 524304 | tf_op jit(solution)/shard_map/reduce_scatter | solution.py:57
  272.4 3.8 gather_fusion.3
  276.2 4.6 broadcast_select_fusion.1
  280.8 5.0 %all-to-all-start.2 = ((bf16[16,128,1024]{2,1,0:T(8,128)(2,1)}), bf16[16,128,1024]{2,1,0:T(8,128)(2,1)}, u32[]{:S(2)}, u32[]{:S(2)}) async-start(bf16[16,128,1024]{2,1,0:T(8,128)(2,1)} %broadcast_select_fusion.1), calls=%async_computation.3 | async-start | bytes 8388608 | tf_op jit(solution)/shard_map/all_to_all | solution.py:83
  285.8 2.7 convolution_bitcast_fusion
  288.5 148.2 %all-reduce.1 = bf16[1024,1024]{0,1:T(8,128)(2,1)} all-reduce(f32[1024,1024]{0,1:T(8,128)} %convolution_bitcast_fusion), channel_id=1, replica_groups=mesh['row'=8,'col'=16] {'row','col'}, use_global_device_ids=true, to_apply=%region_3.4 | all-reduce | flops 1048576 | bytes 6291456 | tf_op jit(solution)/shard_map/psum | solution.py:64
  436.8 2.9 gather_fusion.6
  441.3 7.0 %all-to-all-start.5 = ((bf16[8,128,1024]{2,1,0:T(8,128)(2,1)}), bf16[8,128,1024]{2,1,0:T(8,128)(2,1)}, u32[]{:S(2)}, u32[]{:S(2)}) async-start(bf16[8,128,1024]{2,1,0:T(8,128)(2,1)} %select_select_fusion.1), calls=%async_computation.6 | async-start | bytes 4194304 | tf_op jit(solution)/shard_map/all_to_all | solution.py:87
  448.2 2.0 fusion.17
  451.2 2.9 fusion.11
  454.1 4.3 convolution_bitcast_fusion.1
  458.4 16.3 %all-to-all-done.5 = bf16[8,128,1024]{2,1,0:T(8,128)(2,1)} async-done(((bf16[8,128,1024]{2,1,0:T(8,128)(2,1)}), bf16[8,128,1024]{2,1,0:T(8,128)(2,1)}, u32[]{:S(2)}, u32[]{:S(2)}) %all-to-all-start.5) | async-done | bytes 2097184 | tf_op jit(solution)/shard_map/all_to_all | solution.py:87
  474.7 6.3 %convolution_convert_fusion = bf16[1024,512]{1,0:T(8,128)(2,1)S(1)} fusion(bf16[1,1,1024,512]{3,2,1,0:T(8,128)(2,1)S(1)} %copy-done, bf16[1024,1024]{1,0:T(8,128)(2,1)} %bitcast.25, bf16[1024,1024]{0,1:T(8,128)(2,1)} %all-reduce.1, bf16[1024,1536]{1,0:T(8,128)(2,1)} %bitcast.10), kind=kOutput, calls=%fused_computation.25 | convolution fusion | flops 3225944064 | bytes 8388608 | tf_op jit(solution)/shard_map/xm,xi->mi/dot_general | solution.py:100
  482.0 2.0 convolution_subtract_fusion.1
  483.9 2.0 fusion.16
  (49 shorter events, 12.5 us)
Async XLA Ops:
  7.2 441.1 %copy-start = (bf16[1,1,1024,512]{3,2,1,0:T(8,128)(2,1)S(1)}, bf16[1,1,1024,512]{3,2,1,0:T(8,128)(2,1)}, u32[]{:S(2)}) copy-start(bf16[1,1,1024,512]{3,2,1,0:T(8,128)(2,1)} %param.9) | copy-start | bytes 3145732
  7.2 121.2 %all-gather.2.cloned.1.call-start = ((), (), s32[]{:S(2)}) async-start(), calls=%async_computation.7 | async-start | bytes 4718592 | tf_op jit(solution)/shard_map/all_gather | solution.py:54
  22.0 100.9 %all-to-all-start = ((bf16[16,128,1536]{2,1,0:T(8,128)(2,1)}), bf16[16,128,1536]{2,1,0:T(8,128)(2,1)}, u32[]{:S(2)}, u32[]{:S(2)}) async-start(bf16[16,128,1536]{2,1,0:T(8,128)(2,1)} %broadcast_select_fusion), calls=%async_computation | async-start | bytes 12582912 | tf_op jit(solution)/shard_map/all_to_all | solution.py:50
  122.9 64.7 %all-to-all-start.1 = ((bf16[16,8,128,128]{3,2,1,0:T(8,128)(2,1)}), bf16[16,8,128,128]{3,2,1,0:T(8,128)(2,1)}, u32[]{:S(2)}, u32[]{:S(2)}) async-start(bf16[16,8,128,128]{3,2,1,0:T(8,128)(2,1)} %bitcast.77), calls=%async_computation.1 | async-start | bytes 8388608 | tf_op jit(solution)/shard_map/all_to_all | solution.py:52
  128.3 144.0 %reduce-scatter.2.cloned.1.call-start = ((), (), s32[]{:S(2)}) async-start(), calls=%async_computation.8 | async-start | bytes 8912896 | tf_op jit(solution)/shard_map/reduce_scatter | solution.py:57
  194.3 33.9 %all-to-all-start.4 = ((bf16[8,8,128,128]{3,1,2,0:T(8,128)(2,1)}), bf16[8,8,128,128]{3,1,2,0:T(8,128)(2,1)S(1)}, u32[]{:S(2)}, u32[]{:S(2)}) async-start(bf16[8,8,128,128]{3,1,2,0:T(8,128)(2,1)} %copy_select_fusion), calls=%async_computation.5 | async-start | bytes 4194304 | tf_op jit(solution)/shard_map/all_to_all | solution.py:78
  228.2 1.3 copy-start.4
  229.5 51.3 %all-to-all-start.3 = ((bf16[8,128,1536]{2,1,0:T(8,128)(2,1)}), bf16[8,128,1536]{2,1,0:T(8,128)(2,1)}, u32[]{:S(2)}, u32[]{:S(2)}) async-start(bf16[8,128,1536]{2,1,0:T(8,128)(2,1)} %select_select_fusion), calls=%async_computation.4 | async-start | bytes 6291456 | tf_op jit(solution)/shard_map/all_to_all | solution.py:77
  280.8 5.0 %copy-start.1 = (bf16[256,1024]{1,0:T(8,128)(2,1)S(1)}, bf16[256,1024]{1,0:T(8,128)(2,1)}, u32[]{:S(2)}) copy-start(bf16[256,1024]{1,0:T(8,128)(2,1)} %reduce-scatter.2.cloned.1.call-done) | copy-start | bytes 1572868
  280.8 5.0 %copy-start.2 = (bf16[256,1024]{1,0:T(8,128)(2,1)S(1)}, bf16[256,1024]{1,0:T(8,128)(2,1)}, u32[]{:S(2)}) copy-start(bf16[256,1024]{1,0:T(8,128)(2,1)} %param.7) | copy-start | bytes 1572868
  280.8 156.0 %all-to-all-start.2 = ((bf16[16,128,1024]{2,1,0:T(8,128)(2,1)}), bf16[16,128,1024]{2,1,0:T(8,128)(2,1)}, u32[]{:S(2)}, u32[]{:S(2)}) async-start(bf16[16,128,1024]{2,1,0:T(8,128)(2,1)} %broadcast_select_fusion.1), calls=%async_computation.3 | async-start | bytes 8388608 | tf_op jit(solution)/shard_map/all_to_all | solution.py:83
  441.3 33.4 %all-to-all-start.5 = ((bf16[8,128,1024]{2,1,0:T(8,128)(2,1)}), bf16[8,128,1024]{2,1,0:T(8,128)(2,1)}, u32[]{:S(2)}, u32[]{:S(2)}) async-start(bf16[8,128,1024]{2,1,0:T(8,128)(2,1)} %select_select_fusion.1), calls=%async_computation.6 | async-start | bytes 4194304 | tf_op jit(solution)/shard_map/all_to_all | solution.py:87
  481.0 1.0 copy-start.3
Sparse Core Ops, SparseCore 0:
  9.7 35.7 all-gather.1
  187.8 84.5 reduce-scatter.1

commit v12 on v11

--- a/solution.py
+++ b/solution.py
@@ -54,14 +54,16 @@
     gathered = lax.all_gather(lmo_coef, "row", axis=0, tiled=True)
     fock_lmo = jnp.dot(panel_fock, gathered, preferred_element_type=F32).astype(BF16)
     rows_a, tiles_a, fock_lmo = lax.optimization_barrier((rows_a, tiles_a, fock_lmo))
-    coef_b = lax.psum_scatter(
-        fock_lmo,
-        "col",
-        scatter_dimension=0,
-        tiled=True,
-    )
-    occ_term = jnp.einsum("ri,rj->ij", lmo_coef, coef_b, preferred_element_type=F32)
-    occ_b = lax.psum(occ_term, ("row", "col")).astype(BF16)
+    half = occ_width // 2
+    coef_lo = lax.psum_scatter(fock_lmo[:, :half], "col", scatter_dimension=0, tiled=True)
+    coef_hi = lax.psum_scatter(fock_lmo[:, half:], "col", scatter_dimension=0, tiled=True)
+    occ_lo = jnp.einsum("ri,rj->ij", lmo_coef, coef_lo, preferred_element_type=F32)
+    occ_lo = lax.psum(occ_lo, ("row", "col")).astype(BF16)
+    coef_hi, occ_lo = lax.optimization_barrier((coef_hi, occ_lo))
+    occ_hi = jnp.einsum("ri,rj->ij", lmo_coef, coef_hi, preferred_element_type=F32)
+    occ_hi = lax.psum(occ_hi, ("row", "col")).astype(BF16)
+    coef_b = jnp.concatenate([coef_lo, coef_hi], axis=1)
+    occ_b = jnp.concatenate([occ_lo, occ_hi], axis=1)
 
     pres_o = lax.dynamic_index_in_dim(present, my_col, 0, keepdims=False)
     cset_o = lax.dynamic_index_in_dim(cset, my_col, 0, keepdims=False)

time: 495 us -> 549 us (1.11)
  blocking collectives: 148 us -> 199 us
    psum x1 -> x2, blocking collectives: 148 us -> 199 us  [the longest x1 121 us: body(): occ_hi = lax.psum(occ_hi, ('row', 'col')).astype(BF16)]
    slice x0 -> x1, local copies, waits for them, and re-layouts: none -> 5.71 us  [body(): fock_lmo[:, :half]]
    reduce_scatter x1 -> x2, waiting for transfers between devices: 37.6 us -> 32.9 us  [the longest x1 29.6 us: body(): lax.psum_scatter(fock_lmo[:, :half], 'col', scatter_dimension=0, tiled=True)]
  transfers between devices with their start and end apart: 8 -> 9, of which waited for: 5 -> 6; matrix products, arithmetic and copies ran while one was open for 21% -> 19% of each run, Pallas kernels for 0% -> 0%
where the time goes in v12:
time: 549 us; the launch traced here: 548 us
  blocking collectives  199 us (36%)
  waiting for transfers between devices  168 us (31%)
  local copies, waits for them, and re-layouts  57.7 us (11%)
  matrix products  46 us (8%)
  starting transfers between devices  36.5 us (7%)
  other arithmetic  26 us (5%)
  between operations  14 us (3%)
    psum x1, blocking collectives, body(): occ_hi = lax.psum(occ_hi, ('row', 'col')).astype(BF16)  121 us
    psum x1, blocking collectives, body(): occ_lo = lax.psum(occ_lo, ('row', 'col')).astype(BF16)  78.1 us
    all_to_all x1, waiting for transfers between devices, body(): rows_a = lax.all_to_all(rows_a, 'col', 0, 0, tiled=True)  65.2 us
    all_to_all x1, waiting for transfers between devices, body(): tiles_a = lax.all_to_all(tiles_a, 'col', 0, 0, tiled=True)  35.8 us
    reduce_scatter x1, waiting for transfers between devices, body(): lax.psum_scatter(fock_lmo[:, :half], 'col', scatter_dimension=0, tiled=True)  29.6 us
    dot_general x1, matrix products, body(): jnp.dot(panel_fock, gathered, preferred_element_type=F32).astype(BF16)  23.4 us
    all_to_all x1, waiting for transfers between devices, body(): lax.all_to_all(tiles_b, 'row', 0, 0, tiled=True)  16.8 us
    all_to_all x1, waiting for transfers between devices, body(): lax.all_to_all(fc_b, 'row', 0, 0, tiled=True).reshape(dom_width, occ_width)  16.3 us
  transfers between devices with their start and end apart: 9, of which 6 were waited for; matrix products, arithmetic and copies ran while one was open for 19% of the time, Pallas kernels for 0%

profile of v12, /device:TPU:1, one launch (start us, length us, event | category | flops | bytes accessed | tf_op | source)
XLA Modules:
  0.0 547.8 jit_solution(13908665346692510921)
XLA Ops:
  12.3 3.6 gather_fusion.2
  15.9 6.1 %broadcast_select_fusion = bf16[16,128,1536]{2,1,0:T(8,128)(2,1)} fusion(bf16[16,128,1536]{2,1,0:T(8,128)(2,1)} %gather_fusion.2, pred[16]{0:T(512)(128)(4,1)S(1)} %compare_and_fusion.2), kind=kLoop, calls=%fused_computation.10 | loop fusion | flops 3145728 | bytes 12582928 | tf_op jit(solution)/shard_map/jit(_take)/select_n | solution.py:49
  22.0 8.5 %all-to-all-start = ((bf16[16,128,1536]{2,1,0:T(8,128)(2,1)}), bf16[16,128,1536]{2,1,0:T(8,128)(2,1)}, u32[]{:S(2)}, u32[]{:S(2)}) async-start(bf16[16,128,1536]{2,1,0:T(8,128)(2,1)} %broadcast_select_fusion), calls=%async_computation | async-start | bytes 12582912 | tf_op jit(solution)/shard_map/all_to_all | solution.py:50
  30.6 9.9 %copy.44 = bf16[512,8,16,128]{3,2,1,0:T(8,128)(2,1)S(1)} copy(bf16[512,8,16,128]{3,1,2,0:T(8,128)(2,1)} %bitcast.80) | data formatting | bytes 33554432
  40.5 8.2 %copy.33 = bf16[32,128,16,128]{3,1,2,0:T(8,128)(2,1)} copy(bf16[32,128,16,128]{3,2,1,0:T(8,128)(2,1)S(1)} %bitcast.77) | data formatting | bytes 33554432 | tf_op jit(solution)/shard_map/reshape;squeeze | solution.py:46
  48.8 8.9 %gather_fusion.1 = bf16[128,128,128]{2,1,0:T(8,128)(2,1)} fusion(bf16[32,128,16,128]{3,1,2,0:T(8,128)(2,1)} %copy.33, s32[128]{0:T(128)S(1)} %reshape.174), kind=kCustom, calls=%fused_computation.1 | custom fusion | bytes 8389632 | tf_op jit(solution)/shard_map/gather | solution.py:47
  57.7 65.2 %all-to-all-done = bf16[16,128,1536]{2,1,0:T(8,128)(2,1)} async-done(((bf16[16,128,1536]{2,1,0:T(8,128)(2,1)}), bf16[16,128,1536]{2,1,0:T(8,128)(2,1)}, u32[]{:S(2)}, u32[]{:S(2)}) %all-to-all-start) | async-done | bytes 6291488 | tf_op jit(solution)/shard_map/all_to_all | solution.py:50
  122.9 5.4 all-to-all-start.1
  128.4 23.4 %fusion.2 = bf16[4096,1024]{1,0:T(8,128)(2,1)} fusion(bf16[2048,1024]{1,0:T(8,128)(2,1)} %all-gather.2.cloned.1.call-done, bf16[4096,1,2048]{2,0,1:T(8,128)(2,1)} %param.6), kind=kOutput, calls=%fused_computation.9 | convolution fusion | flops 17184063488 | bytes 29360128 | tf_op jit(solution)/shard_map/dot_general | solution.py:55
  151.9 35.8 %all-to-all-done.1 = bf16[16,8,128,128]{3,2,1,0:T(8,128)(2,1)} async-done(((bf16[16,8,128,128]{3,2,1,0:T(8,128)(2,1)}), bf16[16,8,128,128]{3,2,1,0:T(8,128)(2,1)}, u32[]{:S(2)}, u32[]{:S(2)}) %all-to-all-start.1) | async-done | bytes 4194336 | tf_op jit(solution)/shard_map/all_to_all | solution.py:52
  187.6 5.7 %fusion.45 = (bf16[4096,512]{1,0:T(8,128)(2,1)}, bf16[4096,512]{1,0:T(8,128)(2,1)}) fusion(bf16[4096,1024]{1,0:T(8,128)(2,1)} %fusion.2), kind=kLoop, calls=%fused_computation.90 | loop fusion | bytes 16777216 | tf_op jit(solution)/shard_map/slice | solution.py:58
  194.9 3.2 gather_fusion.5
  198.1 2.7 copy_select_fusion
  200.8 7.5 %all-to-all-start.4 = ((bf16[8,8,128,128]{3,1,2,0:T(8,128)(2,1)}), bf16[8,8,128,128]{3,1,2,0:T(8,128)(2,1)S(1)}, u32[]{:S(2)}, u32[]{:S(2)}) async-start(bf16[8,8,128,128]{3,1,2,0:T(8,128)(2,1)} %copy_select_fusion), calls=%async_computation.6 | async-start | bytes 4194304 | tf_op jit(solution)/shard_map/all_to_all | solution.py:80
  208.5 5.3 gather_fusion.4
  213.8 4.1 select_select_fusion
  217.9 16.8 %all-to-all-done.4 = bf16[8,8,128,128]{3,1,2,0:T(8,128)(2,1)S(1)} async-done(((bf16[8,8,128,128]{3,1,2,0:T(8,128)(2,1)}), bf16[8,8,128,128]{3,1,2,0:T(8,128)(2,1)S(1)}, u32[]{:S(2)}, u32[]{:S(2)}) %all-to-all-start.4) | async-done | bytes 2097184 | tf_op jit(solution)/shard_map/all_to_all | solution.py:80
  236.0 5.2 all-to-all-start.3
  241.2 29.6 %reduce-scatter.3.cloned.1.call-done = bf16[256,512]{1,0:T(8,128)(2,1)} async-done(((bf16[4096,512]{1,0:T(8,128)(2,1)}), bf16[256,512]{1,0:T(8,128)(2,1)}) %reduce-scatter.3.cloned.1.call-update) | async-done | bytes 262160 | tf_op jit(solution)/shard_map/reduce_scatter | solution.py:58
  272.4 78.1 %all-reduce.2 = bf16[1024,512]{0,1:T(8,128)(2,1)} all-reduce(f32[1024,512]{0,1:T(8,128)S(1)} %convolution_bitcast_fusion.1), channel_id=1, replica_groups=mesh['row'=8,'col'=16] {'row','col'}, use_global_device_ids=true, to_apply=%region_4.5 | all-reduce | flops 524288 | bytes 3145728 | tf_op jit(solution)/shard_map/psum | solution.py:61
  350.5 3.2 reduce-scatter.5.cloned.1.call-done
  354.8 2.8 gather_fusion.3
  357.6 4.6 broadcast_select_fusion.1
  362.2 4.7 all-to-all-start.2
  368.4 121.2 %all-reduce.3 = bf16[1024,512]{0,1:T(8,128)(2,1)} all-reduce(f32[1024,512]{0,1:T(8,128)S(1)} %convolution_bitcast_fusion), channel_id=1, replica_groups=mesh['row'=8,'col'=16] {'row','col'}, use_global_device_ids=true, to_apply=%region_5.6 | all-reduce | flops 524288 | bytes 3145728 | tf_op jit(solution)/shard_map/psum | solution.py:64
  489.6 3.1 pad_maximum_fusion
  492.7 2.9 gather_fusion.6
  497.2 5.0 all-to-all-start.5
  505.2 2.9 fusion.11
  508.1 4.3 convolution_bitcast_fusion.2
  512.4 16.3 %all-to-all-done.5 = bf16[8,128,1024]{2,1,0:T(8,128)(2,1)} async-done(((bf16[8,128,1024]{2,1,0:T(8,128)(2,1)}), bf16[8,128,1024]{2,1,0:T(8,128)(2,1)}, u32[]{:S(2)}, u32[]{:S(2)}) %all-to-all-start.5) | async-done | bytes 2097184 | tf_op jit(solution)/shard_map/all_to_all | solution.py:89
  528.7 6.3 %convolution_convert_fusion = bf16[1024,512]{1,0:T(8,128)(2,1)S(1)} fusion(bf16[1,1,1024,512]{3,2,1,0:T(8,128)(2,1)S(1)} %copy-done, bf16[1024,1024]{1,0:T(8,128)(2,1)} %bitcast.26, bf16[1024,1024]{0,1:T(8,128)(2,1)} %pad_maximum_fusion, bf16[1024,1536]{1,0:T(8,128)(2,1)} %bitcast.11), kind=kOutput, calls=%fused_computation.27 | convolution fusion | flops 3225944064 | bytes 8388608 | tf_op jit(solution)/shard_map/xm,xi->mi/dot_general | solution.py:102
  (57 shorter events, 23.4 us)
Async XLA Ops:
  7.2 495.1 %copy-start = (bf16[1,1,1024,512]{3,2,1,0:T(8,128)(2,1)S(1)}, bf16[1,1,1024,512]{3,2,1,0:T(8,128)(2,1)}, u32[]{:S(2)}) copy-start(bf16[1,1,1024,512]{3,2,1,0:T(8,128)(2,1)} %param.9) | copy-start | bytes 3145732
  7.2 121.2 %all-gather.2.cloned.1.call-start = ((), (), s32[]{:S(2)}) async-start(), calls=%async_computation.8 | async-start | bytes 4718592 | tf_op jit(solution)/shard_map/all_gather | solution.py:54
  22.0 100.9 %all-to-all-start = ((bf16[16,128,1536]{2,1,0:T(8,128)(2,1)}), bf16[16,128,1536]{2,1,0:T(8,128)(2,1)}, u32[]{:S(2)}, u32[]{:S(2)}) async-start(bf16[16,128,1536]{2,1,0:T(8,128)(2,1)} %broadcast_select_fusion), calls=%async_computation | async-start | bytes 12582912 | tf_op jit(solution)/shard_map/all_to_all | solution.py:50
  122.9 64.7 %all-to-all-start.1 = ((bf16[16,8,128,128]{3,2,1,0:T(8,128)(2,1)}), bf16[16,8,128,128]{3,2,1,0:T(8,128)(2,1)}, u32[]{:S(2)}, u32[]{:S(2)}) async-start(bf16[16,8,128,128]{3,2,1,0:T(8,128)(2,1)} %bitcast.81), calls=%async_computation.1 | async-start | bytes 8388608 | tf_op jit(solution)/shard_map/all_to_all | solution.py:52
  128.4 142.5 %reduce-scatter.3.cloned.1.call-start = ((), (), s32[]{:S(2)}) async-start(), calls=%async_computation.9 | async-start | bytes 4456448 | tf_op jit(solution)/shard_map/reduce_scatter | solution.py:58
  193.4 160.4 %reduce-scatter.5.cloned.1.call-start = ((), (), s32[]{:S(2)}) async-start(), calls=%async_computation.10 | async-start | bytes 4456448 | tf_op jit(solution)/shard_map/reduce_scatter | solution.py:59
  200.8 33.9 %all-to-all-start.4 = ((bf16[8,8,128,128]{3,1,2,0:T(8,128)(2,1)}), bf16[8,8,128,128]{3,1,2,0:T(8,128)(2,1)S(1)}, u32[]{:S(2)}, u32[]{:S(2)}) async-start(bf16[8,8,128,128]{3,1,2,0:T(8,128)(2,1)} %copy_select_fusion), calls=%async_computation.6 | async-start | bytes 4194304 | tf_op jit(solution)/shard_map/all_to_all | solution.py:80
  234.6 1.3 copy-start.2
  236.0 126.2 %all-to-all-start.3 = ((bf16[8,128,1536]{2,1,0:T(8,128)(2,1)}), bf16[8,128,1536]{2,1,0:T(8,128)(2,1)}, u32[]{:S(2)}, u32[]{:S(2)}) async-start(bf16[8,128,1536]{2,1,0:T(8,128)(2,1)} %select_select_fusion), calls=%async_computation.5 | async-start | bytes 6291456 | tf_op jit(solution)/shard_map/all_to_all | solution.py:79
  270.8 82.9 %copy-start.4 = (bf16[256,512]{1,0:T(8,128)(2,1)S(1)}, bf16[256,512]{1,0:T(8,128)(2,1)}, u32[]{:S(2)}) copy-start(bf16[256,512]{1,0:T(8,128)(2,1)} %reduce-scatter.3.cloned.1.call-done) | copy-start | bytes 786436
  362.2 4.7 copy-start.3
  362.2 130.5 %all-to-all-start.2 = ((bf16[16,128,1024]{2,1,0:T(8,128)(2,1)}), bf16[16,128,1024]{2,1,0:T(8,128)(2,1)}, u32[]{:S(2)}, u32[]{:S(2)}) async-start(bf16[16,128,1024]{2,1,0:T(8,128)(2,1)} %broadcast_select_fusion.1), calls=%async_computation.4 | async-start | bytes 8388608 | tf_op jit(solution)/shard_map/all_to_all | solution.py:85
  497.2 31.5 %all-to-all-start.5 = ((bf16[8,128,1024]{2,1,0:T(8,128)(2,1)}), bf16[8,128,1024]{2,1,0:T(8,128)(2,1)}, u32[]{:S(2)}, u32[]{:S(2)}) async-start(bf16[8,128,1024]{2,1,0:T(8,128)(2,1)} %select_select_fusion.1), calls=%async_computation.7 | async-start | bytes 4194304 | tf_op jit(solution)/shard_map/all_to_all | solution.py:89
  535.0 1.0 copy-start.1
Sparse Core Ops, SparseCore 0:
  9.7 35.7 all-gather.1
  193.5 77.2 reduce-scatter.2
  274.5 79.1 reduce-scatter.4

commit v13 on v11

--- a/solution.py
+++ b/solution.py
@@ -53,7 +53,7 @@
 
     gathered = lax.all_gather(lmo_coef, "row", axis=0, tiled=True)
     fock_lmo = jnp.dot(panel_fock, gathered, preferred_element_type=F32).astype(BF16)
-    rows_a, tiles_a, fock_lmo = lax.optimization_barrier((rows_a, tiles_a, fock_lmo))
+    rows_a, fock_lmo = lax.optimization_barrier((rows_a, fock_lmo))
     coef_b = lax.psum_scatter(
         fock_lmo,
         "col",

time: 495 us -> 521 us (1.053)
  waiting for transfers between devices: 172 us -> 190 us
  starting transfers between devices: 38.7 us -> 44.5 us
    reduce_scatter x1, waiting for transfers between devices: 37.6 us -> 0.01 us  [body(): coef_b = lax.psum_scatter(fock_lmo, 'col', scatter_dimension=0, tiled=True)]
    all_to_all x1, waiting for transfers between devices: 0.01 us -> 31.2 us  [body(): lax.all_to_all(rows_b, 'row', 0, 0, tiled=True)]
    all_to_all x1, waiting for transfers between devices: 35.8 us -> 58.9 us  [body(): tiles_a = lax.all_to_all(tiles_a, 'col', 0, 0, tiled=True)]
    all_to_all x1, starting transfers between devices: 5.21 us -> 10.5 us  [body(): lax.all_to_all(rows_b, 'row', 0, 0, tiled=True)]
    unnamed x14 -> x12, local copies, waits for them, and re-layouts: 15.3 us -> 14 us
  transfers between devices with their start and end apart: 8 -> 8, of which waited for: 5 -> 5; matrix products, arithmetic and copies ran while one was open for 21% -> 15% of each run, Pallas kernels for 0% -> 0%
where the time goes in v13:
time: 521 us; the launch traced here: 519 us
  waiting for transfers between devices  190 us (36%)
  blocking collectives  151 us (29%)
  local copies, waits for them, and re-layouts  51.7 us (10%)
  matrix products  45.6 us (9%)
  starting transfers between devices  44.5 us (9%)
  other arithmetic  21.9 us (4%)
  between operations  14.2 us (3%)
    psum x1, blocking collectives, body(): occ_b = lax.psum(occ_term, ('row', 'col')).astype(BF16)  151 us
    all_to_all x1, waiting for transfers between devices, body(): rows_a = lax.all_to_all(rows_a, 'col', 0, 0, tiled=True)  65.2 us
    all_to_all x1, waiting for transfers between devices, body(): tiles_a = lax.all_to_all(tiles_a, 'col', 0, 0, tiled=True)  58.9 us
    all_to_all x1, waiting for transfers between devices, body(): lax.all_to_all(rows_b, 'row', 0, 0, tiled=True)  31.2 us
    dot_general x1, matrix products, body(): jnp.dot(panel_fock, gathered, preferred_element_type=F32).astype(BF16)  23.4 us
    all_to_all x1, waiting for transfers between devices, body(): lax.all_to_all(tiles_b, 'row', 0, 0, tiled=True)  18 us
    all_to_all x1, waiting for transfers between devices, body(): lax.all_to_all(fc_b, 'row', 0, 0, tiled=True).reshape(dom_width, occ_width)  16.3 us
    unnamed x12, local copies, waits for them, and re-layouts  14 us
  transfers between devices with their start and end apart: 8, of which 5 were waited for; matrix products, arithmetic and copies ran while one was open for 15% of the time, Pallas kernels for 0%

profile of v13, /device:TPU:1, one launch (start us, length us, event | category | flops | bytes accessed | tf_op | source)
XLA Modules:
  0.0 519.3 jit_solution(8720471499534701685)
XLA Ops:
  12.3 3.6 gather_fusion.2
  15.9 6.1 %broadcast_select_fusion = bf16[16,128,1536]{2,1,0:T(8,128)(2,1)} fusion(bf16[16,128,1536]{2,1,0:T(8,128)(2,1)} %gather_fusion.2, pred[16]{0:T(512)(128)(4,1)S(1)} %compare_and_fusion.2), kind=kLoop, calls=%fused_computation.10 | loop fusion | flops 3145728 | bytes 12582928 | tf_op jit(solution)/shard_map/jit(_take)/select_n | solution.py:49
  22.0 8.5 %all-to-all-start = ((bf16[16,128,1536]{2,1,0:T(8,128)(2,1)}), bf16[16,128,1536]{2,1,0:T(8,128)(2,1)}, u32[]{:S(2)}, u32[]{:S(2)}) async-start(bf16[16,128,1536]{2,1,0:T(8,128)(2,1)} %broadcast_select_fusion), calls=%async_computation | async-start | bytes 12582912 | tf_op jit(solution)/shard_map/all_to_all | solution.py:50
  30.6 9.9 %copy.44 = bf16[512,8,16,128]{3,2,1,0:T(8,128)(2,1)S(1)} copy(bf16[512,8,16,128]{3,1,2,0:T(8,128)(2,1)} %bitcast.76) | data formatting | bytes 33554432
  40.5 8.2 %copy.33 = bf16[32,128,16,128]{3,1,2,0:T(8,128)(2,1)} copy(bf16[32,128,16,128]{3,2,1,0:T(8,128)(2,1)S(1)} %bitcast.73) | data formatting | bytes 33554432 | tf_op jit(solution)/shard_map/reshape;squeeze | solution.py:46
  48.9 8.8 %gather_fusion.1 = bf16[128,128,128]{2,1,0:T(8,128)(2,1)} fusion(bf16[32,128,16,128]{3,1,2,0:T(8,128)(2,1)} %copy.33, s32[128]{0:T(128)S(1)} %reshape.174), kind=kCustom, calls=%fused_computation.1 | custom fusion | bytes 8389632 | tf_op jit(solution)/shard_map/gather | solution.py:47
  57.7 65.2 %all-to-all-done = bf16[16,128,1536]{2,1,0:T(8,128)(2,1)} async-done(((bf16[16,128,1536]{2,1,0:T(8,128)(2,1)}), bf16[16,128,1536]{2,1,0:T(8,128)(2,1)}, u32[]{:S(2)}, u32[]{:S(2)}) %all-to-all-start) | async-done | bytes 6291488 | tf_op jit(solution)/shard_map/all_to_all | solution.py:50
  122.9 23.4 %fusion.2 = bf16[4096,1024]{1,0:T(8,128)(2,1)} fusion(bf16[2048,1024]{1,0:T(8,128)(2,1)} %all-gather.2.cloned.1.call-done, bf16[4096,1,2048]{2,0,1:T(8,128)(2,1)} %param.6), kind=kOutput, calls=%fused_computation.9 | convolution fusion | flops 17184063488 | bytes 29360128 | tf_op jit(solution)/shard_map/dot_general | solution.py:55
  146.4 5.4 %all-to-all-start.3 = ((bf16[16,8,128,128]{3,2,1,0:T(8,128)(2,1)}), bf16[16,8,128,128]{3,2,1,0:T(8,128)(2,1)}, u32[]{:S(2)}, u32[]{:S(2)}) async-start(bf16[16,8,128,128]{3,2,1,0:T(8,128)(2,1)} %bitcast.77), calls=%async_computation.4 | async-start | bytes 8388608 | tf_op jit(solution)/shard_map/all_to_all | solution.py:52
  152.2 5.3 %gather_fusion.4 = bf16[8,128,1536]{2,1,0:T(8,128)(2,1)} fusion(bf16[16,128,1536]{2,1,0:T(8,128)(2,1)} %all-to-all-done, s32[1024]{0:T(1024)S(1)} %pad_clamp_fusion), kind=kCustom, calls=%fused_computation.4 | custom fusion | bytes 6291488 | tf_op jit(solution)/shard_map/jit(_take)/gather | solution.py:70
  157.5 4.1 select_select_fusion
  161.6 58.9 %all-to-all-done.3 = bf16[16,8,128,128]{3,2,1,0:T(8,128)(2,1)} async-done(((bf16[16,8,128,128]{3,2,1,0:T(8,128)(2,1)}), bf16[16,8,128,128]{3,2,1,0:T(8,128)(2,1)}, u32[]{:S(2)}, u32[]{:S(2)}) %all-to-all-start.3) | async-done | bytes 4194336 | tf_op jit(solution)/shard_map/all_to_all | solution.py:52
  220.5 10.5 %all-to-all-start.2 = ((bf16[8,128,1536]{2,1,0:T(8,128)(2,1)}), bf16[8,128,1536]{2,1,0:T(8,128)(2,1)}, u32[]{:S(2)}, u32[]{:S(2)}) async-start(bf16[8,128,1536]{2,1,0:T(8,128)(2,1)} %select_select_fusion), calls=%async_computation.3 | async-start | bytes 6291456 | tf_op jit(solution)/shard_map/all_to_all | solution.py:77
  231.5 3.2 gather_fusion.5
  234.8 2.7 copy_select_fusion
  237.5 31.2 %all-to-all-done.2 = bf16[8,128,1536]{2,1,0:T(8,128)(2,1)} async-done(((bf16[8,128,1536]{2,1,0:T(8,128)(2,1)}), bf16[8,128,1536]{2,1,0:T(8,128)(2,1)}, u32[]{:S(2)}, u32[]{:S(2)}) %all-to-all-start.2) | async-done | bytes 3145760 | tf_op jit(solution)/shard_map/all_to_all | solution.py:77
  268.6 5.1 all-to-all-start.4
  273.7 3.8 gather_fusion.3
  277.5 4.6 broadcast_select_fusion.1
  282.2 18.0 %all-to-all-done.4 = bf16[8,8,128,128]{3,1,2,0:T(8,128)(2,1)} async-done(((bf16[8,8,128,128]{3,1,2,0:T(8,128)(2,1)}), bf16[8,8,128,128]{3,1,2,0:T(8,128)(2,1)}, u32[]{:S(2)}, u32[]{:S(2)}) %all-to-all-start.4) | async-done | bytes 2097184 | tf_op jit(solution)/shard_map/all_to_all | solution.py:78
  300.2 9.7 %all-to-all-start.1 = ((bf16[16,128,1024]{2,1,0:T(8,128)(2,1)}), bf16[16,128,1024]{2,1,0:T(8,128)(2,1)}, u32[]{:S(2)}, u32[]{:S(2)}) async-start(bf16[16,128,1024]{2,1,0:T(8,128)(2,1)} %broadcast_select_fusion.1), calls=%async_computation.2 | async-start | bytes 8388608 | tf_op jit(solution)/shard_map/all_to_all | solution.py:83
  309.9 2.7 convolution_bitcast_fusion
  312.6 151.2 %all-reduce.1 = bf16[1024,1024]{0,1:T(8,128)(2,1)} all-reduce(f32[1024,1024]{0,1:T(8,128)} %convolution_bitcast_fusion), channel_id=1, replica_groups=mesh['row'=8,'col'=16] {'row','col'}, use_global_device_ids=true, to_apply=%region_3.4 | all-reduce | flops 1048576 | bytes 6291456 | tf_op jit(solution)/shard_map/psum | solution.py:64
  463.8 2.9 gather_fusion.6
  468.3 5.2 all-to-all-start.5
  473.4 2.0 fusion.17
  476.4 2.9 fusion.11
  479.3 4.3 convolution_bitcast_fusion.1
  483.6 16.3 %all-to-all-done.5 = bf16[8,128,1024]{2,1,0:T(8,128)(2,1)} async-done(((bf16[8,128,1024]{2,1,0:T(8,128)(2,1)}), bf16[8,128,1024]{2,1,0:T(8,128)(2,1)}, u32[]{:S(2)}, u32[]{:S(2)}) %all-to-all-start.5) | async-done | bytes 2097184 | tf_op jit(solution)/shard_map/all_to_all | solution.py:87
  499.9 6.3 %convolution_convert_fusion = bf16[1024,512]{1,0:T(8,128)(2,1)S(1)} fusion(bf16[1,1,1024,512]{3,2,1,0:T(8,128)(2,1)S(1)} %copy-done, bf16[1024,1024]{1,0:T(8,128)(2,1)} %bitcast.25, bf16[1024,1024]{0,1:T(8,128)(2,1)} %all-reduce.1, bf16[1024,1536]{1,0:T(8,128)(2,1)} %bitcast.10), kind=kOutput, calls=%fused_computation.25 | convolution fusion | flops 3225944064 | bytes 8388608 | tf_op jit(solution)/shard_map/xm,xi->mi/dot_general | solution.py:100
  507.2 2.0 convolution_subtract_fusion.1
  509.2 2.0 fusion.16
  (47 shorter events, 11.2 us)
Async XLA Ops:
  7.2 466.3 %copy-start = (bf16[1,1,1024,512]{3,2,1,0:T(8,128)(2,1)S(1)}, bf16[1,1,1024,512]{3,2,1,0:T(8,128)(2,1)}, u32[]{:S(2)}) copy-start(bf16[1,1,1024,512]{3,2,1,0:T(8,128)(2,1)} %param.9) | copy-start | bytes 3145732
  7.2 115.8 %all-gather.2.cloned.1.call-start = ((), (), s32[]{:S(2)}) async-start(), calls=%async_computation.7 | async-start | bytes 4718592 | tf_op jit(solution)/shard_map/all_gather | solution.py:54
  22.0 100.9 %all-to-all-start = ((bf16[16,128,1536]{2,1,0:T(8,128)(2,1)}), bf16[16,128,1536]{2,1,0:T(8,128)(2,1)}, u32[]{:S(2)}, u32[]{:S(2)}) async-start(bf16[16,128,1536]{2,1,0:T(8,128)(2,1)} %broadcast_select_fusion), calls=%async_computation | async-start | bytes 12582912 | tf_op jit(solution)/shard_map/all_to_all | solution.py:50
  30.6 243.2 %reduce-scatter.2.cloned.1.call-start = ((), (), s32[]{:S(2)}) async-start(), calls=%async_computation.8 | async-start | bytes 8912896 | tf_op jit(solution)/shard_map/reduce_scatter | solution.py:57
  146.4 74.1 %all-to-all-start.3 = ((bf16[16,8,128,128]{3,2,1,0:T(8,128)(2,1)}), bf16[16,8,128,128]{3,2,1,0:T(8,128)(2,1)}, u32[]{:S(2)}, u32[]{:S(2)}) async-start(bf16[16,8,128,128]{3,2,1,0:T(8,128)(2,1)} %bitcast.77), calls=%async_computation.4 | async-start | bytes 8388608 | tf_op jit(solution)/shard_map/all_to_all | solution.py:52
  220.5 48.2 %all-to-all-start.2 = ((bf16[8,128,1536]{2,1,0:T(8,128)(2,1)}), bf16[8,128,1536]{2,1,0:T(8,128)(2,1)}, u32[]{:S(2)}, u32[]{:S(2)}) async-start(bf16[8,128,1536]{2,1,0:T(8,128)(2,1)} %select_select_fusion), calls=%async_computation.3 | async-start | bytes 6291456 | tf_op jit(solution)/shard_map/all_to_all | solution.py:77
  268.6 31.6 %all-to-all-start.4 = ((bf16[8,8,128,128]{3,1,2,0:T(8,128)(2,1)}), bf16[8,8,128,128]{3,1,2,0:T(8,128)(2,1)}, u32[]{:S(2)}, u32[]{:S(2)}) async-start(bf16[8,8,128,128]{3,1,2,0:T(8,128)(2,1)} %copy_select_fusion), calls=%async_computation.5 | async-start | bytes 4194304 | tf_op jit(solution)/shard_map/all_to_all | solution.py:78
  282.2 27.7 %copy-start.1 = (bf16[256,1024]{1,0:T(8,128)(2,1)S(1)}, bf16[256,1024]{1,0:T(8,128)(2,1)}, u32[]{:S(2)}) copy-start(bf16[256,1024]{1,0:T(8,128)(2,1)} %reduce-scatter.2.cloned.1.call-done) | copy-start | bytes 1572868
  282.2 27.7 %copy-start.2 = (bf16[256,1024]{1,0:T(8,128)(2,1)S(1)}, bf16[256,1024]{1,0:T(8,128)(2,1)}, u32[]{:S(2)}) copy-start(bf16[256,1024]{1,0:T(8,128)(2,1)} %param.7) | copy-start | bytes 1572868
  300.2 163.6 %all-to-all-start.1 = ((bf16[16,128,1024]{2,1,0:T(8,128)(2,1)}), bf16[16,128,1024]{2,1,0:T(8,128)(2,1)}, u32[]{:S(2)}, u32[]{:S(2)}) async-start(bf16[16,128,1024]{2,1,0:T(8,128)(2,1)} %broadcast_select_fusion.1), calls=%async_computation.2 | async-start | bytes 8388608 | tf_op jit(solution)/shard_map/all_to_all | solution.py:83
  468.3 31.6 %all-to-all-start.5 = ((bf16[8,128,1024]{2,1,0:T(8,128)(2,1)}), bf16[8,128,1024]{2,1,0:T(8,128)(2,1)}, u32[]{:S(2)}, u32[]{:S(2)}) async-start(bf16[8,128,1024]{2,1,0:T(8,128)(2,1)} %select_select_fusion.1), calls=%async_computation.6 | async-start | bytes 4194304 | tf_op jit(solution)/shard_map/all_to_all | solution.py:87
  506.2 1.0 copy-start.3
Sparse Core Ops, SparseCore 0:
  9.7 35.7 all-gather.1
  146.5 125.9 reduce-scatter.1

commit v14 on v11

--- a/solution.py
+++ b/solution.py
@@ -44,9 +44,9 @@
     mine2 = present & (cset == my_col)
     ct = pick(mine2, col_tile)
     fock_tiles = panel_fock.reshape(panel_blocks, BLK, col_blocks, BLK)
-    tiles_a = fock_tiles[rtile_k, :, ct, :]
+    tiles_a = fock_tiles.at[rtile_k, :, ct, :].get(mode="promise_in_bounds")
     in_rows = jnp.concatenate([lmo_coef, three_index], axis=1).reshape(dev_blocks, BLK, -1)
-    rows_a = jnp.take(in_rows, sub_o, axis=0)
+    rows_a = jnp.take(in_rows, sub_o, axis=0, mode="clip")
     rows_a = lax.all_to_all(rows_a, "col", 0, 0, tiled=True)
     tiles_a, rows_a = lax.optimization_barrier((tiles_a, rows_a))
     tiles_a = lax.all_to_all(tiles_a, "col", 0, 0, tiled=True)
@@ -67,10 +67,10 @@
     cset_o = lax.dynamic_index_in_dim(cset, my_col, 0, keepdims=False)
     pres_jk = lax.dynamic_index_in_dim(pres_o, my_row, 1, keepdims=False)
     cset_jk = lax.dynamic_index_in_dim(cset_o, my_row, 1, keepdims=False)
-    rows_b = jnp.take(rows_a, cset_jk, axis=0)
+    rows_b = jnp.take(rows_a, cset_jk, axis=0, mode="clip")
     rows_b = jnp.where(pres_jk[:, None, None], rows_b, jnp.zeros_like(rows_b))
     slot_ids = jnp.broadcast_to(jnp.arange(dom_blocks, dtype=jnp.int32)[:, None], cset_o.shape)
-    tiles_b = tiles_a[cset_o, slot_ids]
+    tiles_b = tiles_a.at[cset_o, slot_ids].get(mode="promise_in_bounds")
     live_b = pres_o & pres_jk[:, None]
     tiles_b = jnp.where(live_b[:, :, None, None], tiles_b, jnp.zeros_like(tiles_b))
     rows_dom, tiles_dom = (
@@ -79,10 +79,10 @@
     )
     rows_dom = rows_dom.reshape(dom_width, -1)
 
-    fc_a = jnp.take(coef_b.reshape(dev_blocks, BLK, occ_width), sub_o, axis=0)
+    fc_a = jnp.take(coef_b.reshape(dev_blocks, BLK, occ_width), sub_o, axis=0, mode="clip")
     fc_a = lax.all_to_all(fc_a, "col", 0, 0, tiled=True)
     fc_a, occ_b, rows_dom, tiles_dom = lax.optimization_barrier((fc_a, occ_b, rows_dom, tiles_dom))
-    fc_b = jnp.take(fc_a, cset_jk, axis=0)
+    fc_b = jnp.take(fc_a, cset_jk, axis=0, mode="clip")
     fc_b = jnp.where(pres_jk[:, None, None], fc_b, jnp.zeros_like(fc_b))
     fc_dom = lax.all_to_all(fc_b, "row", 0, 0, tiled=True).reshape(dom_width, occ_width)
 

time: 495 us -> 484 us (0.978)
  other arithmetic: 21.9 us -> 11 us
    select_n x4 -> x0, other arithmetic: 10.7 us -> none  [the longest x1 6.08 us: body(): rows_a = jnp.take(in_rows, sub_o, axis=0)]
  transfers between devices with their start and end apart: 8 -> 8, of which waited for: 5 -> 5; matrix products, arithmetic and copies ran while one was open for 21% -> 19% of each run, Pallas kernels for 0% -> 0%
where the time goes in v14:
time: 484 us; the launch traced here: 483 us
  waiting for transfers between devices  172 us (36%)
  blocking collectives  149 us (31%)
  local copies, waits for them, and re-layouts  53 us (11%)
  matrix products  45.6 us (9%)
  starting transfers between devices  38.6 us (8%)
  between operations  14.2 us (3%)
  other arithmetic  11 us (2%)
    psum x1, blocking collectives, body(): occ_b = lax.psum(occ_term, ('row', 'col')).astype(BF16)  149 us
    all_to_all x1, waiting for transfers between devices, body(): rows_a = lax.all_to_all(rows_a, 'col', 0, 0, tiled=True)  65.2 us
    reduce_scatter x1, waiting for transfers between devices, body(): coef_b = lax.psum_scatter(fock_lmo, 'col', scatter_dimension=0, tiled=True)  37.5 us
    all_to_all x1, waiting for transfers between devices, body(): tiles_a = lax.all_to_all(tiles_a, 'col', 0, 0, tiled=True)  35.7 us
    dot_general x1, matrix products, body(): jnp.dot(panel_fock, gathered, preferred_element_type=F32).astype(BF16)  23.4 us
    all_to_all x1, waiting for transfers between devices, body(): lax.all_to_all(tiles_b, 'row', 0, 0, tiled=True)  16.8 us
    all_to_all x1, waiting for transfers between devices, body(): lax.all_to_all(fc_b, 'row', 0, 0, tiled=True).reshape(dom_width, occ_width)  16.3 us
    unnamed x14, local copies, waits for them, and re-layouts  15.1 us
  transfers between devices with their start and end apart: 8, of which 5 were waited for; matrix products, arithmetic and copies ran while one was open for 19% of the time, Pallas kernels for 0%

profile of v14, /device:TPU:1, one launch (start us, length us, event | category | flops | bytes accessed | tf_op | source)
XLA Modules:
  0.0 483.2 jit_solution(15179841917422128813)
XLA Ops:
  12.3 3.6 gather_fusion.2
  15.9 8.5 %all-to-all-start = ((bf16[16,128,1536]{2,1,0:T(8,128)(2,1)}), bf16[16,128,1536]{2,1,0:T(8,128)(2,1)}, u32[]{:S(2)}, u32[]{:S(2)}) async-start(bf16[16,128,1536]{2,1,0:T(8,128)(2,1)} %gather_fusion.2), calls=%async_computation | async-start | bytes 12582912 | tf_op jit(solution)/shard_map/all_to_all | solution.py:50
  24.4 9.7 %copy.44 = bf16[512,8,16,128]{3,2,1,0:T(8,128)(2,1)S(1)} copy(bf16[512,8,16,128]{3,1,2,0:T(8,128)(2,1)} %bitcast.68) | data formatting | bytes 33554432
  34.1 8.2 %copy.33 = bf16[32,128,16,128]{3,1,2,0:T(8,128)(2,1)} copy(bf16[32,128,16,128]{3,2,1,0:T(8,128)(2,1)S(1)} %bitcast.65) | data formatting | bytes 33554432 | tf_op jit(solution)/shard_map/reshape;squeeze | solution.py:46
  42.5 9.0 %gather_fusion.1 = bf16[128,128,128]{2,1,0:T(8,128)(2,1)} fusion(bf16[32,128,16,128]{3,1,2,0:T(8,128)(2,1)} %copy.33, s32[128]{0:T(128)S(1)} %reshape.121), kind=kCustom, calls=%fused_computation.1 | custom fusion | bytes 8389632 | tf_op jit(solution)/shard_map/gather | solution.py:47
  51.5 65.2 %all-to-all-done = bf16[16,128,1536]{2,1,0:T(8,128)(2,1)} async-done(((bf16[16,128,1536]{2,1,0:T(8,128)(2,1)}), bf16[16,128,1536]{2,1,0:T(8,128)(2,1)}, u32[]{:S(2)}, u32[]{:S(2)}) %all-to-all-start) | async-done | bytes 6291488 | tf_op jit(solution)/shard_map/all_to_all | solution.py:50
  116.7 5.4 %all-to-all-start.1 = ((bf16[16,8,128,128]{3,2,1,0:T(8,128)(2,1)}), bf16[16,8,128,128]{3,2,1,0:T(8,128)(2,1)}, u32[]{:S(2)}, u32[]{:S(2)}) async-start(bf16[16,8,128,128]{3,2,1,0:T(8,128)(2,1)} %bitcast.69), calls=%async_computation.1 | async-start | bytes 8388608 | tf_op jit(solution)/shard_map/all_to_all | solution.py:52
  122.2 23.4 %fusion.2 = bf16[4096,1024]{1,0:T(8,128)(2,1)} fusion(bf16[2048,1024]{1,0:T(8,128)(2,1)} %all-gather.2.cloned.1.call-done, bf16[4096,1,2048]{2,0,1:T(8,128)(2,1)} %param.6), kind=kOutput, calls=%fused_computation.9 | convolution fusion | flops 17184063488 | bytes 29360128 | tf_op jit(solution)/shard_map/dot_general | solution.py:55
  145.7 35.7 %all-to-all-done.1 = bf16[16,8,128,128]{3,2,1,0:T(8,128)(2,1)} async-done(((bf16[16,8,128,128]{3,2,1,0:T(8,128)(2,1)}), bf16[16,8,128,128]{3,2,1,0:T(8,128)(2,1)}, u32[]{:S(2)}, u32[]{:S(2)}) %all-to-all-start.1) | async-done | bytes 4194336 | tf_op jit(solution)/shard_map/all_to_all | solution.py:52
  182.2 3.2 gather_fusion.5
  185.4 2.8 copy_select_fusion
  188.2 7.4 %all-to-all-start.4 = ((bf16[8,8,128,128]{3,1,2,0:T(8,128)(2,1)}), bf16[8,8,128,128]{3,1,2,0:T(8,128)(2,1)S(1)}, u32[]{:S(2)}, u32[]{:S(2)}) async-start(bf16[8,8,128,128]{3,1,2,0:T(8,128)(2,1)} %copy_select_fusion), calls=%async_computation.5 | async-start | bytes 4194304 | tf_op jit(solution)/shard_map/all_to_all | solution.py:78
  195.8 5.4 %gather_fusion.4 = bf16[8,128,1536]{2,1,0:T(8,128)(2,1)} fusion(bf16[16,128,1536]{2,1,0:T(8,128)(2,1)} %all-to-all-done, s32[1024]{0:T(1024)S(1)} %pad_clamp_fusion), kind=kCustom, calls=%fused_computation.4 | custom fusion | bytes 6291488 | tf_op jit(solution)/shard_map/jit(_take)/gather | solution.py:70
  201.2 4.0 broadcast_select_fusion
  205.1 16.8 %all-to-all-done.4 = bf16[8,8,128,128]{3,1,2,0:T(8,128)(2,1)S(1)} async-done(((bf16[8,8,128,128]{3,1,2,0:T(8,128)(2,1)}), bf16[8,8,128,128]{3,1,2,0:T(8,128)(2,1)S(1)}, u32[]{:S(2)}, u32[]{:S(2)}) %all-to-all-start.4) | async-done | bytes 2097184 | tf_op jit(solution)/shard_map/all_to_all | solution.py:78
  223.2 5.2 %all-to-all-start.3 = ((bf16[8,128,1536]{2,1,0:T(8,128)(2,1)}), bf16[8,128,1536]{2,1,0:T(8,128)(2,1)}, u32[]{:S(2)}, u32[]{:S(2)}) async-start(bf16[8,128,1536]{2,1,0:T(8,128)(2,1)} %broadcast_select_fusion), calls=%async_computation.4 | async-start | bytes 6291456 | tf_op jit(solution)/shard_map/all_to_all | solution.py:77
  228.4 37.5 %reduce-scatter.2.cloned.1.call-done = bf16[256,1024]{1,0:T(8,128)(2,1)} async-done(((bf16[4096,1024]{1,0:T(8,128)(2,1)}), bf16[256,1024]{1,0:T(8,128)(2,1)}) %reduce-scatter.2.cloned.1.call-update) | async-done | bytes 524304 | tf_op jit(solution)/shard_map/reduce_scatter | solution.py:57
  266.0 3.8 gather_fusion.3
  269.8 4.9 %all-to-all-start.2 = ((bf16[16,128,1024]{2,1,0:T(8,128)(2,1)}), bf16[16,128,1024]{2,1,0:T(8,128)(2,1)}, u32[]{:S(2)}, u32[]{:S(2)}) async-start(bf16[16,128,1024]{2,1,0:T(8,128)(2,1)} %gather_fusion.3), calls=%async_computation.3 | async-start | bytes 8388608 | tf_op jit(solution)/shard_map/all_to_all | solution.py:83
  274.7 2.7 convolution_bitcast_fusion
  277.4 148.5 %all-reduce.1 = bf16[1024,1024]{0,1:T(8,128)(2,1)} all-reduce(f32[1024,1024]{0,1:T(8,128)} %convolution_bitcast_fusion), channel_id=1, replica_groups=mesh['row'=8,'col'=16] {'row','col'}, use_global_device_ids=true, to_apply=%region_3.4 | all-reduce | flops 1048576 | bytes 6291456 | tf_op jit(solution)/shard_map/psum | solution.py:64
  425.9 2.9 gather_fusion.6
  428.8 1.5 broadcast_select_fusion.1
  430.3 7.0 %all-to-all-start.5 = ((bf16[8,128,1024]{2,1,0:T(8,128)(2,1)}), bf16[8,128,1024]{2,1,0:T(8,128)(2,1)}, u32[]{:S(2)}, u32[]{:S(2)}) async-start(bf16[8,128,1024]{2,1,0:T(8,128)(2,1)} %broadcast_select_fusion.1), calls=%async_computation.6 | async-start | bytes 4194304 | tf_op jit(solution)/shard_map/all_to_all | solution.py:87
  437.4 2.0 fusion.17
  440.3 2.9 fusion.11
  443.2 4.3 convolution_bitcast_fusion.1
  447.6 16.3 %all-to-all-done.5 = bf16[8,128,1024]{2,1,0:T(8,128)(2,1)} async-done(((bf16[8,128,1024]{2,1,0:T(8,128)(2,1)}), bf16[8,128,1024]{2,1,0:T(8,128)(2,1)}, u32[]{:S(2)}, u32[]{:S(2)}) %all-to-all-start.5) | async-done | bytes 2097184 | tf_op jit(solution)/shard_map/all_to_all | solution.py:87
  463.8 6.3 %convolution_convert_fusion = bf16[1024,512]{1,0:T(8,128)(2,1)S(1)} fusion(bf16[1,1,1024,512]{3,2,1,0:T(8,128)(2,1)S(1)} %copy-done, bf16[1024,1024]{1,0:T(8,128)(2,1)} %bitcast.22, bf16[1024,1024]{0,1:T(8,128)(2,1)} %all-reduce.1, bf16[1024,1536]{1,0:T(8,128)(2,1)} %bitcast.7), kind=kOutput, calls=%fused_computation.23 | convolution fusion | flops 3225944064 | bytes 8388608 | tf_op jit(solution)/shard_map/xm,xi->mi/dot_general | solution.py:100
  471.1 2.0 convolution_subtract_fusion.1
  473.1 2.0 fusion.16
  475.1 1.3 copy.40
  (43 shorter events, 9.6 us)
Async XLA Ops:
  7.2 430.2 %copy-start = (bf16[1,1,1024,512]{3,2,1,0:T(8,128)(2,1)S(1)}, bf16[1,1,1024,512]{3,2,1,0:T(8,128)(2,1)}, u32[]{:S(2)}) copy-start(bf16[1,1,1024,512]{3,2,1,0:T(8,128)(2,1)} %param.9) | copy-start | bytes 3145732
  7.2 115.0 %all-gather.2.cloned.1.call-start = ((), (), s32[]{:S(2)}) async-start(), calls=%async_computation.7 | async-start | bytes 4718592 | tf_op jit(solution)/shard_map/all_gather | solution.py:54
  15.9 100.8 %all-to-all-start = ((bf16[16,128,1536]{2,1,0:T(8,128)(2,1)}), bf16[16,128,1536]{2,1,0:T(8,128)(2,1)}, u32[]{:S(2)}, u32[]{:S(2)}) async-start(bf16[16,128,1536]{2,1,0:T(8,128)(2,1)} %gather_fusion.2), calls=%async_computation | async-start | bytes 12582912 | tf_op jit(solution)/shard_map/all_to_all | solution.py:50
  116.7 64.7 %all-to-all-start.1 = ((bf16[16,8,128,128]{3,2,1,0:T(8,128)(2,1)}), bf16[16,8,128,128]{3,2,1,0:T(8,128)(2,1)}, u32[]{:S(2)}, u32[]{:S(2)}) async-start(bf16[16,8,128,128]{3,2,1,0:T(8,128)(2,1)} %bitcast.69), calls=%async_computation.1 | async-start | bytes 8388608 | tf_op jit(solution)/shard_map/all_to_all | solution.py:52
  122.1 143.8 %reduce-scatter.2.cloned.1.call-start = ((), (), s32[]{:S(2)}) async-start(), calls=%async_computation.8 | async-start | bytes 8912896 | tf_op jit(solution)/shard_map/reduce_scatter | solution.py:57
  188.2 33.8 %all-to-all-start.4 = ((bf16[8,8,128,128]{3,1,2,0:T(8,128)(2,1)}), bf16[8,8,128,128]{3,1,2,0:T(8,128)(2,1)S(1)}, u32[]{:S(2)}, u32[]{:S(2)}) async-start(bf16[8,8,128,128]{3,1,2,0:T(8,128)(2,1)} %copy_select_fusion), calls=%async_computation.5 | async-start | bytes 4194304 | tf_op jit(solution)/shard_map/all_to_all | solution.py:78
  221.9 1.3 copy-start.4
  223.2 46.6 %all-to-all-start.3 = ((bf16[8,128,1536]{2,1,0:T(8,128)(2,1)}), bf16[8,128,1536]{2,1,0:T(8,128)(2,1)}, u32[]{:S(2)}, u32[]{:S(2)}) async-start(bf16[8,128,1536]{2,1,0:T(8,128)(2,1)} %broadcast_select_fusion), calls=%async_computation.4 | async-start | bytes 6291456 | tf_op jit(solution)/shard_map/all_to_all | solution.py:77
  269.8 4.9 %copy-start.1 = (bf16[256,1024]{1,0:T(8,128)(2,1)S(1)}, bf16[256,1024]{1,0:T(8,128)(2,1)}, u32[]{:S(2)}) copy-start(bf16[256,1024]{1,0:T(8,128)(2,1)} %reduce-scatter.2.cloned.1.call-done) | copy-start | bytes 1572868
  269.8 4.9 %copy-start.2 = (bf16[256,1024]{1,0:T(8,128)(2,1)S(1)}, bf16[256,1024]{1,0:T(8,128)(2,1)}, u32[]{:S(2)}) copy-start(bf16[256,1024]{1,0:T(8,128)(2,1)} %param.7) | copy-start | bytes 1572868
  269.8 156.2 %all-to-all-start.2 = ((bf16[16,128,1024]{2,1,0:T(8,128)(2,1)}), bf16[16,128,1024]{2,1,0:T(8,128)(2,1)}, u32[]{:S(2)}, u32[]{:S(2)}) async-start(bf16[16,128,1024]{2,1,0:T(8,128)(2,1)} %gather_fusion.3), calls=%async_computation.3 | async-start | bytes 8388608 | tf_op jit(solution)/shard_map/all_to_all | solution.py:83
  430.3 33.5 %all-to-all-start.5 = ((bf16[8,128,1024]{2,1,0:T(8,128)(2,1)}), bf16[8,128,1024]{2,1,0:T(8,128)(2,1)}, u32[]{:S(2)}, u32[]{:S(2)}) async-start(bf16[8,128,1024]{2,1,0:T(8,128)(2,1)} %broadcast_select_fusion.1), calls=%async_computation.6 | async-start | bytes 4194304 | tf_op jit(solution)/shard_map/all_to_all | solution.py:87
  470.1 1.0 copy-start.3
Sparse Core Ops, SparseCore 0:
  9.7 35.7 all-gather.1
  181.5 84.3 reduce-scatter.1

commit v15 on v14

--- a/solution.py
+++ b/solution.py
@@ -25,7 +25,7 @@
     panel_blocks = panel_fock.shape[0] // BLK
     col_blocks = panel_fock.shape[1] // BLK
 
-    doms = jnp.take(domains, lmo_ids, axis=0)
+    doms = jnp.take(domains, lmo_ids, axis=0, mode="clip")
     present = doms >= 0
     clipped = jnp.maximum(doms, 0)
     flat = clipped // dev_blocks
@@ -83,12 +83,14 @@
     fc_a = lax.all_to_all(fc_a, "col", 0, 0, tiled=True)
     fc_a, occ_b, rows_dom, tiles_dom = lax.optimization_barrier((fc_a, occ_b, rows_dom, tiles_dom))
     fc_b = jnp.take(fc_a, cset_jk, axis=0, mode="clip")
-    fc_b = jnp.where(pres_jk[:, None, None], fc_b, jnp.zeros_like(fc_b))
     fc_dom = lax.all_to_all(fc_b, "row", 0, 0, tiled=True).reshape(dom_width, occ_width)
+    pres_me = lax.dynamic_index_in_dim(pres_o, my_row, 0, keepdims=False)
+    row_live = jnp.repeat(pres_me, BLK, total_repeat_length=dom_width)
 
     coef_dom = rows_dom[:, :occ_width]
     three_dom = rows_dom[:, occ_width:]
     correction = jnp.dot(coef_dom, occ_b, preferred_element_type=F32)
+    fc_dom = jnp.where(row_live[:, None], fc_dom, jnp.zeros_like(fc_dom))
     proj_dom = (fc_dom.astype(F32) - 0.5 * correction).astype(BF16)
 
     slot_rot = rotation[0, 0]

time: 484 us -> 485 us (level)
  waiting for transfers between devices: 172 us -> 164 us
    all_to_all x1, waiting for transfers between devices: 16.3 us -> 7.46 us  [body(): lax.all_to_all(fc_b, 'row', 0, 0, tiled=True).reshape(dom_width, occ_width)]
    unnamed x14 -> x17, local copies, waits for them, and re-layouts: 15.1 us -> 16.9 us
  transfers between devices with their start and end apart: 8 -> 8, of which waited for: 5 -> 5; matrix products, arithmetic and copies ran while one was open for 19% -> 21% of each run, Pallas kernels for 0% -> 0%
where the time goes in v15:
time: 485 us; the launch traced here: 484 us
  waiting for transfers between devices  164 us (34%)
  blocking collectives  149 us (31%)
  local copies, waits for them, and re-layouts  56.9 us (12%)
  matrix products  47.4 us (10%)
  starting transfers between devices  37.8 us (8%)
  other arithmetic  15 us (3%)
  between operations  14.2 us (3%)
    psum x1, blocking collectives, body(): occ_b = lax.psum(occ_term, ('row', 'col')).astype(BF16)  149 us
    all_to_all x1, waiting for transfers between devices, body(): rows_a = lax.all_to_all(rows_a, 'col', 0, 0, tiled=True)  65.2 us
    reduce_scatter x1, waiting for transfers between devices, body(): coef_b = lax.psum_scatter(fock_lmo, 'col', scatter_dimension=0, tiled=True)  37.8 us
    all_to_all x1, waiting for transfers between devices, body(): tiles_a = lax.all_to_all(tiles_a, 'col', 0, 0, tiled=True)  35.7 us
    dot_general x1, matrix products, body(): jnp.dot(panel_fock, gathered, preferred_element_type=F32).astype(BF16)  23.4 us
    unnamed x17, local copies, waits for them, and re-layouts  16.9 us
    all_to_all x1, waiting for transfers between devices, body(): lax.all_to_all(tiles_b, 'row', 0, 0, tiled=True)  16.8 us
  transfers between devices with their start and end apart: 8, of which 5 were waited for; matrix products, arithmetic and copies ran while one was open for 21% of the time, Pallas kernels for 0%

profile of v15, /device:TPU:1, one launch (start us, length us, event | category | flops | bytes accessed | tf_op | source)
XLA Modules:
  0.0 483.9 jit_solution(8566273227185597927)
XLA Ops:
  12.0 3.6 gather_fusion.2
  15.6 8.5 %all-to-all-start = ((bf16[16,128,1536]{2,1,0:T(8,128)(2,1)}), bf16[16,128,1536]{2,1,0:T(8,128)(2,1)}, u32[]{:S(2)}, u32[]{:S(2)}) async-start(bf16[16,128,1536]{2,1,0:T(8,128)(2,1)} %gather_fusion.2), calls=%async_computation | async-start | bytes 12582912 | tf_op jit(solution)/shard_map/all_to_all | solution.py:50
  24.1 9.7 %copy.65 = bf16[512,8,16,128]{3,2,1,0:T(8,128)(2,1)S(1)} copy(bf16[512,8,16,128]{3,1,2,0:T(8,128)(2,1)} %bitcast.93) | data formatting | bytes 33554432
  33.7 8.2 %copy.54 = bf16[32,128,16,128]{3,1,2,0:T(8,128)(2,1)} copy(bf16[32,128,16,128]{3,2,1,0:T(8,128)(2,1)S(1)} %bitcast.90) | data formatting | bytes 33554432 | tf_op jit(solution)/shard_map/reshape;squeeze | solution.py:46
  42.1 9.0 %gather_fusion.1 = bf16[128,128,128]{2,1,0:T(8,128)(2,1)} fusion(bf16[32,128,16,128]{3,1,2,0:T(8,128)(2,1)} %copy.54, s32[128]{0:T(128)S(1)} %reshape.208), kind=kCustom, calls=%fused_computation.1 | custom fusion | bytes 8389632 | tf_op jit(solution)/shard_map/gather | solution.py:47
  51.1 65.2 %all-to-all-done = bf16[16,128,1536]{2,1,0:T(8,128)(2,1)} async-done(((bf16[16,128,1536]{2,1,0:T(8,128)(2,1)}), bf16[16,128,1536]{2,1,0:T(8,128)(2,1)}, u32[]{:S(2)}, u32[]{:S(2)}) %all-to-all-start) | async-done | bytes 6291488 | tf_op jit(solution)/shard_map/all_to_all | solution.py:50
  116.4 5.4 %all-to-all-start.1 = ((bf16[16,8,128,128]{3,2,1,0:T(8,128)(2,1)}), bf16[16,8,128,128]{3,2,1,0:T(8,128)(2,1)}, u32[]{:S(2)}, u32[]{:S(2)}) async-start(bf16[16,8,128,128]{3,2,1,0:T(8,128)(2,1)} %bitcast.94), calls=%async_computation.1 | async-start | bytes 8388608 | tf_op jit(solution)/shard_map/all_to_all | solution.py:52
  121.9 23.4 %fusion.2 = bf16[4096,1024]{1,0:T(8,128)(2,1)} fusion(bf16[2048,1024]{1,0:T(8,128)(2,1)} %all-gather.2.cloned.1.call-done, bf16[4096,1,2048]{2,0,1:T(8,128)(2,1)} %param.8), kind=kOutput, calls=%fused_computation.9 | convolution fusion | flops 17184063488 | bytes 29360128 | tf_op jit(solution)/shard_map/dot_general | solution.py:55
  145.3 35.7 %all-to-all-done.1 = bf16[16,8,128,128]{3,2,1,0:T(8,128)(2,1)} async-done(((bf16[16,8,128,128]{3,2,1,0:T(8,128)(2,1)}), bf16[16,8,128,128]{3,2,1,0:T(8,128)(2,1)}, u32[]{:S(2)}, u32[]{:S(2)}) %all-to-all-start.1) | async-done | bytes 4194336 | tf_op jit(solution)/shard_map/all_to_all | solution.py:52
  181.7 3.2 gather_fusion.5
  184.8 2.8 copy_select_fusion
  187.6 7.4 %all-to-all-start.4 = ((bf16[8,8,128,128]{3,1,2,0:T(8,128)(2,1)}), bf16[8,8,128,128]{3,1,2,0:T(8,128)(2,1)S(1)}, u32[]{:S(2)}, u32[]{:S(2)}) async-start(bf16[8,8,128,128]{3,1,2,0:T(8,128)(2,1)} %copy_select_fusion), calls=%async_computation.5 | async-start | bytes 4194304 | tf_op jit(solution)/shard_map/all_to_all | solution.py:78
  195.2 5.4 %gather_fusion.4 = bf16[8,128,1536]{2,1,0:T(8,128)(2,1)} fusion(bf16[16,128,1536]{2,1,0:T(8,128)(2,1)} %all-to-all-done, s32[1024]{0:T(1024)S(1)} %pad_clamp_fusion), kind=kCustom, calls=%fused_computation.4 | custom fusion | bytes 6291488 | tf_op jit(solution)/shard_map/jit(_take)/gather | solution.py:70
  200.6 4.0 broadcast_select_fusion
  204.6 16.8 %all-to-all-done.4 = bf16[8,8,128,128]{3,1,2,0:T(8,128)(2,1)S(1)} async-done(((bf16[8,8,128,128]{3,1,2,0:T(8,128)(2,1)}), bf16[8,8,128,128]{3,1,2,0:T(8,128)(2,1)S(1)}, u32[]{:S(2)}, u32[]{:S(2)}) %all-to-all-start.4) | async-done | bytes 2097184 | tf_op jit(solution)/shard_map/all_to_all | solution.py:78
  222.7 5.2 %all-to-all-start.3 = ((bf16[8,128,1536]{2,1,0:T(8,128)(2,1)}), bf16[8,128,1536]{2,1,0:T(8,128)(2,1)}, u32[]{:S(2)}, u32[]{:S(2)}) async-start(bf16[8,128,1536]{2,1,0:T(8,128)(2,1)} %broadcast_select_fusion), calls=%async_computation.4 | async-start | bytes 6291456 | tf_op jit(solution)/shard_map/all_to_all | solution.py:77
  227.9 37.8 %reduce-scatter.2.cloned.1.call-done = bf16[256,1024]{1,0:T(8,128)(2,1)} async-done(((bf16[4096,1024]{1,0:T(8,128)(2,1)}), bf16[256,1024]{1,0:T(8,128)(2,1)}) %reduce-scatter.2.cloned.1.call-update) | async-done | bytes 524304 | tf_op jit(solution)/shard_map/reduce_scatter | solution.py:57
  265.7 3.8 gather_fusion.3
  269.5 4.9 %all-to-all-start.2 = ((bf16[16,128,1024]{2,1,0:T(8,128)(2,1)}), bf16[16,128,1024]{2,1,0:T(8,128)(2,1)}, u32[]{:S(2)}, u32[]{:S(2)}) async-start(bf16[16,128,1024]{2,1,0:T(8,128)(2,1)} %gather_fusion.3), calls=%async_computation.3 | async-start | bytes 8388608 | tf_op jit(solution)/shard_map/all_to_all | solution.py:83
  274.5 2.7 convolution_bitcast_fusion
  277.2 148.8 %all-reduce.1 = bf16[1024,1024]{0,1:T(8,128)(2,1)} all-reduce(f32[1024,1024]{0,1:T(8,128)} %convolution_bitcast_fusion), channel_id=1, replica_groups=mesh['row'=8,'col'=16] {'row','col'}, use_global_device_ids=true, to_apply=%region_3.4 | all-reduce | flops 1048576 | bytes 6291456 | tf_op jit(solution)/shard_map/psum | solution.py:64
  426.0 4.2 gather_fusion.6
  430.2 6.2 %all-to-all-start.5 = ((bf16[8,128,1024]{2,1,0:T(8,128)(2,1)}), bf16[8,128,1024]{2,1,0:T(8,128)(2,1)S(1)}, u32[]{:S(2)}, u32[]{:S(2)}) async-start(bf16[8,128,1024]{2,1,0:T(8,128)(2,1)} %gather_fusion.6), calls=%async_computation.6 | async-start | bytes 4194304 | tf_op jit(solution)/shard_map/all_to_all | solution.py:86
  437.1 4.5 select_reduce_fusion
  442.2 2.8 fusion.16
  445.0 2.0 copy.62
  447.0 3.8 fusion.10
  450.9 4.3 convolution_bitcast_fusion.1
  455.2 7.5 %all-to-all-done.5 = bf16[8,128,1024]{2,1,0:T(8,128)(2,1)S(1)} async-done(((bf16[8,128,1024]{2,1,0:T(8,128)(2,1)}), bf16[8,128,1024]{2,1,0:T(8,128)(2,1)S(1)}, u32[]{:S(2)}, u32[]{:S(2)}) %all-to-all-start.5) | async-done | bytes 2097184 | tf_op jit(solution)/shard_map/all_to_all | solution.py:86
  464.4 6.4 %convolution_convert_fusion = bf16[1024,512]{1,0:T(8,128)(2,1)S(1)} fusion(bf16[1,1,1024,512]{3,2,1,0:T(8,128)(2,1)S(1)} %copy-done, bf16[1024,1024]{1,0:T(8,128)(2,1)} %bitcast_select_fusion, bf16[1024,1024]{0,1:T(8,128)(2,1)} %all-reduce.1, bf16[1024,1536]{1,0:T(8,128)(2,1)} %bitcast.10), kind=kOutput, calls=%fused_computation.22 | convolution fusion | flops 3225944064 | bytes 8388608 | tf_op jit(solution)/shard_map/xm,xi->mi/dot_general | solution.py:102
  471.8 2.0 convolution_subtract_fusion.1
  473.8 2.0 fusion.15
  (51 shorter events, 12.4 us)
Async XLA Ops:
  7.2 435.1 %copy-start = (bf16[1,1,1024,512]{3,2,1,0:T(8,128)(2,1)S(1)}, bf16[1,1,1024,512]{3,2,1,0:T(8,128)(2,1)}, u32[]{:S(2)}) copy-start(bf16[1,1,1024,512]{3,2,1,0:T(8,128)(2,1)} %param.11) | copy-start | bytes 3145732
  7.2 114.7 %all-gather.2.cloned.1.call-start = ((), (), s32[]{:S(2)}) async-start(), calls=%async_computation.7 | async-start | bytes 4718592 | tf_op jit(solution)/shard_map/all_gather | solution.py:54
  15.6 100.8 %all-to-all-start = ((bf16[16,128,1536]{2,1,0:T(8,128)(2,1)}), bf16[16,128,1536]{2,1,0:T(8,128)(2,1)}, u32[]{:S(2)}, u32[]{:S(2)}) async-start(bf16[16,128,1536]{2,1,0:T(8,128)(2,1)} %gather_fusion.2), calls=%async_computation | async-start | bytes 12582912 | tf_op jit(solution)/shard_map/all_to_all | solution.py:50
  116.4 64.7 %all-to-all-start.1 = ((bf16[16,8,128,128]{3,2,1,0:T(8,128)(2,1)}), bf16[16,8,128,128]{3,2,1,0:T(8,128)(2,1)}, u32[]{:S(2)}, u32[]{:S(2)}) async-start(bf16[16,8,128,128]{3,2,1,0:T(8,128)(2,1)} %bitcast.94), calls=%async_computation.1 | async-start | bytes 8388608 | tf_op jit(solution)/shard_map/all_to_all | solution.py:52
  121.8 143.9 %reduce-scatter.2.cloned.1.call-start = ((), (), s32[]{:S(2)}) async-start(), calls=%async_computation.8 | async-start | bytes 8912896 | tf_op jit(solution)/shard_map/reduce_scatter | solution.py:57
  187.6 33.8 %all-to-all-start.4 = ((bf16[8,8,128,128]{3,1,2,0:T(8,128)(2,1)}), bf16[8,8,128,128]{3,1,2,0:T(8,128)(2,1)S(1)}, u32[]{:S(2)}, u32[]{:S(2)}) async-start(bf16[8,8,128,128]{3,1,2,0:T(8,128)(2,1)} %copy_select_fusion), calls=%async_computation.5 | async-start | bytes 4194304 | tf_op jit(solution)/shard_map/all_to_all | solution.py:78
  221.4 1.3 copy-start.5
  222.7 46.9 %all-to-all-start.3 = ((bf16[8,128,1536]{2,1,0:T(8,128)(2,1)}), bf16[8,128,1536]{2,1,0:T(8,128)(2,1)}, u32[]{:S(2)}, u32[]{:S(2)}) async-start(bf16[8,128,1536]{2,1,0:T(8,128)(2,1)} %broadcast_select_fusion), calls=%async_computation.4 | async-start | bytes 6291456 | tf_op jit(solution)/shard_map/all_to_all | solution.py:77
  269.5 4.9 %copy-start.1 = (bf16[256,1024]{1,0:T(8,128)(2,1)S(1)}, bf16[256,1024]{1,0:T(8,128)(2,1)}, u32[]{:S(2)}) copy-start(bf16[256,1024]{1,0:T(8,128)(2,1)} %reduce-scatter.2.cloned.1.call-done) | copy-start | bytes 1572868
  269.5 5.0 %copy-start.2 = (bf16[256,1024]{1,0:T(8,128)(2,1)S(1)}, bf16[256,1024]{1,0:T(8,128)(2,1)}, u32[]{:S(2)}) copy-start(bf16[256,1024]{1,0:T(8,128)(2,1)} %param.9) | copy-start | bytes 1572868
  269.5 156.4 %all-to-all-start.2 = ((bf16[16,128,1024]{2,1,0:T(8,128)(2,1)}), bf16[16,128,1024]{2,1,0:T(8,128)(2,1)}, u32[]{:S(2)}, u32[]{:S(2)}) async-start(bf16[16,128,1024]{2,1,0:T(8,128)(2,1)} %gather_fusion.3), calls=%async_computation.3 | async-start | bytes 8388608 | tf_op jit(solution)/shard_map/all_to_all | solution.py:83
  430.2 32.6 %all-to-all-start.5 = ((bf16[8,128,1024]{2,1,0:T(8,128)(2,1)}), bf16[8,128,1024]{2,1,0:T(8,128)(2,1)S(1)}, u32[]{:S(2)}, u32[]{:S(2)}) async-start(bf16[8,128,1024]{2,1,0:T(8,128)(2,1)} %gather_fusion.6), calls=%async_computation.6 | async-start | bytes 4194304 | tf_op jit(solution)/shard_map/all_to_all | solution.py:86
  464.4 7.4 %copy-start.3 = (bf16[1024,512]{1,0:T(8,128)(2,1)S(1)}, bf16[1024,512]{1,0:T(8,128)(2,1)}, u32[]{:S(2)}) copy-start(bf16[1024,512]{1,0:T(8,128)(2,1)} %fusion.10) | copy-start | bytes 3145732
  470.8 1.0 copy-start.4
Sparse Core Ops, SparseCore 0:
  9.7 35.7 all-gather.1
  181.2 84.4 reduce-scatter.1
